TPU v7x, 256 devices: a whole 4x4x8 slice. The times are simulated.
256 devices in a mesh: seq: 8 (over z_hi, core), chan: 16 (over y, x), dp: 2 (over z_lo).
Axes of the slice: x: 4, y: 4, z: 8 (z_hi: 4, z_lo: 2; z = z_hi * 2 + z_lo), core: 2. Of those that a mesh axis runs over, the one named last changes fastest.
Arguments:
- query_proj: bfloat16 [2, 4096, 8192], P('dp', 'seq', 'chan'), may hold values from -6 to 6
- key_proj: bfloat16 [2, 4096, 8192], P('dp', 'seq', 'chan')
- value_proj: bfloat16 [2, 4096, 8192], P('dp', 'seq', 'chan')
- cotangent: bfloat16 [2, 4096, 8192], P('dp', 'seq', 'chan'), may hold values from -6 to 6
- long_filter: float32 [4096, 8192], P('seq', 'chan')
- skip_gain: float32 [8192], P('chan'), may hold values from -3 to 3
Outputs:
- output: bfloat16 [2, 4096, 8192], P('dp', 'seq', 'chan')
- grad_query: bfloat16 [2, 4096, 8192], P('dp', 'seq', 'chan')
- grad_key: bfloat16 [2, 4096, 8192], P('dp', 'seq', 'chan')
- grad_value: bfloat16 [2, 4096, 8192], P('dp', 'seq', 'chan')
- grad_filter: float32 [4096, 8192], P('seq', 'chan')
- grad_skip: float32 [8192], P('chan')
All inputs are finite; a program needn't handle non-finite values.
Results may differ from a plain program's by a relative error of at most 0.0095.
Values may be sent and summed in bfloat16 or wider, within the bound.
No kernel may reach another device: no remote copies, remote signals or barrier semaphores. Data moves between devices by JAX's collectives and lax.ppermute only.
A program may use at most 64 MiB of HBM per device.

v0:
```python
import math

import jax
import jax.numpy as jnp
from jax import lax
from jax.experimental import pallas as pl
from jax.experimental.pallas import tpu as pltpu
from jax.sharding import PartitionSpec as P

full_precision = lax.Precision.HIGHEST


def spectral_tables(seq_length):
    full_size = 2 * seq_length
    inner = 128
    outer = full_size // inner
    rows = seq_length // inner
    half = outer // 2 + 1
    k_index = jnp.arange(half, dtype=jnp.int32)
    n_index = jnp.arange(rows, dtype=jnp.int32)
    m_index = jnp.arange(inner, dtype=jnp.int32)
    j_index = jnp.arange(inner, dtype=jnp.int32)
    first_angle = (2.0 * math.pi / outer) * (
        (k_index[:, None] * n_index[None, :]) % outer
    ).astype(jnp.float32)
    first_cos = jnp.cos(first_angle)
    first_sin = jnp.sin(first_angle)
    stage_a = jnp.concatenate([first_cos, -first_sin], axis=0)
    weight = jnp.where((k_index == 0) | (k_index == outer // 2), 1.0, 2.0) / full_size
    inv_a = jnp.concatenate(
        [(first_cos * weight[:, None]).T, (-first_sin * weight[:, None]).T], axis=1
    )
    twist_angle = (2.0 * math.pi / full_size) * (
        (k_index[:, None] * m_index[None, :]) % full_size
    ).astype(jnp.float32)
    twist_cos, twist_sin = jnp.cos(twist_angle), jnp.sin(twist_angle)
    last_angle = (2.0 * math.pi / inner) * (
        (j_index[:, None] * m_index[None, :]) % inner
    ).astype(jnp.float32)
    last_cos, last_sin = jnp.cos(last_angle), jnp.sin(last_angle)
    g_re = twist_cos[:, None, :] * last_cos[None] - twist_sin[:, None, :] * last_sin[None]
    g_im = -(twist_sin[:, None, :] * last_cos[None] + twist_cos[:, None, :] * last_sin[None])
    fwd_table = jnp.concatenate([g_re, g_im], axis=1).astype(jnp.bfloat16)
    g_re_t = jnp.swapaxes(g_re, 1, 2)
    g_im_t = jnp.swapaxes(g_im, 1, 2)
    inv_table = jnp.concatenate([g_re_t, -g_im_t], axis=1).astype(jnp.bfloat16)
    return stage_a, inv_a, fwd_table, inv_table


def complex_stage(table, real_part, imag_part):
    inner = real_part.shape[1]
    a = jnp.einsum(
        "kjm,kml->kjl", table, real_part.astype(jnp.bfloat16),
        preferred_element_type=jnp.float32,
    )
    b = jnp.einsum(
        "kjm,kml->kjl", table, imag_part.astype(jnp.bfloat16),
        preferred_element_type=jnp.float32,
    )
    out_real = a[:, :inner] - b[:, inner:]
    out_imag = b[:, :inner] + a[:, inner:]
    return out_real, out_imag


def forward_spectrum(slab, tables):
    stage_a, _, fwd_table, _ = tables
    half = fwd_table.shape[0]
    first = jnp.einsum("kn,nml->kml", stage_a, slab, precision=full_precision)
    return complex_stage(fwd_table, first[:half], first[half:])


def inverse_spectrum(prod_re, prod_im, tables):
    _, inv_a, _, inv_table = tables
    back_re, back_im = complex_stage(inv_table, prod_re, prod_im)
    both = jnp.concatenate([back_re, back_im], axis=0)
    return jnp.einsum("nk,kml->nml", inv_a, both, precision=full_precision)


def middle_kernel(
    sig_re_ref, sig_im_ref, taps_re_ref, taps_im_ref, fwd_ref, inv_ref,
    pair_re_ref, pair_im_ref, cross_re_ref, cross_im_ref,
):
    inner = sig_re_ref.shape[1]
    lanes = sig_re_ref.shape[2]
    half_lanes = lanes // 2
    fwd = fwd_ref[0]
    inv = inv_ref[0]

    def stage(table, real_part, imag_part):
        a = jnp.dot(table, real_part.astype(jnp.bfloat16), preferred_element_type=jnp.float32)
        b = jnp.dot(table, imag_part.astype(jnp.bfloat16), preferred_element_type=jnp.float32)
        return a[:inner] - b[inner:], b[:inner] + a[inner:]

    sig_re, sig_im = stage(fwd, sig_re_ref[0], sig_im_ref[0])
    taps_re, taps_im = stage(fwd, taps_re_ref[0], taps_im_ref[0])
    lane = lax.broadcasted_iota(jnp.int32, (inner, lanes), 1)
    taps_im = jnp.where(lane < half_lanes, taps_im, -taps_im)
    prod_re = sig_re * taps_re - sig_im * taps_im
    prod_im = sig_re * taps_im + sig_im * taps_re
    out_re, out_im = stage(inv, prod_re, prod_im)
    pair_re_ref[0] = out_re
    pair_im_ref[0] = out_im
    turned_re = pltpu.roll(sig_re, half_lanes, 1)
    turned_im = pltpu.roll(sig_im, half_lanes, 1)
    prod_re = sig_re * turned_re + sig_im * turned_im
    prod_im = sig_re * turned_im - sig_im * turned_re
    out_re, out_im = stage(inv, prod_re, prod_im)
    cross_re_ref[0] = out_re
    cross_im_ref[0] = out_im


def spectral_middle(sig_first, taps_first, fwd_table, inv_table):
    half, rows2, inner = fwd_table.shape
    lanes = sig_first.shape[2]
    block = pl.BlockSpec((1, inner, lanes), lambda k: (k, 0, 0))
    block_im = pl.BlockSpec((1, inner, lanes), lambda k: (k + half, 0, 0))
    table_block = pl.BlockSpec((1, rows2, inner), lambda k: (k, 0, 0))
    out_shape = jax.ShapeDtypeStruct((half, inner, lanes), jnp.float32)
    flops = half * 6 * 2 * 2 * rows2 * inner * lanes
    bytes_accessed = half * (8 * inner * lanes * 4 + 2 * rows2 * inner * 2)
    return pl.pallas_call(
        middle_kernel,
        grid=(half,),
        in_specs=[block, block_im, block, block_im, table_block, table_block],
        out_specs=[block] * 4,
        out_shape=[out_shape] * 4,
        cost_estimate=pl.CostEstimate(
            flops=flops, transcendentals=0, bytes_accessed=bytes_accessed
        ),
    )(sig_first, sig_first, taps_first, taps_first, fwd_table, inv_table)


def spectral_products(signals, taps, carry):
    seq_length, lanes = signals.shape
    tables = spectral_tables(seq_length)
    stage_a, _, fwd_table, inv_table = tables
    inner = fwd_table.shape[2]
    rows = seq_length // inner
    taps_first = jnp.einsum(
        "kn,nml->kml", stage_a, taps.reshape(rows, inner, lanes), precision=full_precision
    )
    sig_first = jnp.einsum(
        "kn,nml->kml", stage_a, signals.reshape(rows, inner, lanes), precision=full_precision
    )
    pair_re, pair_im, cross_re, cross_im = spectral_middle(
        sig_first, taps_first, fwd_table, inv_table
    )
    carry, pair_re, pair_im, cross_re, cross_im = lax.optimization_barrier(
        (carry, pair_re, pair_im, cross_re, cross_im)
    )
    return tables, (pair_re, pair_im), (cross_re, cross_im), carry


def spectral_inverse(back_re, back_im, tables):
    inv_a = tables[1]
    both = jnp.concatenate([back_re, back_im], axis=0)
    return jnp.einsum("nk,kml->nml", inv_a, both, precision=full_precision)


def on_device(query_proj, key_proj, value_proj, cotangent, long_filter, skip_gain):
    query_rows = query_proj[0].astype(jnp.float32)
    key_rows = key_proj[0].astype(jnp.float32)
    value_rows = value_proj[0].astype(jnp.float32)
    cot_rows = cotangent[0].astype(jnp.float32)
    local_length, chan_width = query_proj.shape[1], query_proj.shape[2]
    seq_count = lax.axis_size("seq")
    batch_count = lax.axis_size("dp")
    groups = seq_count * batch_count
    share = chan_width // groups
    seq_length = seq_count * local_length
    factor = (batch_count * seq_length) ** (-0.5)
    mixed = (key_rows * value_rows).astype(jnp.bfloat16)
    weighted = (cot_rows * query_rows).astype(jnp.bfloat16)

    mixed_wide = mixed.astype(jnp.float32)
    weighted_wide = weighted.astype(jnp.float32)
    gain_part = jnp.sum(weighted_wide * mixed_wide, axis=0)

    pair = jnp.stack([mixed.T, weighted.T], axis=0).reshape(2, groups, share, local_length)
    pair = jnp.transpose(pair, (1, 0, 2, 3)).reshape(groups, 2 * share, local_length)
    half_length = local_length // batch_count
    taps_t = long_filter.T.reshape(groups, share, batch_count, half_length)
    taps_mine = lax.dynamic_index_in_dim(taps_t, lax.axis_index("dp"), axis=2, keepdims=False)
    taps_rows = share * half_length // local_length
    taps_mine = taps_mine.astype(jnp.bfloat16).reshape(groups, taps_rows, local_length)
    taps_got = lax.all_to_all(taps_mine, ("seq", "dp"), 0, 0, tiled=True)
    got = lax.all_to_all(pair, ("seq", "dp"), 0, 0, tiled=True)
    gain_part, got = lax.optimization_barrier((gain_part, got))
    total = gain_part
    distance = 1
    while distance < groups:
        partners = [(i, i ^ distance) for i in range(groups)]
        total = total + lax.ppermute(total, ("seq", "dp"), partners)
        distance *= 2
    grad_skip = factor * total

    pair_t = got.reshape(seq_count, batch_count, 2, share, local_length)
    signals = jnp.transpose(pair_t, (0, 4, 2, 1, 3)).reshape(seq_length, 2 * batch_count * share)
    taps_t = taps_got.reshape(seq_count, batch_count, share, half_length)
    taps = jnp.transpose(taps_t, (0, 1, 3, 2)).reshape(seq_length, 1, share)
    taps = jnp.broadcast_to(taps, (seq_length, 2 * batch_count, share)).reshape(
        seq_length, 2 * batch_count * share
    )

    tables, pair_spec, cross_spec, grad_skip = spectral_products(
        signals.astype(jnp.float32), taps.astype(jnp.float32), grad_skip
    )
    pair_vals = spectral_inverse(pair_spec[0], pair_spec[1], tables)
    pair_vals = pair_vals.reshape(seq_length, 2, batch_count, share)

    pair_back = pair_vals.astype(jnp.bfloat16).reshape(
        seq_count, local_length, 2, batch_count, share
    )
    pair_back = jnp.transpose(pair_back, (0, 3, 2, 4, 1)).reshape(
        groups, 2 * share, local_length
    )
    pair_home = lax.all_to_all(pair_back, ("seq", "dp"), 0, 0, tiled=True)

    cross = spectral_inverse(cross_spec[0], cross_spec[1], tables)
    cross = cross.reshape(seq_length, 2, batch_count, share)
    slope = jnp.sum(cross[:, 0], axis=1)
    slope_blocks = jnp.swapaxes(slope.astype(jnp.bfloat16).reshape(seq_count, local_length, share), 1, 2)
    slope_send = jnp.broadcast_to(
        slope_blocks[:, None], (seq_count, batch_count, share, local_length)
    ).reshape(groups, share, local_length)
    slope_home = lax.all_to_all(slope_send, ("seq", "dp"), 0, 0, tiled=True)

    pair_home = pair_home.reshape(groups, 2, share, local_length)
    pair_home = jnp.transpose(pair_home, (1, 0, 2, 3)).reshape(2, chan_width, local_length)
    conv_rows = pair_home[0].T.astype(jnp.float32)
    corr_rows = pair_home[1].T.astype(jnp.float32)
    grad_filter = factor * slope_home.reshape(chan_width, local_length).T.astype(jnp.float32)

    signal = conv_rows + skip_gain[None, :] * mixed_wide
    output = (query_rows * signal).astype(jnp.bfloat16)
    grad_query = (cot_rows * signal).astype(jnp.bfloat16)
    back = corr_rows + skip_gain[None, :] * weighted_wide
    grad_key = (back * value_rows).astype(jnp.bfloat16)
    grad_value = (back * key_rows).astype(jnp.bfloat16)
    return (
        output[None],
        grad_query[None],
        grad_key[None],
        grad_value[None],
        grad_filter,
        grad_skip,
    )


def solution(mesh):
    return jax.shard_map(
        on_device,
        mesh=mesh,
        in_specs=(
            P("dp", "seq", "chan"),
            P("dp", "seq", "chan"),
            P("dp", "seq", "chan"),
            P("dp", "seq", "chan"),
            P("seq", "chan"),
            P("chan"),
        ),
        out_specs=(
            P("dp", "seq", "chan"),
            P("dp", "seq", "chan"),
            P("dp", "seq", "chan"),
            P("dp", "seq", "chan"),
            P("seq", "chan"),
            P("chan"),
        ),
        check_vma=False,
    )
```

profile of v0, /device:TPU:1, one launch (start us, length us, event | category | flops | bytes accessed | tf_op | source)
XLA Modules:
  0.0 187.0 jit_solution(17173113024927655699)
XLA Ops:
  5.6 10.1 %all-to-all-start = ((bf16[16,64,512]{2,1,0:T(8,128)(2,1)}), bf16[16,64,512]{2,1,0:T(8,128)(2,1)}, u32[]{:S(2)}, u32[]{:S(2)}) async-start(bf16[16,64,512]{2,1,0:T(8,128)(2,1)} %bitcast.121), calls=%async_computation | async-start | bytes 2097152 | tf_op jit(solution)/shard_map/all_to_all | solution.py:187
  19.1 3.2 %subtract_convert_fusion = (bf16[33,128,128]{2,1,0:T(8,128)(2,1)S(1)}, bf16[33,128,128]{2,1,0:T(8,128)(2,1)S(1)}, bf16[33,128,128]{2,1,0:T(8,128)(2,1)}, bf16[33,128,128]{2,1,0:T(8,128)(2,1)}) fusion(f32[33,128]{1,0:T(8,128)S(1)} %fusion.44, f32[33,128]{1,0:T(8,128)S(1)} %fusion.45, f32[128,128]{1,0:T(8,128)S(1)} %fusion.24, f32[128,128]{1,0:T(8,128)S(1)} %fusion.25), kind=kLoop, calls=%fused_computation.7 | loop fusion | flops 9191424 | bytes 4490240 | tf_op jit(solution)/shard_map/convert.8
  22.3 20.5 %all-to-all-done = bf16[16,64,512]{2,1,0:T(8,128)(2,1)} async-done(((bf16[16,64,512]{2,1,0:T(8,128)(2,1)}), bf16[16,64,512]{2,1,0:T(8,128)(2,1)}, u32[]{:S(2)}, u32[]{:S(2)}) %all-to-all-start) | async-done | bytes 1048608 | tf_op jit(solution)/shard_map/all_to_all | solution.py:187
  42.8 4.5 %all-to-all-start.1 = ((bf16[16,16,512]{2,1,0:T(8,128)(2,1)}), bf16[16,16,512]{2,1,0:T(8,128)(2,1)S(1)}, u32[]{:S(2)}, u32[]{:S(2)}) async-start(bf16[16,16,512]{2,1,0:T(8,128)(2,1)} %convert_element_type.156), calls=%async_computation.1 | async-start | bytes 524288 | tf_op jit(solution)/shard_map/all_to_all | solution.py:186
  47.3 4.0 %pad_maximum_fusion.2 = (bf16[33,256,128]{2,1,0:T(8,128)(2,1)}, bf16[33,256,128]{2,1,0:T(8,128)(2,1)}) fusion(bf16[33,128,128]{2,1,0:T(8,128)(2,1)S(1)} %get-tuple-element.44, bf16[33,128,128]{2,1,0:T(8,128)(2,1)} %get-tuple-element.46, bf16[33,128,128]{2,1,0:T(8,128)(2,1)} %get-tuple-element.45, bf16[33,128,128]{2,1,0:T(8,128)(2,1)S(1)} %get-tuple-element.43), kind=kLoop, calls=%fused_computation.4 | loop fusion | flops 8650752 | bytes 8650752 | tf_op jit(solution)/shard_map/concatenate | solution.py:43
  52.9 4.5 %all-to-all-done.1 = bf16[16,16,512]{2,1,0:T(8,128)(2,1)S(1)} async-done(((bf16[16,16,512]{2,1,0:T(8,128)(2,1)}), bf16[16,16,512]{2,1,0:T(8,128)(2,1)S(1)}, u32[]{:S(2)}, u32[]{:S(2)}) %all-to-all-start.1) | async-done | bytes 262176 | tf_op jit(solution)/shard_map/all_to_all | solution.py:186
  58.3 1.5 copy.27
  60.5 2.1 %fusion.47 = f32[66,128,128]{2,0,1:T(8,128)S(1)} fusion(bf16[32,128,128]{2,0,1:T(8,128)(2,1)S(1)} %copy.27, f32[33,32]{0,1:T(8,128)S(1)} %get-tuple-element.51, f32[33,32]{0,1:T(8,128)S(1)} %get-tuple-element.52), kind=kOutput, calls=%fused_computation.87 | convolution fusion | flops 415238208 | bytes 5382400 | tf_op jit(solution)/shard_map/kn,nml->kml/dot_general | solution.py:139
  62.6 2.9 %copy.30.taps_re_ref.taps_im_ref = f32[66,128,128]{2,1,0:T(8,128)} copy(f32[66,128,128]{2,0,1:T(8,128)S(1)} %fusion.47) | data formatting | bytes 8650752 | tf_op jit(solution)/shard_map/kn,nml->kml/dot_general | solution.py:139
  65.5 1.8 copy.54
  68.0 1.5 copy.24
  69.5 1.8 collective-permute-start.2
  71.3 2.1 %fusion.48 = f32[66,128,128]{2,0,1:T(8,128)S(1)} fusion(bf16[32,128,128]{2,0,1:T(8,128)(2,1)S(1)} %copy.24, f32[33,32]{0,1:T(8,128)S(1)} %get-tuple-element.51, f32[33,32]{0,1:T(8,128)S(1)} %get-tuple-element.52), kind=kOutput, calls=%fused_computation.88 | convolution fusion | flops 415238208 | bytes 5382400 | tf_op jit(solution)/shard_map/kn,nml->kml/dot_general | solution.py:142
  73.4 2.8 %copy.28.sig_re_ref.sig_im_ref = f32[66,128,128]{2,1,0:T(8,128)} copy(f32[66,128,128]{2,0,1:T(8,128)S(1)} %fusion.48) | data formatting | bytes 8650752 | tf_op jit(solution)/shard_map/kn,nml->kml/dot_general | solution.py:142
  76.2 2.0 %collective-permute-start.3 = (f32[512]{0:T(512)S(1)}, f32[512]{0:T(512)S(1)}, u32[]{:S(2)}, u32[]{:S(2)}) collective-permute-start(f32[512]{0:T(512)S(1)} %add.85), channel_id=1, source_target_pairs={{0,128},{1,129},{32,160},{33,161},{64,192},{65,193},{96,224},{97,2... | collective-permute-start | bytes 6152 | tf_op jit(solution)/shard_map/ppermute | solution.py:193
  78.3 26.4 %shard_map.109 = (f32[33,128,128]{2,1,0:T(8,128)}, f32[33,128,128]{2,1,0:T(8,128)}, f32[33,128,128]{2,1,0:T(8,128)}, f32[33,128,128]{2,1,0:T(8,128)}) custom-call(f32[66,128,128]{2,1,0:T(8,128)} %copy.28.sig_re_ref.sig_im_ref, f32[66,128,128]{2,1,0:T(8,128)} %copy.28.sig_re_ref.sig_im_ref, f32[66,128,128]{2,1,0:T(8,128)} %copy.30.taps_re_ref.taps_im_ref, ...), custom_call_target="tpu_custom_call" | custom-call | flops 3321888768 | bytes 21626880 | tf_op jit(solution)/shard_map/pallas_call | solution.py:121
  105.2 4.8 %pad_maximum_fusion.1 = f32[66,128,128]{2,1,0:T(8,128)} fusion(f32[33,128,128]{2,1,0:T(8,128)} %get-tuple-element.26, f32[33,128,128]{2,1,0:T(8,128)} %get-tuple-element.25), kind=kLoop, calls=%fused_computation.3 | loop fusion | flops 1081344 | bytes 8650752 | tf_op jit(solution)/shard_map/concatenate | solution.py:156
  110.1 5.7 %copy.43 = f32[66,128,128]{1,0,2:T(8,128)} copy(f32[66,128,128]{2,1,0:T(8,128)} %pad_maximum_fusion.1) | data formatting | bytes 8650752 | tf_op jit(solution)/shard_map/concatenate | solution.py:156
  115.8 4.3 %fusion.49 = f32[32,128,128]{1,0,2:T(8,128)S(1)} fusion(f32[66,128,128]{1,0,2:T(8,128)} %copy.43, f32[32,33]{1,0:T(8,128)S(1)} %get-tuple-element.50, f32[32,33]{1,0:T(8,128)S(1)} %get-tuple-element.49), kind=kOutput, calls=%fused_computation.89 | convolution fusion | flops 415238208 | bytes 6430976 | tf_op jit(solution)/shard_map/nk,kml->nml/dot_general | solution.py:157
  120.1 1.6 reshape.173
  124.2 5.9 %all-to-all-start.3 = ((bf16[16,32,512]{2,1,0:T(8,128)(2,1)}), bf16[16,32,512]{2,1,0:T(8,128)(2,1)}, u32[]{:S(2)}, u32[]{:S(2)}) async-start(bf16[16,32,512]{2,1,0:T(8,128)(2,1)} %bitcast.126), calls=%async_computation.3 | async-start | bytes 1048576 | tf_op jit(solution)/shard_map/all_to_all | solution.py:226
  130.1 2.0 %pad_maximum_fusion = f32[66,128,128]{2,1,0:T(8,128)S(1)} fusion(f32[33,128,128]{2,1,0:T(8,128)} %get-tuple-element.24, f32[33,128,128]{2,1,0:T(8,128)S(1)} %copy-done.8), kind=kLoop, calls=%fused_computation.2 | loop fusion | flops 1081344 | bytes 8650752 | tf_op jit(solution)/shard_map/concatenate | solution.py:156
  132.1 5.0 %fusion.2 = bf16[32,128,128]{2,0,1:T(8,128)(2,1)S(1)} fusion(f32[66,128,128]{2,1,0:T(8,128)S(1)} %pad_maximum_fusion, f32[32,33]{1,0:T(8,128)S(1)} %get-tuple-element.50, f32[32,33]{1,0:T(8,128)S(1)} %get-tuple-element.49), kind=kOutput, calls=%fused_computation.10 | convolution fusion | flops 415762496 | bytes 5382400 | tf_op jit(solution)/shard_map/nk,kml->nml/dot_general | solution.py:157
  137.1 1.5 copy.33
  140.6 5.2 %all-to-all-done.3 = bf16[16,32,512]{2,1,0:T(8,128)(2,1)} async-done(((bf16[16,32,512]{2,1,0:T(8,128)(2,1)}), bf16[16,32,512]{2,1,0:T(8,128)(2,1)}, u32[]{:S(2)}, u32[]{:S(2)}) %all-to-all-start.3) | async-done | bytes 524320 | tf_op jit(solution)/shard_map/all_to_all | solution.py:226
  145.8 4.6 %all-to-all-start.2 = ((bf16[16,64,512]{2,1,0:T(8,128)(2,1)}), bf16[16,64,512]{2,1,0:T(8,128)(2,1)}, u32[]{:S(2)}, u32[]{:S(2)}) async-start(bf16[16,64,512]{2,1,0:T(8,128)(2,1)} %bitcast.18), calls=%async_computation.2 | async-start | bytes 2097152 | tf_op jit(solution)/shard_map/all_to_all | solution.py:217
  150.4 2.2 %convert_multiply_fusion.9 = f32[16,32,512]{2,1,0:T(8,128)} fusion(bf16[16,32,512]{2,1,0:T(8,128)(2,1)} %all-to-all-done.3), kind=kLoop, calls=%fused_computation.34 | loop fusion | flops 524288 | bytes 1572864 | tf_op jit(solution)/shard_map/mul | solution.py:232
  152.6 2.7 %copy.42 = f32[512,512]{1,0:T(8,128)} copy(f32[512,512]{0,1:T(8,128)} %bitcast.125) | data formatting | bytes 2097152
  155.3 22.2 %all-to-all-done.2 = bf16[16,64,512]{2,1,0:T(8,128)(2,1)} async-done(((bf16[16,64,512]{2,1,0:T(8,128)(2,1)}), bf16[16,64,512]{2,1,0:T(8,128)(2,1)}, u32[]{:S(2)}, u32[]{:S(2)}) %all-to-all-start.2) | async-done | bytes 1048608 | tf_op jit(solution)/shard_map/all_to_all | solution.py:217
  178.8 2.0 %fusion.14 = (bf16[1,512,512]{1,2,0:T(8,128)(2,1)}, bf16[1,512,512]{1,2,0:T(8,128)(2,1)}, bf16[1,512,512]{1,2,0:T(8,128)(2,1)}, bf16[1,512,512]{1,2,0:T(8,128)(2,1)}) fusion(bf16[512,512]{0,1:T(8,128)(2,1)S(1)} %copy-done.5, bf16[1,16,32,512]{3,2,0,1:T(8,128)(2,1)S(1)} %get-tuple-element.41, bf16[1,512,512]{1,2,0:T(8,128)(2,1)S(1)} %copy-done.1, ...), kind=kLoop, calls=%fused_computation.35 | loop fusion | flops 5242880 | bytes 6293504 | tf_op jit(solution)/shard_map/broadcast_in_dim | solution.py:244
  180.9 2.1 %copy.38 = bf16[1,512,512]{2,1,0:T(8,128)(2,1)} copy(bf16[1,512,512]{1,2,0:T(8,128)(2,1)} %get-tuple-element.47) | data formatting | bytes 1048576
  183.0 2.0 %copy.39 = bf16[1,512,512]{2,1,0:T(8,128)(2,1)} copy(bf16[1,512,512]{1,2,0:T(8,128)(2,1)} %get-tuple-element.48) | data formatting | bytes 1048576
  (73 shorter events, 20.4 us)
Async XLA Ops:
  0.6 2.6 %copy-start.12 = (bf16[1,512,512]{2,1,0:T(8,128)(2,1)S(1)}, bf16[1,512,512]{2,1,0:T(8,128)(2,1)}, u32[]{:S(2)}) copy-start(bf16[1,512,512]{2,1,0:T(8,128)(2,1)} %param.7) | copy-start | bytes 1572868
  0.6 2.8 %copy-start.13 = (bf16[1,512,512]{2,1,0:T(8,128)(2,1)S(1)}, bf16[1,512,512]{2,1,0:T(8,128)(2,1)}, u32[]{:S(2)}) copy-start(bf16[1,512,512]{2,1,0:T(8,128)(2,1)} %param.8) | copy-start | bytes 1572868
  3.5 0.8 copy-start
  3.7 0.8 copy-start.2
  4.1 1.5 copy-start.4
  4.1 1.4 copy-start.6
  5.6 10.1 %copy-start.11 = (f32[512,512]{1,0:T(8,128)S(1)}, f32[512,512]{1,0:T(8,128)}, u32[]{:S(2)}) copy-start(f32[512,512]{1,0:T(8,128)} %param.10) | copy-start | bytes 3145732
  5.6 37.2 %all-to-all-start = ((bf16[16,64,512]{2,1,0:T(8,128)(2,1)}), bf16[16,64,512]{2,1,0:T(8,128)(2,1)}, u32[]{:S(2)}, u32[]{:S(2)}) async-start(bf16[16,64,512]{2,1,0:T(8,128)(2,1)} %bitcast.121), calls=%async_computation | async-start | bytes 2097152 | tf_op jit(solution)/shard_map/all_to_all | solution.py:187
  42.8 14.6 %all-to-all-start.1 = ((bf16[16,16,512]{2,1,0:T(8,128)(2,1)}), bf16[16,16,512]{2,1,0:T(8,128)(2,1)S(1)}, u32[]{:S(2)}, u32[]{:S(2)}) async-start(bf16[16,16,512]{2,1,0:T(8,128)(2,1)} %convert_element_type.156), calls=%async_computation.1 | async-start | bytes 524288 | tf_op jit(solution)/shard_map/all_to_all | solution.py:186
  51.4 8.5 %collective-permute-start = (f32[512]{0:T(512)S(1)}, f32[512]{0:T(512)S(1)}, u32[]{:S(2)}, u32[]{:S(2)}) collective-permute-start(f32[512]{0:T(512)S(1)} %get-tuple-element.17), channel_id=1, source_target_pairs={{0,1},{1,0},{32,33},{33,32},{64,65},{65,64},{96,97},{97,96},{128,1... | collective-permute-start | bytes 6152 | tf_op jit(solution)/shard_map/ppermute | solution.py:193
  59.9 9.7 %collective-permute-start.1 = (f32[512]{0:T(512)S(1)}, f32[512]{0:T(512)S(1)}, u32[]{:S(2)}, u32[]{:S(2)}) collective-permute-start(f32[512]{0:T(512)S(1)} %add.83), channel_id=1, source_target_pairs={{0,32},{1,33},{32,0},{33,1},{64,96},{65,97},{96,64},{97,65},{128,1... | collective-permute-start | bytes 6152 | tf_op jit(solution)/shard_map/ppermute | solution.py:193
  69.5 6.7 %collective-permute-start.2 = (f32[512]{0:T(512)S(1)}, f32[512]{0:T(512)S(1)}, u32[]{:S(2)}, u32[]{:S(2)}) collective-permute-start(f32[512]{0:T(512)S(1)} %add.84), channel_id=1, source_target_pairs={{0,64},{1,65},{32,96},{33,97},{64,0},{65,1},{96,32},{97,33},{128,1... | collective-permute-start | bytes 6152 | tf_op jit(solution)/shard_map/ppermute | solution.py:193
  76.2 28.4 %collective-permute-start.3 = (f32[512]{0:T(512)S(1)}, f32[512]{0:T(512)S(1)}, u32[]{:S(2)}, u32[]{:S(2)}) collective-permute-start(f32[512]{0:T(512)S(1)} %add.85), channel_id=1, source_target_pairs={{0,128},{1,129},{32,160},{33,161},{64,192},{65,193},{96,224},{97,2... | collective-permute-start | bytes 6152 | tf_op jit(solution)/shard_map/ppermute | solution.py:193
  121.7 8.4 %copy-start.8 = (f32[33,128,128]{2,1,0:T(8,128)S(1)}, f32[33,128,128]{2,1,0:T(8,128)}, u32[]{:S(2)}) copy-start(f32[33,128,128]{2,1,0:T(8,128)} %get-tuple-element.23) | copy-start | bytes 6488068
  124.2 21.6 %all-to-all-start.3 = ((bf16[16,32,512]{2,1,0:T(8,128)(2,1)}), bf16[16,32,512]{2,1,0:T(8,128)(2,1)}, u32[]{:S(2)}, u32[]{:S(2)}) async-start(bf16[16,32,512]{2,1,0:T(8,128)(2,1)} %bitcast.126), calls=%async_computation.3 | async-start | bytes 1048576 | tf_op jit(solution)/shard_map/all_to_all | solution.py:226
  145.8 31.7 %all-to-all-start.2 = ((bf16[16,64,512]{2,1,0:T(8,128)(2,1)}), bf16[16,64,512]{2,1,0:T(8,128)(2,1)}, u32[]{:S(2)}, u32[]{:S(2)}) async-start(bf16[16,64,512]{2,1,0:T(8,128)(2,1)} %bitcast.18), calls=%async_computation.2 | async-start | bytes 2097152 | tf_op jit(solution)/shard_map/all_to_all | solution.py:217
  152.6 26.2 %copy-start.1 = (bf16[1,512,512]{1,2,0:T(8,128)(2,1)S(1)}, bf16[1,512,512]{1,2,0:T(8,128)(2,1)}, u32[]{:S(2)}) copy-start(bf16[1,512,512]{1,2,0:T(8,128)(2,1)} %copy-done) | copy-start | bytes 1572868
  152.6 26.2 %copy-start.3 = (bf16[1,512,512]{1,2,0:T(8,128)(2,1)S(1)}, bf16[1,512,512]{1,2,0:T(8,128)(2,1)}, u32[]{:S(2)}) copy-start(bf16[1,512,512]{1,2,0:T(8,128)(2,1)} %copy-done.2) | copy-start | bytes 1572868
  152.6 26.2 %copy-start.5 = (bf16[512,512]{0,1:T(8,128)(2,1)S(1)}, bf16[512,512]{0,1:T(8,128)(2,1)}, u32[]{:S(2)}) copy-start(bf16[512,512]{0,1:T(8,128)(2,1)} %copy-done.4) | copy-start | bytes 1572868
  152.6 26.2 %copy-start.7 = (bf16[512,512]{0,1:T(8,128)(2,1)S(1)}, bf16[512,512]{0,1:T(8,128)(2,1)}, u32[]{:S(2)}) copy-start(bf16[512,512]{0,1:T(8,128)(2,1)} %copy-done.6) | copy-start | bytes 1572868
  152.6 26.2 %copy-start.14 = (f32[512]{0:T(512)S(1)}, f32[512]{0:T(512)}, u32[]{:S(2)}) copy-start(f32[512]{0:T(512)} %param.11) | copy-start | bytes 6148
  180.8 4.2 %copy-start.10 = (bf16[1,512,512]{1,2,0:T(8,128)(2,1)S(1)}, bf16[1,512,512]{1,2,0:T(8,128)(2,1)}, u32[]{:S(2)}) copy-start(bf16[1,512,512]{1,2,0:T(8,128)(2,1)} %get-tuple-element.38) | copy-start | bytes 1572868
  180.8 5.2 %copy-start.9 = (bf16[1,512,512]{1,2,0:T(8,128)(2,1)S(1)}, bf16[1,512,512]{1,2,0:T(8,128)(2,1)}, u32[]{:S(2)}) copy-start(bf16[1,512,512]{1,2,0:T(8,128)(2,1)} %get-tuple-element.37) | copy-start | bytes 1572868
where the time goes:
time: 190 us; the launch traced here: 187 us
  waiting for transfers between devices  52.4 us (28%)
  local copies, waits for them, and re-layouts  41.1 us (22%)
  starting transfers between devices  31 us (16%)
  Pallas kernels  26.4 us (14%)
  other arithmetic  21.7 us (11%)
  matrix products  13.4 us (7%)
    pallas_call x1, Pallas kernels, spectral_middle(): pl.pallas_call(middle_kernel, grid=(half,), in_specs=[block, block_im, bl...  26.4 us
    all_to_all x1, waiting for transfers between devices, on_device(): pair_home = lax.all_to_all(pair_back, ('seq', 'dp'), 0, 0, tiled=True)  22.2 us
    all_to_all x1, waiting for transfers between devices, on_device(): got = lax.all_to_all(pair, ('seq', 'dp'), 0, 0, tiled=True)  20.5 us
    unnamed x41, local copies, waits for them, and re-layouts  12.5 us
    all_to_all x1, starting transfers between devices, on_device(): got = lax.all_to_all(pair, ('seq', 'dp'), 0, 0, tiled=True)  10.1 us
    dot_general x2, matrix products, spectral_inverse(): return jnp.einsum('nk,kml->nml', inv_a, both, precision=full_precision)  9.24 us
    concatenate x2, other arithmetic, spectral_inverse(): both = jnp.concatenate([back_re, back_im], axis=0)  6.85 us
    all_to_all x1, starting transfers between devices, on_device(): slope_home = lax.all_to_all(slope_send, ('seq', 'dp'), 0, 0, tiled=True)  5.91 us
  transfers between devices with their start and end apart: 8, of which 4 were waited for; matrix products, arithmetic and copies ran while one was open for 23% of the time, Pallas kernels for 14%

commit v1 on v0

--- a/solution.py
+++ b/solution.py
@@ -80,47 +80,49 @@
     sig_re_ref, sig_im_ref, taps_re_ref, taps_im_ref, fwd_ref, inv_ref,
     pair_re_ref, pair_im_ref, cross_re_ref, cross_im_ref,
 ):
-    inner = sig_re_ref.shape[1]
-    lanes = sig_re_ref.shape[2]
+    steps, inner, lanes = sig_re_ref.shape
     half_lanes = lanes // 2
-    fwd = fwd_ref[0]
-    inv = inv_ref[0]
-
-    def stage(table, real_part, imag_part):
-        a = jnp.dot(table, real_part.astype(jnp.bfloat16), preferred_element_type=jnp.float32)
-        b = jnp.dot(table, imag_part.astype(jnp.bfloat16), preferred_element_type=jnp.float32)
-        return a[:inner] - b[inner:], b[:inner] + a[inner:]
-
-    sig_re, sig_im = stage(fwd, sig_re_ref[0], sig_im_ref[0])
-    taps_re, taps_im = stage(fwd, taps_re_ref[0], taps_im_ref[0])
     lane = lax.broadcasted_iota(jnp.int32, (inner, lanes), 1)
-    taps_im = jnp.where(lane < half_lanes, taps_im, -taps_im)
-    prod_re = sig_re * taps_re - sig_im * taps_im
-    prod_im = sig_re * taps_im + sig_im * taps_re
-    out_re, out_im = stage(inv, prod_re, prod_im)
-    pair_re_ref[0] = out_re
-    pair_im_ref[0] = out_im
-    turned_re = pltpu.roll(sig_re, half_lanes, 1)
-    turned_im = pltpu.roll(sig_im, half_lanes, 1)
-    prod_re = sig_re * turned_re + sig_im * turned_im
-    prod_im = sig_re * turned_im - sig_im * turned_re
-    out_re, out_im = stage(inv, prod_re, prod_im)
-    cross_re_ref[0] = out_re
-    cross_im_ref[0] = out_im
+    for step in range(steps):
+        first = jnp.concatenate(
+            [sig_re_ref[step], sig_im_ref[step], taps_re_ref[step], taps_im_ref[step]], axis=1
+        ).astype(jnp.bfloat16)
+        spec = jnp.dot(fwd_ref[step], first, preferred_element_type=jnp.float32)
+        sig_re = spec[:inner, 0:lanes] - spec[inner:, lanes : 2 * lanes]
+        sig_im = spec[:inner, lanes : 2 * lanes] + spec[inner:, 0:lanes]
+        taps_re = spec[:inner, 2 * lanes : 3 * lanes] - spec[inner:, 3 * lanes :]
+        taps_im = spec[:inner, 3 * lanes :] + spec[inner:, 2 * lanes : 3 * lanes]
+        taps_im = jnp.where(lane < half_lanes, taps_im, -taps_im)
+        pair_re = sig_re * taps_re - sig_im * taps_im
+        pair_im = sig_re * taps_im + sig_im * taps_re
+        turned_re = pltpu.roll(sig_re, half_lanes, 1)
+        turned_im = pltpu.roll(sig_im, half_lanes, 1)
+        cross_re = sig_re * turned_re + sig_im * turned_im
+        cross_im = sig_re * turned_im - sig_im * turned_re
+        second = jnp.concatenate([pair_re, pair_im, cross_re, cross_im], axis=1).astype(
+            jnp.bfloat16
+        )
+        back = jnp.dot(inv_ref[step], second, preferred_element_type=jnp.float32)
+        pair_re_ref[step] = back[:inner, 0:lanes] - back[inner:, lanes : 2 * lanes]
+        pair_im_ref[step] = back[:inner, lanes : 2 * lanes] + back[inner:, 0:lanes]
+        cross_re_ref[step] = back[:inner, 2 * lanes : 3 * lanes] - back[inner:, 3 * lanes :]
+        cross_im_ref[step] = back[:inner, 3 * lanes :] + back[inner:, 2 * lanes : 3 * lanes]
 
 
 def spectral_middle(sig_first, taps_first, fwd_table, inv_table):
     half, rows2, inner = fwd_table.shape
     lanes = sig_first.shape[2]
-    block = pl.BlockSpec((1, inner, lanes), lambda k: (k, 0, 0))
-    block_im = pl.BlockSpec((1, inner, lanes), lambda k: (k + half, 0, 0))
-    table_block = pl.BlockSpec((1, rows2, inner), lambda k: (k, 0, 0))
+    steps = 3 if half % 3 == 0 else 1
+    count = half // steps
+    block = pl.BlockSpec((steps, inner, lanes), lambda k: (k, 0, 0))
+    block_im = pl.BlockSpec((steps, inner, lanes), lambda k: (k + count, 0, 0))
+    table_block = pl.BlockSpec((steps, rows2, inner), lambda k: (k, 0, 0))
     out_shape = jax.ShapeDtypeStruct((half, inner, lanes), jnp.float32)
-    flops = half * 6 * 2 * 2 * rows2 * inner * lanes
+    flops = half * 2 * 2 * rows2 * inner * 4 * lanes
     bytes_accessed = half * (8 * inner * lanes * 4 + 2 * rows2 * inner * 2)
     return pl.pallas_call(
         middle_kernel,
-        grid=(half,),
+        grid=(count,),
         in_specs=[block, block_im, block, block_im, table_block, table_block],
         out_specs=[block] * 4,
         out_shape=[out_shape] * 4,
@@ -184,6 +186,7 @@
     taps_rows = share * half_length // local_length
     taps_mine = taps_mine.astype(jnp.bfloat16).reshape(groups, taps_rows, local_length)
     taps_got = lax.all_to_all(taps_mine, ("seq", "dp"), 0, 0, tiled=True)
+    taps_got, pair = lax.optimization_barrier((taps_got, pair))
     got = lax.all_to_all(pair, ("seq", "dp"), 0, 0, tiled=True)
     gain_part, got = lax.optimization_barrier((gain_part, got))
     total = gain_part

time: 190 us -> 178 us (0.937)
  Pallas kernels: 26.4 us -> 16.2 us
  waiting for transfers between devices: 52.4 us -> 56.5 us
  other arithmetic: 21.7 us -> 19 us
    pallas_call x1, Pallas kernels: 26.4 us -> 16.2 us  [spectral_middle(): pl.pallas_call(middle_kernel, grid=(count,), in_specs=[block, block_im, b...]
    all_to_all x1, starting transfers between devices: 10.1 us -> 4.47 us  [on_device(): got = lax.all_to_all(pair, ('seq', 'dp'), 0, 0, tiled=True)]
    all_to_all x1, starting transfers between devices: 4.47 us -> 9.98 us  [on_device(): taps_got = lax.all_to_all(taps_mine, ('seq', 'dp'), 0, 0, tiled=True)]
    all_to_all x1, waiting for transfers between devices: 4.46 us -> 7.38 us  [on_device(): taps_got = lax.all_to_all(taps_mine, ('seq', 'dp'), 0, 0, tiled=True)]
    unnamed x41 -> x43, local copies, waits for them, and re-layouts: 12.5 us -> 10.4 us
  transfers between devices with their start and end apart: 8 -> 8, of which waited for: 4 -> 4; matrix products, arithmetic and copies ran while one was open for 23% -> 23% of each run, Pallas kernels for 14% -> 9%
where the time goes in v1:
time: 178 us; the launch traced here: 177 us
  waiting for transfers between devices  56.5 us (32%)
  local copies, waits for them, and re-layouts  39.6 us (22%)
  starting transfers between devices  29.7 us (17%)
  other arithmetic  19 us (11%)
  Pallas kernels  16.2 us (9%)
  matrix products  14.7 us (8%)
    all_to_all x1, waiting for transfers between devices, on_device(): pair_home = lax.all_to_all(pair_back, ('seq', 'dp'), 0, 0, tiled=True)  22.2 us
    all_to_all x1, waiting for transfers between devices, on_device(): got = lax.all_to_all(pair, ('seq', 'dp'), 0, 0, tiled=True)  21.7 us
    pallas_call x1, Pallas kernels, spectral_middle(): pl.pallas_call(middle_kernel, grid=(count,), in_specs=[block, block_im, b...  16.2 us
    unnamed x43, local copies, waits for them, and re-layouts  10.4 us
    all_to_all x1, starting transfers between devices, on_device(): taps_got = lax.all_to_all(taps_mine, ('seq', 'dp'), 0, 0, tiled=True)  9.98 us
    dot_general x2, matrix products, spectral_inverse(): return jnp.einsum('nk,kml->nml', inv_a, both, precision=full_precision)  9.24 us
    all_to_all x1, waiting for transfers between devices, on_device(): taps_got = lax.all_to_all(taps_mine, ('seq', 'dp'), 0, 0, tiled=True)  7.38 us
    concatenate x2, other arithmetic, spectral_inverse(): both = jnp.concatenate([back_re, back_im], axis=0)  6.87 us
  transfers between devices with their start and end apart: 8, of which 4 were waited for; matrix products, arithmetic and copies ran while one was open for 23% of the time, Pallas kernels for 9%

profile of v1, /device:TPU:1, one launch (start us, length us, event | category | flops | bytes accessed | tf_op | source)
XLA Modules:
  0.0 176.7 jit_solution(1341246916762763152)
XLA Ops:
  2.3 1.5 convert_reduce_fusion
  4.6 10.0 %all-to-all-start = ((bf16[16,16,512]{2,1,0:T(8,128)(2,1)}), bf16[16,16,512]{2,1,0:T(8,128)(2,1)S(1)}, u32[]{:S(2)}, u32[]{:S(2)}) async-start(bf16[16,16,512]{2,1,0:T(8,128)(2,1)} %convert_element_type.155), calls=%async_computation | async-start | bytes 524288 | tf_op jit(solution)/shard_map/all_to_all | solution.py:188
  17.4 7.4 %all-to-all-done = bf16[16,16,512]{2,1,0:T(8,128)(2,1)S(1)} async-done(((bf16[16,16,512]{2,1,0:T(8,128)(2,1)}), bf16[16,16,512]{2,1,0:T(8,128)(2,1)S(1)}, u32[]{:S(2)}, u32[]{:S(2)}) %all-to-all-start) | async-done | bytes 262176 | tf_op jit(solution)/shard_map/all_to_all | solution.py:188
  24.7 4.5 %all-to-all-start.1 = ((bf16[16,64,512]{2,1,0:T(8,128)(2,1)}), bf16[16,64,512]{2,1,0:T(8,128)(2,1)S(1)}, u32[]{:S(2)}, u32[]{:S(2)}) async-start(bf16[16,64,512]{2,1,0:T(8,128)(2,1)} %bitcast.122), calls=%async_computation.1 | async-start | bytes 2097152 | tf_op jit(solution)/shard_map/all_to_all | solution.py:190
  29.9 1.9 %subtract_convert_fusion = (bf16[33,128,128]{2,1,0:T(8,128)(2,1)S(1)}, bf16[33,128,128]{2,1,0:T(8,128)(2,1)S(1)}, bf16[33,128,128]{2,1,0:T(8,128)(2,1)S(1)}, bf16[33,128,128]{2,1,0:T(8,128)(2,1)S(1)}) fusion(f32[33,128]{1,0:T(8,128)S(1)} %fusion.44, f32[33,128]{1,0:T(8,128)S(1)} %fusion.45, f32[128,128]{1,0:T(8,128)S(1)} %fusion.24, f32[128,128]{1,0:T(8,128)S(1)} %fusion.25), kind=kLoop, calls=%fused_computation.7 | loop fusion | flops 9191424 | bytes 4490240 | tf_op jit(solution)/shard_map/convert.8
  31.9 2.5 %pad_maximum_fusion.2 = (bf16[33,256,128]{2,1,0:T(8,128)(2,1)}, bf16[33,256,128]{2,1,0:T(8,128)(2,1)}) fusion(bf16[33,128,128]{2,1,0:T(8,128)(2,1)S(1)} %get-tuple-element.48, bf16[33,128,128]{2,1,0:T(8,128)(2,1)S(1)} %get-tuple-element.50, bf16[33,128,128]{2,1,0:T(8,128)(2,1)S(1)} %get-tuple-element.49, bf16[33,128,128]{2,1,0:T(8,128)(2,1)S(1)} %get-tuple-element.47), kind=kLoop, calls=%fused_computation.4 | loop fusion | flops 8650752 | bytes 8650752 | tf_op jit(solution)/shard_map/concatenate | solution.py:43
  34.5 21.7 %all-to-all-done.1 = bf16[16,64,512]{2,1,0:T(8,128)(2,1)S(1)} async-done(((bf16[16,64,512]{2,1,0:T(8,128)(2,1)}), bf16[16,64,512]{2,1,0:T(8,128)(2,1)S(1)}, u32[]{:S(2)}, u32[]{:S(2)}) %all-to-all-start.1) | async-done | bytes 1048608 | tf_op jit(solution)/shard_map/all_to_all | solution.py:190
  57.4 2.3 %copy.27 = bf16[32,128,128]{2,0,1:T(8,128)(2,1)} copy(bf16[32,128,128]{1,0,2:T(8,128)(2,1)S(1)} %bitcast.123) | data formatting | bytes 2097152 | tf_op jit(solution)/shard_map/reshape | solution.py:142
  59.7 3.3 %fusion.47 = f32[66,128,128]{2,0,1:T(8,128)S(1)} fusion(bf16[32,128,128]{2,0,1:T(8,128)(2,1)} %copy.27, f32[33,32]{0,1:T(8,128)S(1)} %get-tuple-element.55, f32[33,32]{0,1:T(8,128)S(1)} %get-tuple-element.56), kind=kOutput, calls=%fused_computation.87 | convolution fusion | flops 415238208 | bytes 5382400 | tf_op jit(solution)/shard_map/kn,nml->kml/dot_general | solution.py:141
  63.0 2.7 %copy.30.taps_re_ref.taps_im_ref = f32[66,128,128]{2,1,0:T(8,128)} copy(f32[66,128,128]{2,0,1:T(8,128)S(1)} %fusion.47) | data formatting | bytes 8650752 | tf_op jit(solution)/shard_map/kn,nml->kml/dot_general | solution.py:141
  67.0 1.5 copy.25
  68.6 2.4 %collective-permute-start.2 = (f32[512]{0:T(512)S(1)}, f32[512]{0:T(512)S(1)}, u32[]{:S(2)}, u32[]{:S(2)}) collective-permute-start(f32[512]{0:T(512)S(1)} %add.85), channel_id=1, source_target_pairs={{0,64},{1,65},{32,96},{33,97},{64,0},{65,1},{96,32},{97,33},{128,1... | collective-permute-start | bytes 6152 | tf_op jit(solution)/shard_map/ppermute | solution.py:196
  71.0 2.1 %fusion.48 = f32[66,128,128]{2,0,1:T(8,128)S(1)} fusion(bf16[32,128,128]{2,0,1:T(8,128)(2,1)S(1)} %copy.25, f32[33,32]{0,1:T(8,128)S(1)} %get-tuple-element.55, f32[33,32]{0,1:T(8,128)S(1)} %get-tuple-element.56), kind=kOutput, calls=%fused_computation.88 | convolution fusion | flops 415238208 | bytes 5382400 | tf_op jit(solution)/shard_map/kn,nml->kml/dot_general | solution.py:144
  73.1 2.9 %copy.28.sig_re_ref.sig_im_ref = f32[66,128,128]{2,1,0:T(8,128)} copy(f32[66,128,128]{2,0,1:T(8,128)S(1)} %fusion.48) | data formatting | bytes 8650752 | tf_op jit(solution)/shard_map/kn,nml->kml/dot_general | solution.py:144
  76.0 2.6 %collective-permute-start.3 = (f32[512]{0:T(512)S(1)}, f32[512]{0:T(512)S(1)}, u32[]{:S(2)}, u32[]{:S(2)}) collective-permute-start(f32[512]{0:T(512)S(1)} %add.86), channel_id=1, source_target_pairs={{0,128},{1,129},{32,160},{33,161},{64,192},{65,193},{96,224},{97,2... | collective-permute-start | bytes 6152 | tf_op jit(solution)/shard_map/ppermute | solution.py:196
  78.5 16.2 %shard_map.109 = (f32[33,128,128]{2,1,0:T(8,128)}, f32[33,128,128]{2,1,0:T(8,128)}, f32[33,128,128]{2,1,0:T(8,128)}, f32[33,128,128]{2,1,0:T(8,128)}) custom-call(f32[66,128,128]{2,1,0:T(8,128)} %copy.28.sig_re_ref.sig_im_ref, f32[66,128,128]{2,1,0:T(8,128)} %copy.28.sig_re_ref.sig_im_ref, f32[66,128,128]{2,1,0:T(8,128)} %copy.30.taps_re_ref.taps_im_ref, ...), custom_call_target="tpu_custom_call" | custom-call | flops 2214592512 | bytes 21626880 | tf_op jit(solution)/shard_map/pallas_call | solution.py:123
  95.4 4.9 %pad_maximum_fusion.1 = f32[66,128,128]{2,1,0:T(8,128)} fusion(f32[33,128,128]{2,1,0:T(8,128)} %get-tuple-element.30, f32[33,128,128]{2,1,0:T(8,128)} %get-tuple-element.29), kind=kLoop, calls=%fused_computation.3 | loop fusion | flops 1081344 | bytes 8650752 | tf_op jit(solution)/shard_map/concatenate | solution.py:158
  100.2 5.7 %copy.43 = f32[66,128,128]{1,0,2:T(8,128)} copy(f32[66,128,128]{2,1,0:T(8,128)} %pad_maximum_fusion.1) | data formatting | bytes 8650752 | tf_op jit(solution)/shard_map/concatenate | solution.py:158
  105.9 4.3 %fusion.49 = f32[32,128,128]{1,0,2:T(8,128)S(1)} fusion(f32[66,128,128]{1,0,2:T(8,128)} %copy.43, f32[32,33]{1,0:T(8,128)S(1)} %get-tuple-element.54, f32[32,33]{1,0:T(8,128)S(1)} %get-tuple-element.53), kind=kOutput, calls=%fused_computation.89 | convolution fusion | flops 415238208 | bytes 6430976 | tf_op jit(solution)/shard_map/nk,kml->nml/dot_general | solution.py:159
  110.2 1.6 reshape.173
  114.3 5.5 %all-to-all-start.3 = ((bf16[16,32,512]{2,1,0:T(8,128)(2,1)}), bf16[16,32,512]{2,1,0:T(8,128)(2,1)}, u32[]{:S(2)}, u32[]{:S(2)}) async-start(bf16[16,32,512]{2,1,0:T(8,128)(2,1)} %bitcast.127), calls=%async_computation.3 | async-start | bytes 1048576 | tf_op jit(solution)/shard_map/all_to_all | solution.py:229
  119.7 2.0 %pad_maximum_fusion = f32[66,128,128]{2,1,0:T(8,128)S(1)} fusion(f32[33,128,128]{2,1,0:T(8,128)} %get-tuple-element.28, f32[33,128,128]{2,1,0:T(8,128)S(1)} %copy-done.8), kind=kLoop, calls=%fused_computation.2 | loop fusion | flops 1081344 | bytes 8650752 | tf_op jit(solution)/shard_map/concatenate | solution.py:158
  121.7 5.0 %fusion.2 = bf16[32,128,128]{2,0,1:T(8,128)(2,1)S(1)} fusion(f32[66,128,128]{2,1,0:T(8,128)S(1)} %pad_maximum_fusion, f32[32,33]{1,0:T(8,128)S(1)} %get-tuple-element.54, f32[32,33]{1,0:T(8,128)S(1)} %get-tuple-element.53), kind=kOutput, calls=%fused_computation.10 | convolution fusion | flops 415762496 | bytes 5382400 | tf_op jit(solution)/shard_map/nk,kml->nml/dot_general | solution.py:159
  126.7 1.5 copy.33
  130.2 5.2 %all-to-all-done.3 = bf16[16,32,512]{2,1,0:T(8,128)(2,1)} async-done(((bf16[16,32,512]{2,1,0:T(8,128)(2,1)}), bf16[16,32,512]{2,1,0:T(8,128)(2,1)}, u32[]{:S(2)}, u32[]{:S(2)}) %all-to-all-start.3) | async-done | bytes 524320 | tf_op jit(solution)/shard_map/all_to_all | solution.py:229
  135.4 4.6 %all-to-all-start.2 = ((bf16[16,64,512]{2,1,0:T(8,128)(2,1)}), bf16[16,64,512]{2,1,0:T(8,128)(2,1)}, u32[]{:S(2)}, u32[]{:S(2)}) async-start(bf16[16,64,512]{2,1,0:T(8,128)(2,1)} %bitcast.18), calls=%async_computation.2 | async-start | bytes 2097152 | tf_op jit(solution)/shard_map/all_to_all | solution.py:220
  140.1 2.2 %convert_multiply_fusion.9 = f32[16,32,512]{2,1,0:T(8,128)} fusion(bf16[16,32,512]{2,1,0:T(8,128)(2,1)} %all-to-all-done.3), kind=kLoop, calls=%fused_computation.34 | loop fusion | flops 524288 | bytes 1572864 | tf_op jit(solution)/shard_map/mul | solution.py:235
  142.3 2.7 %copy.42 = f32[512,512]{1,0:T(8,128)} copy(f32[512,512]{0,1:T(8,128)} %bitcast.126) | data formatting | bytes 2097152
  144.9 22.2 %all-to-all-done.2 = bf16[16,64,512]{2,1,0:T(8,128)(2,1)} async-done(((bf16[16,64,512]{2,1,0:T(8,128)(2,1)}), bf16[16,64,512]{2,1,0:T(8,128)(2,1)}, u32[]{:S(2)}, u32[]{:S(2)}) %all-to-all-start.2) | async-done | bytes 1048608 | tf_op jit(solution)/shard_map/all_to_all | solution.py:220
  168.5 2.0 %fusion.14 = (bf16[1,512,512]{1,2,0:T(8,128)(2,1)}, bf16[1,512,512]{1,2,0:T(8,128)(2,1)}, bf16[1,512,512]{1,2,0:T(8,128)(2,1)}, bf16[1,512,512]{1,2,0:T(8,128)(2,1)}) fusion(bf16[512,512]{0,1:T(8,128)(2,1)S(1)} %copy-done.5, bf16[1,16,32,512]{3,2,0,1:T(8,128)(2,1)S(1)} %get-tuple-element.45, bf16[1,512,512]{1,2,0:T(8,128)(2,1)S(1)} %copy-done.1, ...), kind=kLoop, calls=%fused_computation.35 | loop fusion | flops 5242880 | bytes 6293504 | tf_op jit(solution)/shard_map/broadcast_in_dim | solution.py:247
  170.5 2.1 %copy.38 = bf16[1,512,512]{2,1,0:T(8,128)(2,1)} copy(bf16[1,512,512]{1,2,0:T(8,128)(2,1)} %get-tuple-element.51) | data formatting | bytes 1048576
  172.6 2.0 %copy.39 = bf16[1,512,512]{2,1,0:T(8,128)(2,1)} copy(bf16[1,512,512]{1,2,0:T(8,128)(2,1)} %get-tuple-element.52) | data formatting | bytes 1048576
  (75 shorter events, 16.6 us)
Async XLA Ops:
  0.6 14.0 %copy-start.11 = (bf16[1,512,512]{2,1,0:T(8,128)(2,1)S(1)}, bf16[1,512,512]{2,1,0:T(8,128)(2,1)}, u32[]{:S(2)}) copy-start(bf16[1,512,512]{2,1,0:T(8,128)(2,1)} %param.6) | copy-start | bytes 1572868
  2.1 12.7 %copy-start.12 = (bf16[1,512,512]{2,1,0:T(8,128)(2,1)S(1)}, bf16[1,512,512]{2,1,0:T(8,128)(2,1)}, u32[]{:S(2)}) copy-start(bf16[1,512,512]{2,1,0:T(8,128)(2,1)} %param.9) | copy-start | bytes 1572868
  2.3 12.8 %copy-start.13 = (bf16[1,512,512]{2,1,0:T(8,128)(2,1)S(1)}, bf16[1,512,512]{2,1,0:T(8,128)(2,1)}, u32[]{:S(2)}) copy-start(bf16[1,512,512]{2,1,0:T(8,128)(2,1)} %param.7) | copy-start | bytes 1572868
  3.8 11.5 %copy-start.14 = (bf16[1,512,512]{2,1,0:T(8,128)(2,1)S(1)}, bf16[1,512,512]{2,1,0:T(8,128)(2,1)}, u32[]{:S(2)}) copy-start(bf16[1,512,512]{2,1,0:T(8,128)(2,1)} %param.8) | copy-start | bytes 1572868
  4.6 20.1 %all-to-all-start = ((bf16[16,16,512]{2,1,0:T(8,128)(2,1)}), bf16[16,16,512]{2,1,0:T(8,128)(2,1)S(1)}, u32[]{:S(2)}, u32[]{:S(2)}) async-start(bf16[16,16,512]{2,1,0:T(8,128)(2,1)} %convert_element_type.155), calls=%async_computation | async-start | bytes 524288 | tf_op jit(solution)/shard_map/all_to_all | solution.py:188
  15.3 0.8 copy-start
  15.5 0.8 copy-start.2
  15.9 8.8 %copy-start.4 = (bf16[512,512]{0,1:T(8,128)(2,1)}, bf16[512,512]{0,1:T(8,128)(2,1)S(1)}, u32[]{:S(2)}) copy-start(bf16[512,512]{0,1:T(8,128)(2,1)S(1)} %get-tuple-element.39) | copy-start | bytes 1572868
  15.9 8.8 %copy-start.6 = (bf16[512,512]{0,1:T(8,128)(2,1)}, bf16[512,512]{0,1:T(8,128)(2,1)S(1)}, u32[]{:S(2)}) copy-start(bf16[512,512]{0,1:T(8,128)(2,1)S(1)} %get-tuple-element.40) | copy-start | bytes 1572868
  24.7 31.5 %all-to-all-start.1 = ((bf16[16,64,512]{2,1,0:T(8,128)(2,1)}), bf16[16,64,512]{2,1,0:T(8,128)(2,1)S(1)}, u32[]{:S(2)}, u32[]{:S(2)}) async-start(bf16[16,64,512]{2,1,0:T(8,128)(2,1)} %bitcast.122), calls=%async_computation.1 | async-start | bytes 2097152 | tf_op jit(solution)/shard_map/all_to_all | solution.py:190
  56.2 3.5 %collective-permute-start = (f32[512]{0:T(512)S(1)}, f32[512]{0:T(512)S(1)}, u32[]{:S(2)}, u32[]{:S(2)}) collective-permute-start(f32[512]{0:T(512)S(1)} %get-tuple-element.20), channel_id=1, source_target_pairs={{0,1},{1,0},{32,33},{33,32},{64,65},{65,64},{96,97},{97,96},{128,1... | collective-permute-start | bytes 6152 | tf_op jit(solution)/shard_map/ppermute | solution.py:196
  59.7 8.9 %collective-permute-start.1 = (f32[512]{0:T(512)S(1)}, f32[512]{0:T(512)S(1)}, u32[]{:S(2)}, u32[]{:S(2)}) collective-permute-start(f32[512]{0:T(512)S(1)} %add.84), channel_id=1, source_target_pairs={{0,32},{1,33},{32,0},{33,1},{64,96},{65,97},{96,64},{97,65},{128,1... | collective-permute-start | bytes 6152 | tf_op jit(solution)/shard_map/ppermute | solution.py:196
  68.6 7.4 %collective-permute-start.2 = (f32[512]{0:T(512)S(1)}, f32[512]{0:T(512)S(1)}, u32[]{:S(2)}, u32[]{:S(2)}) collective-permute-start(f32[512]{0:T(512)S(1)} %add.85), channel_id=1, source_target_pairs={{0,64},{1,65},{32,96},{33,97},{64,0},{65,1},{96,32},{97,33},{128,1... | collective-permute-start | bytes 6152 | tf_op jit(solution)/shard_map/ppermute | solution.py:196
  76.0 18.8 %collective-permute-start.3 = (f32[512]{0:T(512)S(1)}, f32[512]{0:T(512)S(1)}, u32[]{:S(2)}, u32[]{:S(2)}) collective-permute-start(f32[512]{0:T(512)S(1)} %add.86), channel_id=1, source_target_pairs={{0,128},{1,129},{32,160},{33,161},{64,192},{65,193},{96,224},{97,2... | collective-permute-start | bytes 6152 | tf_op jit(solution)/shard_map/ppermute | solution.py:196
  111.8 8.0 %copy-start.8 = (f32[33,128,128]{2,1,0:T(8,128)S(1)}, f32[33,128,128]{2,1,0:T(8,128)}, u32[]{:S(2)}) copy-start(f32[33,128,128]{2,1,0:T(8,128)} %get-tuple-element.27) | copy-start | bytes 6488068
  114.3 21.2 %all-to-all-start.3 = ((bf16[16,32,512]{2,1,0:T(8,128)(2,1)}), bf16[16,32,512]{2,1,0:T(8,128)(2,1)}, u32[]{:S(2)}, u32[]{:S(2)}) async-start(bf16[16,32,512]{2,1,0:T(8,128)(2,1)} %bitcast.127), calls=%async_computation.3 | async-start | bytes 1048576 | tf_op jit(solution)/shard_map/all_to_all | solution.py:229
  135.4 31.7 %all-to-all-start.2 = ((bf16[16,64,512]{2,1,0:T(8,128)(2,1)}), bf16[16,64,512]{2,1,0:T(8,128)(2,1)}, u32[]{:S(2)}, u32[]{:S(2)}) async-start(bf16[16,64,512]{2,1,0:T(8,128)(2,1)} %bitcast.18), calls=%async_computation.2 | async-start | bytes 2097152 | tf_op jit(solution)/shard_map/all_to_all | solution.py:220
  142.2 26.2 %copy-start.1 = (bf16[1,512,512]{1,2,0:T(8,128)(2,1)S(1)}, bf16[1,512,512]{1,2,0:T(8,128)(2,1)}, u32[]{:S(2)}) copy-start(bf16[1,512,512]{1,2,0:T(8,128)(2,1)} %copy-done) | copy-start | bytes 1572868
  142.2 26.2 %copy-start.3 = (bf16[1,512,512]{1,2,0:T(8,128)(2,1)S(1)}, bf16[1,512,512]{1,2,0:T(8,128)(2,1)}, u32[]{:S(2)}) copy-start(bf16[1,512,512]{1,2,0:T(8,128)(2,1)} %copy-done.2) | copy-start | bytes 1572868
  142.2 26.2 %copy-start.5 = (bf16[512,512]{0,1:T(8,128)(2,1)S(1)}, bf16[512,512]{0,1:T(8,128)(2,1)}, u32[]{:S(2)}) copy-start(bf16[512,512]{0,1:T(8,128)(2,1)} %copy-done.4) | copy-start | bytes 1572868
  142.2 26.2 %copy-start.7 = (bf16[512,512]{0,1:T(8,128)(2,1)S(1)}, bf16[512,512]{0,1:T(8,128)(2,1)}, u32[]{:S(2)}) copy-start(bf16[512,512]{0,1:T(8,128)(2,1)} %copy-done.6) | copy-start | bytes 1572868
  142.2 26.2 %copy-start.15 = (f32[512]{0:T(512)S(1)}, f32[512]{0:T(512)}, u32[]{:S(2)}) copy-start(f32[512]{0:T(512)} %param.11) | copy-start | bytes 6148
  170.5 4.2 %copy-start.10 = (bf16[1,512,512]{1,2,0:T(8,128)(2,1)S(1)}, bf16[1,512,512]{1,2,0:T(8,128)(2,1)}, u32[]{:S(2)}) copy-start(bf16[1,512,512]{1,2,0:T(8,128)(2,1)} %get-tuple-element.42) | copy-start | bytes 1572868
  170.5 5.2 %copy-start.9 = (bf16[1,512,512]{1,2,0:T(8,128)(2,1)S(1)}, bf16[1,512,512]{1,2,0:T(8,128)(2,1)}, u32[]{:S(2)}) copy-start(bf16[1,512,512]{1,2,0:T(8,128)(2,1)} %get-tuple-element.41) | copy-start | bytes 1572868

commit v2 on v1

--- a/solution.py
+++ b/solution.py
@@ -226,6 +226,7 @@
     slope_send = jnp.broadcast_to(
         slope_blocks[:, None], (seq_count, batch_count, share, local_length)
     ).reshape(groups, share, local_length)
+    pair_home, slope_send = lax.optimization_barrier((pair_home, slope_send))
     slope_home = lax.all_to_all(slope_send, ("seq", "dp"), 0, 0, tiled=True)
 
     pair_home = pair_home.reshape(groups, 2, share, local_length)

time: 178 us -> 164 us (0.921)
  waiting for transfers between devices: 56.5 us -> 44.5 us
    all_to_all x1, waiting for transfers between devices: 22.2 us -> 9.19 us  [on_device(): pair_home = lax.all_to_all(pair_back, ('seq', 'dp'), 0, 0, tiled=True)]
    unnamed x43 -> x41, local copies, waits for them, and re-layouts: 10.4 us -> 9.03 us
  transfers between devices with their start and end apart: 8 -> 8, of which waited for: 4 -> 4; matrix products, arithmetic and copies ran while one was open for 23% -> 32% of each run, Pallas kernels for 9% -> 10%
where the time goes in v2:
time: 164 us; the launch traced here: 163 us
  waiting for transfers between devices  44.5 us (27%)
  local copies, waits for them, and re-layouts  38.3 us (23%)
  starting transfers between devices  29.5 us (18%)
  other arithmetic  18.5 us (11%)
  Pallas kernels  16.2 us (10%)
  matrix products  14.7 us (9%)
    all_to_all x1, waiting for transfers between devices, on_device(): got = lax.all_to_all(pair, ('seq', 'dp'), 0, 0, tiled=True)  21.7 us
    pallas_call x1, Pallas kernels, spectral_middle(): pl.pallas_call(middle_kernel, grid=(count,), in_specs=[block, block_im, b...  16.2 us
    all_to_all x1, starting transfers between devices, on_device(): taps_got = lax.all_to_all(taps_mine, ('seq', 'dp'), 0, 0, tiled=True)  9.98 us
    dot_general x2, matrix products, spectral_inverse(): return jnp.einsum('nk,kml->nml', inv_a, both, precision=full_precision)  9.23 us
    all_to_all x1, waiting for transfers between devices, on_device(): pair_home = lax.all_to_all(pair_back, ('seq', 'dp'), 0, 0, tiled=True)  9.19 us
    unnamed x41, local copies, waits for them, and re-layouts  9.03 us
    concatenate x2, other arithmetic, spectral_inverse(): both = jnp.concatenate([back_re, back_im], axis=0)  7.58 us
    all_to_all x1, waiting for transfers between devices, on_device(): taps_got = lax.all_to_all(taps_mine, ('seq', 'dp'), 0, 0, tiled=True)  7.38 us
  transfers between devices with their start and end apart: 8, of which 4 were waited for; matrix products, arithmetic and copies ran while one was open for 32% of the time, Pallas kernels for 10%

profile of v2, /device:TPU:1, one launch (start us, length us, event | category | flops | bytes accessed | tf_op | source)
XLA Modules:
  0.0 162.7 jit_solution(3329071480615776301)
XLA Ops:
  0.6 1.5 copy.22
  2.3 1.5 convert_reduce_fusion
  4.6 10.0 %all-to-all-start = ((bf16[16,16,512]{2,1,0:T(8,128)(2,1)}), bf16[16,16,512]{2,1,0:T(8,128)(2,1)S(1)}, u32[]{:S(2)}, u32[]{:S(2)}) async-start(bf16[16,16,512]{2,1,0:T(8,128)(2,1)} %convert_element_type.155), calls=%async_computation | async-start | bytes 524288 | tf_op jit(solution)/shard_map/all_to_all | solution.py:188
  17.4 7.4 %all-to-all-done = bf16[16,16,512]{2,1,0:T(8,128)(2,1)S(1)} async-done(((bf16[16,16,512]{2,1,0:T(8,128)(2,1)}), bf16[16,16,512]{2,1,0:T(8,128)(2,1)S(1)}, u32[]{:S(2)}, u32[]{:S(2)}) %all-to-all-start) | async-done | bytes 262176 | tf_op jit(solution)/shard_map/all_to_all | solution.py:188
  24.8 4.5 %all-to-all-start.1 = ((bf16[16,64,512]{2,1,0:T(8,128)(2,1)}), bf16[16,64,512]{2,1,0:T(8,128)(2,1)S(1)}, u32[]{:S(2)}, u32[]{:S(2)}) async-start(bf16[16,64,512]{2,1,0:T(8,128)(2,1)} %bitcast.122), calls=%async_computation.1 | async-start | bytes 2097152 | tf_op jit(solution)/shard_map/all_to_all | solution.py:190
  30.0 1.9 %subtract_convert_fusion = (bf16[33,128,128]{2,1,0:T(8,128)(2,1)S(1)}, bf16[33,128,128]{2,1,0:T(8,128)(2,1)S(1)}, bf16[33,128,128]{2,1,0:T(8,128)(2,1)S(1)}, bf16[33,128,128]{2,1,0:T(8,128)(2,1)S(1)}) fusion(f32[33,128]{1,0:T(8,128)S(1)} %fusion.44, f32[33,128]{1,0:T(8,128)S(1)} %fusion.45, f32[128,128]{1,0:T(8,128)S(1)} %fusion.24, f32[128,128]{1,0:T(8,128)S(1)} %fusion.25), kind=kLoop, calls=%fused_computation.7 | loop fusion | flops 9191424 | bytes 4490240 | tf_op jit(solution)/shard_map/convert.8
  31.9 2.5 %pad_maximum_fusion.2 = (bf16[33,256,128]{2,1,0:T(8,128)(2,1)}, bf16[33,256,128]{2,1,0:T(8,128)(2,1)}) fusion(bf16[33,128,128]{2,1,0:T(8,128)(2,1)S(1)} %get-tuple-element.52, bf16[33,128,128]{2,1,0:T(8,128)(2,1)S(1)} %get-tuple-element.54, bf16[33,128,128]{2,1,0:T(8,128)(2,1)S(1)} %get-tuple-element.53, bf16[33,128,128]{2,1,0:T(8,128)(2,1)S(1)} %get-tuple-element.51), kind=kLoop, calls=%fused_computation.4 | loop fusion | flops 8650752 | bytes 8650752 | tf_op jit(solution)/shard_map/concatenate | solution.py:43
  34.5 21.7 %all-to-all-done.1 = bf16[16,64,512]{2,1,0:T(8,128)(2,1)S(1)} async-done(((bf16[16,64,512]{2,1,0:T(8,128)(2,1)}), bf16[16,64,512]{2,1,0:T(8,128)(2,1)S(1)}, u32[]{:S(2)}, u32[]{:S(2)}) %all-to-all-start.1) | async-done | bytes 1048608 | tf_op jit(solution)/shard_map/all_to_all | solution.py:190
  57.4 2.3 %copy.27 = bf16[32,128,128]{2,0,1:T(8,128)(2,1)} copy(bf16[32,128,128]{1,0,2:T(8,128)(2,1)S(1)} %bitcast.123) | data formatting | bytes 2097152 | tf_op jit(solution)/shard_map/reshape | solution.py:142
  59.7 3.3 %fusion.47 = f32[66,128,128]{2,0,1:T(8,128)S(1)} fusion(bf16[32,128,128]{2,0,1:T(8,128)(2,1)} %copy.27, f32[33,32]{0,1:T(8,128)S(1)} %get-tuple-element.59, f32[33,32]{0,1:T(8,128)S(1)} %get-tuple-element.60), kind=kOutput, calls=%fused_computation.87 | convolution fusion | flops 415238208 | bytes 5382400 | tf_op jit(solution)/shard_map/kn,nml->kml/dot_general | solution.py:141
  63.0 2.9 %copy.30.taps_re_ref.taps_im_ref = f32[66,128,128]{2,1,0:T(8,128)} copy(f32[66,128,128]{2,0,1:T(8,128)S(1)} %fusion.47) | data formatting | bytes 8650752 | tf_op jit(solution)/shard_map/kn,nml->kml/dot_general | solution.py:141
  67.1 1.5 copy.25
  68.7 2.4 %collective-permute-start.2 = (f32[512]{0:T(512)S(1)}, f32[512]{0:T(512)S(1)}, u32[]{:S(2)}, u32[]{:S(2)}) collective-permute-start(f32[512]{0:T(512)S(1)} %add.85), channel_id=1, source_target_pairs={{0,64},{1,65},{32,96},{33,97},{64,0},{65,1},{96,32},{97,33},{128,1... | collective-permute-start | bytes 6152 | tf_op jit(solution)/shard_map/ppermute | solution.py:196
  71.1 2.1 %fusion.48 = f32[66,128,128]{2,0,1:T(8,128)S(1)} fusion(bf16[32,128,128]{2,0,1:T(8,128)(2,1)S(1)} %copy.25, f32[33,32]{0,1:T(8,128)S(1)} %get-tuple-element.59, f32[33,32]{0,1:T(8,128)S(1)} %get-tuple-element.60), kind=kOutput, calls=%fused_computation.88 | convolution fusion | flops 415238208 | bytes 5382400 | tf_op jit(solution)/shard_map/kn,nml->kml/dot_general | solution.py:144
  73.2 2.8 %copy.28.sig_re_ref.sig_im_ref = f32[66,128,128]{2,1,0:T(8,128)} copy(f32[66,128,128]{2,0,1:T(8,128)S(1)} %fusion.48) | data formatting | bytes 8650752 | tf_op jit(solution)/shard_map/kn,nml->kml/dot_general | solution.py:144
  76.0 2.6 %collective-permute-start.3 = (f32[512]{0:T(512)S(1)}, f32[512]{0:T(512)S(1)}, u32[]{:S(2)}, u32[]{:S(2)}) collective-permute-start(f32[512]{0:T(512)S(1)} %add.86), channel_id=1, source_target_pairs={{0,128},{1,129},{32,160},{33,161},{64,192},{65,193},{96,224},{97,2... | collective-permute-start | bytes 6152 | tf_op jit(solution)/shard_map/ppermute | solution.py:196
  78.5 16.2 %shard_map.109 = (f32[33,128,128]{2,1,0:T(8,128)}, f32[33,128,128]{2,1,0:T(8,128)}, f32[33,128,128]{2,1,0:T(8,128)}, f32[33,128,128]{2,1,0:T(8,128)}) custom-call(f32[66,128,128]{2,1,0:T(8,128)} %copy.28.sig_re_ref.sig_im_ref, f32[66,128,128]{2,1,0:T(8,128)} %copy.28.sig_re_ref.sig_im_ref, f32[66,128,128]{2,1,0:T(8,128)} %copy.30.taps_re_ref.taps_im_ref, ...), custom_call_target="tpu_custom_call" | custom-call | flops 2214592512 | bytes 21626880 | tf_op jit(solution)/shard_map/pallas_call | solution.py:123
  95.4 2.8 %pad_maximum_fusion = f32[66,128,128]{2,1,0:T(8,128)S(1)} fusion(f32[33,128,128]{2,1,0:T(8,128)} %get-tuple-element.30, f32[33,128,128]{2,1,0:T(8,128)} %get-tuple-element.29), kind=kLoop, calls=%fused_computation.2 | loop fusion | flops 1081344 | bytes 8650752 | tf_op jit(solution)/shard_map/concatenate | solution.py:158
  98.1 5.0 %fusion.2 = bf16[32,128,128]{2,0,1:T(8,128)(2,1)S(1)} fusion(f32[66,128,128]{2,1,0:T(8,128)S(1)} %pad_maximum_fusion, f32[32,33]{1,0:T(8,128)S(1)} %get-tuple-element.58, f32[32,33]{1,0:T(8,128)S(1)} %get-tuple-element.57), kind=kOutput, calls=%fused_computation.10 | convolution fusion | flops 415762496 | bytes 5382400 | tf_op jit(solution)/shard_map/nk,kml->nml/dot_general | solution.py:159
  103.1 1.5 copy.33
  106.6 5.5 %all-to-all-start.2 = ((bf16[16,64,512]{2,1,0:T(8,128)(2,1)}), bf16[16,64,512]{2,1,0:T(8,128)(2,1)}, u32[]{:S(2)}, u32[]{:S(2)}) async-start(bf16[16,64,512]{2,1,0:T(8,128)(2,1)} %bitcast.18), calls=%async_computation.2 | async-start | bytes 2097152 | tf_op jit(solution)/shard_map/all_to_all | solution.py:220
  112.1 4.8 %pad_maximum_fusion.1 = f32[66,128,128]{2,1,0:T(8,128)} fusion(f32[33,128,128]{2,1,0:T(8,128)} %get-tuple-element.32, f32[33,128,128]{2,1,0:T(8,128)} %get-tuple-element.31), kind=kLoop, calls=%fused_computation.3 | loop fusion | flops 1081344 | bytes 8650752 | tf_op jit(solution)/shard_map/concatenate | solution.py:158
  116.9 5.7 %copy.43 = f32[66,128,128]{1,0,2:T(8,128)} copy(f32[66,128,128]{2,1,0:T(8,128)} %pad_maximum_fusion.1) | data formatting | bytes 8650752 | tf_op jit(solution)/shard_map/concatenate | solution.py:158
  122.6 4.3 %fusion.49 = f32[32,128,128]{1,0,2:T(8,128)S(1)} fusion(f32[66,128,128]{1,0,2:T(8,128)} %copy.43, f32[32,33]{1,0:T(8,128)S(1)} %get-tuple-element.58, f32[32,33]{1,0:T(8,128)S(1)} %get-tuple-element.57), kind=kOutput, calls=%fused_computation.89 | convolution fusion | flops 415238208 | bytes 6430976 | tf_op jit(solution)/shard_map/nk,kml->nml/dot_general | solution.py:159
  126.9 1.5 reshape.172
  128.4 1.3 slice_reduce_fusion
  130.0 9.2 %all-to-all-done.2 = bf16[16,64,512]{2,1,0:T(8,128)(2,1)} async-done(((bf16[16,64,512]{2,1,0:T(8,128)(2,1)}), bf16[16,64,512]{2,1,0:T(8,128)(2,1)}, u32[]{:S(2)}, u32[]{:S(2)}) %all-to-all-start.2) | async-done | bytes 1048608 | tf_op jit(solution)/shard_map/all_to_all | solution.py:220
  140.0 4.5 %all-to-all-start.3 = ((bf16[16,32,512]{2,1,0:T(8,128)(2,1)}), bf16[16,32,512]{2,1,0:T(8,128)(2,1)}, u32[]{:S(2)}, u32[]{:S(2)}) async-start(bf16[16,32,512]{2,1,0:T(8,128)(2,1)} %bitcast.127), calls=%async_computation.3 | async-start | bytes 1048576 | tf_op jit(solution)/shard_map/all_to_all | solution.py:230
  145.8 2.0 %fusion.14 = (bf16[1,512,512]{1,2,0:T(8,128)(2,1)}, bf16[1,512,512]{1,2,0:T(8,128)(2,1)}, bf16[1,512,512]{1,2,0:T(8,128)(2,1)}, bf16[1,512,512]{1,2,0:T(8,128)(2,1)}) fusion(bf16[512,512]{0,1:T(8,128)(2,1)S(1)} %copy-done.5, bf16[1,16,32,512]{3,2,0,1:T(8,128)(2,1)S(1)} %get-tuple-element.49, bf16[1,512,512]{1,2,0:T(8,128)(2,1)S(1)} %copy-done.1, ...), kind=kLoop, calls=%fused_computation.35 | loop fusion | flops 5242880 | bytes 6293504 | tf_op jit(solution)/shard_map/broadcast_in_dim | solution.py:248
  147.8 2.1 %copy.38 = bf16[1,512,512]{2,1,0:T(8,128)(2,1)} copy(bf16[1,512,512]{1,2,0:T(8,128)(2,1)} %get-tuple-element.55) | data formatting | bytes 1048576
  150.0 2.0 %copy.39 = bf16[1,512,512]{2,1,0:T(8,128)(2,1)} copy(bf16[1,512,512]{1,2,0:T(8,128)(2,1)} %get-tuple-element.56) | data formatting | bytes 1048576
  154.0 6.2 %all-to-all-done.3 = bf16[16,32,512]{2,1,0:T(8,128)(2,1)} async-done(((bf16[16,32,512]{2,1,0:T(8,128)(2,1)}), bf16[16,32,512]{2,1,0:T(8,128)(2,1)}, u32[]{:S(2)}, u32[]{:S(2)}) %all-to-all-start.3) | async-done | bytes 524320 | tf_op jit(solution)/shard_map/all_to_all | solution.py:230
  (73 shorter events, 16.2 us)
Async XLA Ops:
  0.6 14.0 %copy-start.10 = (bf16[1,512,512]{2,1,0:T(8,128)(2,1)S(1)}, bf16[1,512,512]{2,1,0:T(8,128)(2,1)}, u32[]{:S(2)}) copy-start(bf16[1,512,512]{2,1,0:T(8,128)(2,1)} %param.6) | copy-start | bytes 1572868
  2.1 12.7 %copy-start.11 = (bf16[1,512,512]{2,1,0:T(8,128)(2,1)S(1)}, bf16[1,512,512]{2,1,0:T(8,128)(2,1)}, u32[]{:S(2)}) copy-start(bf16[1,512,512]{2,1,0:T(8,128)(2,1)} %param.9) | copy-start | bytes 1572868
  2.3 12.8 %copy-start.12 = (bf16[1,512,512]{2,1,0:T(8,128)(2,1)S(1)}, bf16[1,512,512]{2,1,0:T(8,128)(2,1)}, u32[]{:S(2)}) copy-start(bf16[1,512,512]{2,1,0:T(8,128)(2,1)} %param.7) | copy-start | bytes 1572868
  3.8 11.5 %copy-start.13 = (bf16[1,512,512]{2,1,0:T(8,128)(2,1)S(1)}, bf16[1,512,512]{2,1,0:T(8,128)(2,1)}, u32[]{:S(2)}) copy-start(bf16[1,512,512]{2,1,0:T(8,128)(2,1)} %param.8) | copy-start | bytes 1572868
  4.6 20.1 %all-to-all-start = ((bf16[16,16,512]{2,1,0:T(8,128)(2,1)}), bf16[16,16,512]{2,1,0:T(8,128)(2,1)S(1)}, u32[]{:S(2)}, u32[]{:S(2)}) async-start(bf16[16,16,512]{2,1,0:T(8,128)(2,1)} %convert_element_type.155), calls=%async_computation | async-start | bytes 524288 | tf_op jit(solution)/shard_map/all_to_all | solution.py:188
  15.3 0.8 copy-start
  15.5 0.8 copy-start.2
  15.9 8.8 %copy-start.4 = (bf16[512,512]{0,1:T(8,128)(2,1)}, bf16[512,512]{0,1:T(8,128)(2,1)S(1)}, u32[]{:S(2)}) copy-start(bf16[512,512]{0,1:T(8,128)(2,1)S(1)} %get-tuple-element.43) | copy-start | bytes 1572868
  15.9 8.8 %copy-start.6 = (bf16[512,512]{0,1:T(8,128)(2,1)}, bf16[512,512]{0,1:T(8,128)(2,1)S(1)}, u32[]{:S(2)}) copy-start(bf16[512,512]{0,1:T(8,128)(2,1)S(1)} %get-tuple-element.44) | copy-start | bytes 1572868
  24.8 31.5 %all-to-all-start.1 = ((bf16[16,64,512]{2,1,0:T(8,128)(2,1)}), bf16[16,64,512]{2,1,0:T(8,128)(2,1)S(1)}, u32[]{:S(2)}, u32[]{:S(2)}) async-start(bf16[16,64,512]{2,1,0:T(8,128)(2,1)} %bitcast.122), calls=%async_computation.1 | async-start | bytes 2097152 | tf_op jit(solution)/shard_map/all_to_all | solution.py:190
  56.2 3.5 %collective-permute-start = (f32[512]{0:T(512)S(1)}, f32[512]{0:T(512)S(1)}, u32[]{:S(2)}, u32[]{:S(2)}) collective-permute-start(f32[512]{0:T(512)S(1)} %get-tuple-element.22), channel_id=1, source_target_pairs={{0,1},{1,0},{32,33},{33,32},{64,65},{65,64},{96,97},{97,96},{128,1... | collective-permute-start | bytes 6152 | tf_op jit(solution)/shard_map/ppermute | solution.py:196
  59.7 9.0 %collective-permute-start.1 = (f32[512]{0:T(512)S(1)}, f32[512]{0:T(512)S(1)}, u32[]{:S(2)}, u32[]{:S(2)}) collective-permute-start(f32[512]{0:T(512)S(1)} %add.84), channel_id=1, source_target_pairs={{0,32},{1,33},{32,0},{33,1},{64,96},{65,97},{96,64},{97,65},{128,1... | collective-permute-start | bytes 6152 | tf_op jit(solution)/shard_map/ppermute | solution.py:196
  68.7 7.3 %collective-permute-start.2 = (f32[512]{0:T(512)S(1)}, f32[512]{0:T(512)S(1)}, u32[]{:S(2)}, u32[]{:S(2)}) collective-permute-start(f32[512]{0:T(512)S(1)} %add.85), channel_id=1, source_target_pairs={{0,64},{1,65},{32,96},{33,97},{64,0},{65,1},{96,32},{97,33},{128,1... | collective-permute-start | bytes 6152 | tf_op jit(solution)/shard_map/ppermute | solution.py:196
  76.0 18.8 %collective-permute-start.3 = (f32[512]{0:T(512)S(1)}, f32[512]{0:T(512)S(1)}, u32[]{:S(2)}, u32[]{:S(2)}) collective-permute-start(f32[512]{0:T(512)S(1)} %add.86), channel_id=1, source_target_pairs={{0,128},{1,129},{32,160},{33,161},{64,192},{65,193},{96,224},{97,2... | collective-permute-start | bytes 6152 | tf_op jit(solution)/shard_map/ppermute | solution.py:196
  106.6 32.5 %all-to-all-start.2 = ((bf16[16,64,512]{2,1,0:T(8,128)(2,1)}), bf16[16,64,512]{2,1,0:T(8,128)(2,1)}, u32[]{:S(2)}, u32[]{:S(2)}) async-start(bf16[16,64,512]{2,1,0:T(8,128)(2,1)} %bitcast.18), calls=%async_computation.2 | async-start | bytes 2097152 | tf_op jit(solution)/shard_map/all_to_all | solution.py:220
  129.8 15.9 %copy-start.1 = (bf16[1,512,512]{1,2,0:T(8,128)(2,1)S(1)}, bf16[1,512,512]{1,2,0:T(8,128)(2,1)}, u32[]{:S(2)}) copy-start(bf16[1,512,512]{1,2,0:T(8,128)(2,1)} %copy-done) | copy-start | bytes 1572868
  129.8 15.9 %copy-start.3 = (bf16[1,512,512]{1,2,0:T(8,128)(2,1)S(1)}, bf16[1,512,512]{1,2,0:T(8,128)(2,1)}, u32[]{:S(2)}) copy-start(bf16[1,512,512]{1,2,0:T(8,128)(2,1)} %copy-done.2) | copy-start | bytes 1572868
  129.8 15.9 %copy-start.5 = (bf16[512,512]{0,1:T(8,128)(2,1)S(1)}, bf16[512,512]{0,1:T(8,128)(2,1)}, u32[]{:S(2)}) copy-start(bf16[512,512]{0,1:T(8,128)(2,1)} %copy-done.4) | copy-start | bytes 1572868
  129.9 15.9 %copy-start.7 = (bf16[512,512]{0,1:T(8,128)(2,1)S(1)}, bf16[512,512]{0,1:T(8,128)(2,1)}, u32[]{:S(2)}) copy-start(bf16[512,512]{0,1:T(8,128)(2,1)} %copy-done.6) | copy-start | bytes 1572868
  129.9 15.9 %copy-start.14 = (f32[512]{0:T(512)S(1)}, f32[512]{0:T(512)}, u32[]{:S(2)}) copy-start(f32[512]{0:T(512)} %param.11) | copy-start | bytes 6148
  140.0 20.2 %all-to-all-start.3 = ((bf16[16,32,512]{2,1,0:T(8,128)(2,1)}), bf16[16,32,512]{2,1,0:T(8,128)(2,1)}, u32[]{:S(2)}, u32[]{:S(2)}) async-start(bf16[16,32,512]{2,1,0:T(8,128)(2,1)} %bitcast.127), calls=%async_computation.3 | async-start | bytes 1048576 | tf_op jit(solution)/shard_map/all_to_all | solution.py:230
  147.8 4.2 %copy-start.9 = (bf16[1,512,512]{1,2,0:T(8,128)(2,1)S(1)}, bf16[1,512,512]{1,2,0:T(8,128)(2,1)}, u32[]{:S(2)}) copy-start(bf16[1,512,512]{1,2,0:T(8,128)(2,1)} %get-tuple-element.46) | copy-start | bytes 1572868
  147.8 5.2 %copy-start.8 = (bf16[1,512,512]{1,2,0:T(8,128)(2,1)S(1)}, bf16[1,512,512]{1,2,0:T(8,128)(2,1)}, u32[]{:S(2)}) copy-start(bf16[1,512,512]{1,2,0:T(8,128)(2,1)} %get-tuple-element.45) | copy-start | bytes 1572868

commit v3 on v2

--- a/solution.py
+++ b/solution.py
@@ -132,15 +132,23 @@
     )(sig_first, sig_first, taps_first, taps_first, fwd_table, inv_table)
 
 
-def spectral_products(signals, taps, carry):
-    seq_length, lanes = signals.shape
+def taps_spectrum_first(taps):
+    seq_length, lanes = taps.shape
     tables = spectral_tables(seq_length)
-    stage_a, _, fwd_table, inv_table = tables
+    stage_a, _, fwd_table, _ = tables
     inner = fwd_table.shape[2]
     rows = seq_length // inner
     taps_first = jnp.einsum(
         "kn,nml->kml", stage_a, taps.reshape(rows, inner, lanes), precision=full_precision
     )
+    return tables, taps_first
+
+
+def spectral_products(signals, taps_first, tables, carry):
+    seq_length, lanes = signals.shape
+    stage_a, _, fwd_table, inv_table = tables
+    inner = fwd_table.shape[2]
+    rows = seq_length // inner
     sig_first = jnp.einsum(
         "kn,nml->kml", stage_a, signals.reshape(rows, inner, lanes), precision=full_precision
     )
@@ -188,7 +196,15 @@
     taps_got = lax.all_to_all(taps_mine, ("seq", "dp"), 0, 0, tiled=True)
     taps_got, pair = lax.optimization_barrier((taps_got, pair))
     got = lax.all_to_all(pair, ("seq", "dp"), 0, 0, tiled=True)
-    gain_part, got = lax.optimization_barrier((gain_part, got))
+    taps_t = taps_got.reshape(seq_count, batch_count, share, half_length)
+    taps = jnp.transpose(taps_t, (0, 1, 3, 2)).reshape(seq_length, 1, share)
+    taps = jnp.broadcast_to(taps, (seq_length, 2 * batch_count, share)).reshape(
+        seq_length, 2 * batch_count * share
+    )
+    tables, taps_first = taps_spectrum_first(taps.astype(jnp.float32))
+    gain_part, got, tables, taps_first = lax.optimization_barrier(
+        (gain_part, got, tables, taps_first)
+    )
     total = gain_part
     distance = 1
     while distance < groups:
@@ -199,14 +215,9 @@
 
     pair_t = got.reshape(seq_count, batch_count, 2, share, local_length)
     signals = jnp.transpose(pair_t, (0, 4, 2, 1, 3)).reshape(seq_length, 2 * batch_count * share)
-    taps_t = taps_got.reshape(seq_count, batch_count, share, half_length)
-    taps = jnp.transpose(taps_t, (0, 1, 3, 2)).reshape(seq_length, 1, share)
-    taps = jnp.broadcast_to(taps, (seq_length, 2 * batch_count, share)).reshape(
-        seq_length, 2 * batch_count * share
-    )
 
     tables, pair_spec, cross_spec, grad_skip = spectral_products(
-        signals.astype(jnp.float32), taps.astype(jnp.float32), grad_skip
+        signals.astype(jnp.float32), taps_first, tables, grad_skip
     )
     pair_vals = spectral_inverse(pair_spec[0], pair_spec[1], tables)
     pair_vals = pair_vals.reshape(seq_length, 2, batch_count, share)

time: 164 us -> 159 us (0.970)
  waiting for transfers between devices: 44.5 us -> 36.6 us
  matrix products: 14.7 us -> 16.6 us
    all_to_all x1, waiting for transfers between devices: 21.7 us -> 12.9 us  [on_device(): got = lax.all_to_all(pair, ('seq', 'dp'), 0, 0, tiled=True)]
    dot_general x1 -> x0, local copies, waits for them, and re-layouts: 2.85 us -> none  [spectral_products(): jnp.einsum('kn,nml->kml', stage_a, taps.reshape(rows, inner, lanes), prec...]
    optimization_barrier x0 -> x1, local copies, waits for them, and re-layouts: none -> 2.75 us  [on_device(): lax.optimization_barrier((gain_part, got, tables, taps_first))]
    ppermute x4, waiting for transfers between devices: 0.01 us -> 2.26 us  [on_device(): total = total + lax.ppermute(total, ('seq', 'dp'), partners)]
    dot_general x1, matrix products: 3.33 us -> 5.36 us  [taps_spectrum_first(): jnp.einsum('kn,nml->kml', stage_a, taps.reshape(rows, inner, lanes), prec...]
    unnamed x41 -> x43, local copies, waits for them, and re-layouts: 9.03 us -> 10.3 us
  transfers between devices with their start and end apart: 8 -> 8, of which waited for: 4 -> 5; matrix products, arithmetic and copies ran while one was open for 32% -> 35% of each run, Pallas kernels for 10% -> 10%
where the time goes in v3:
time: 159 us; the launch traced here: 158 us
  local copies, waits for them, and re-layouts  39.5 us (25%)
  waiting for transfers between devices  36.6 us (23%)
  starting transfers between devices  28.8 us (18%)
  other arithmetic  18.7 us (12%)
  matrix products  16.6 us (10%)
  Pallas kernels  16.2 us (10%)
    pallas_call x1, Pallas kernels, spectral_middle(): pl.pallas_call(middle_kernel, grid=(count,), in_specs=[block, block_im, b...  16.2 us
    all_to_all x1, waiting for transfers between devices, on_device(): got = lax.all_to_all(pair, ('seq', 'dp'), 0, 0, tiled=True)  12.9 us
    unnamed x43, local copies, waits for them, and re-layouts  10.3 us
    all_to_all x1, starting transfers between devices, on_device(): taps_got = lax.all_to_all(taps_mine, ('seq', 'dp'), 0, 0, tiled=True)  9.98 us
    dot_general x2, matrix products, spectral_inverse(): return jnp.einsum('nk,kml->nml', inv_a, both, precision=full_precision)  9.21 us
    all_to_all x1, waiting for transfers between devices, on_device(): pair_home = lax.all_to_all(pair_back, ('seq', 'dp'), 0, 0, tiled=True)  9.12 us
    concatenate x2, other arithmetic, spectral_inverse(): both = jnp.concatenate([back_re, back_im], axis=0)  7.63 us
    all_to_all x1, waiting for transfers between devices, on_device(): slope_home = lax.all_to_all(slope_send, ('seq', 'dp'), 0, 0, tiled=True)  6.17 us
  transfers between devices with their start and end apart: 8, of which 5 were waited for; matrix products, arithmetic and copies ran while one was open for 35% of the time, Pallas kernels for 10%

profile of v3, /device:TPU:1, one launch (start us, length us, event | category | flops | bytes accessed | tf_op | source)
XLA Modules:
  0.0 157.5 jit_solution(16975515344510678523)
XLA Ops:
  0.6 1.5 copy.22
  2.3 1.5 convert_reduce_fusion
  4.6 10.0 %all-to-all-start = ((bf16[16,16,512]{2,1,0:T(8,128)(2,1)}), bf16[16,16,512]{2,1,0:T(8,128)(2,1)S(1)}, u32[]{:S(2)}, u32[]{:S(2)}) async-start(bf16[16,16,512]{2,1,0:T(8,128)(2,1)} %convert_element_type.154), calls=%async_computation | async-start | bytes 524288 | tf_op jit(solution)/shard_map/all_to_all | solution.py:196
  18.6 6.2 %all-to-all-done = bf16[16,16,512]{2,1,0:T(8,128)(2,1)S(1)} async-done(((bf16[16,16,512]{2,1,0:T(8,128)(2,1)}), bf16[16,16,512]{2,1,0:T(8,128)(2,1)S(1)}, u32[]{:S(2)}, u32[]{:S(2)}) %all-to-all-start) | async-done | bytes 262176 | tf_op jit(solution)/shard_map/all_to_all | solution.py:196
  24.7 4.5 %all-to-all-start.1 = ((bf16[16,64,512]{2,1,0:T(8,128)(2,1)}), bf16[16,64,512]{2,1,0:T(8,128)(2,1)S(1)}, u32[]{:S(2)}, u32[]{:S(2)}) async-start(bf16[16,64,512]{2,1,0:T(8,128)(2,1)} %bitcast.127), calls=%async_computation.1 | async-start | bytes 2097152 | tf_op jit(solution)/shard_map/all_to_all | solution.py:198
  30.3 1.9 %subtract_convert_fusion = (bf16[33,128,128]{2,1,0:T(8,128)(2,1)S(1)}, bf16[33,128,128]{2,1,0:T(8,128)(2,1)S(1)}, bf16[33,128,128]{2,1,0:T(8,128)(2,1)S(1)}, bf16[33,128,128]{2,1,0:T(8,128)(2,1)S(1)}) fusion(f32[33,128]{1,0:T(8,128)S(1)} %fusion.51, f32[33,128]{1,0:T(8,128)S(1)} %fusion.52, f32[128,128]{1,0:T(8,128)S(1)} %fusion.24, f32[128,128]{1,0:T(8,128)S(1)} %fusion.25), kind=kLoop, calls=%fused_computation.7 | loop fusion | flops 9191424 | bytes 4490240 | tf_op jit(solution)/shard_map/convert.8
  32.2 2.5 %pad_maximum_fusion.2 = (bf16[33,256,128]{2,1,0:T(8,128)(2,1)}, bf16[33,256,128]{2,1,0:T(8,128)(2,1)}) fusion(bf16[33,128,128]{2,1,0:T(8,128)(2,1)S(1)} %get-tuple-element.62, bf16[33,128,128]{2,1,0:T(8,128)(2,1)S(1)} %get-tuple-element.64, bf16[33,128,128]{2,1,0:T(8,128)(2,1)S(1)} %get-tuple-element.63, bf16[33,128,128]{2,1,0:T(8,128)(2,1)S(1)} %get-tuple-element.61), kind=kLoop, calls=%fused_computation.4 | loop fusion | flops 8650752 | bytes 8650752 | tf_op jit(solution)/shard_map/concatenate | solution.py:43
  35.7 2.3 %copy.25 = bf16[32,128,128]{2,0,1:T(8,128)(2,1)} copy(bf16[32,128,128]{1,0,2:T(8,128)(2,1)S(1)} %bitcast.128) | data formatting | bytes 2097152 | tf_op jit(solution)/shard_map/reshape | solution.py:142
  37.9 5.4 %fusion.43 = f32[66,128,128]{2,0,1:T(8,128)} fusion(bf16[32,128,128]{2,0,1:T(8,128)(2,1)} %copy.25, f32[66,32]{0,1:T(8,128)S(1)} %pad_maximum_fusion.4), kind=kOutput, calls=%fused_computation.80 | convolution fusion | flops 415236096 | bytes 5382400 | tf_op jit(solution)/shard_map/kn,nml->kml/dot_general | solution.py:141
  43.3 12.9 %all-to-all-done.1 = bf16[16,64,512]{2,1,0:T(8,128)(2,1)S(1)} async-done(((bf16[16,64,512]{2,1,0:T(8,128)(2,1)}), bf16[16,64,512]{2,1,0:T(8,128)(2,1)S(1)}, u32[]{:S(2)}, u32[]{:S(2)}) %all-to-all-start.1) | async-done | bytes 1048608 | tf_op jit(solution)/shard_map/all_to_all | solution.py:198
  56.4 2.3 %collective-permute-done = f32[512]{0:T(512)S(1)} collective-permute-done((f32[512]{0:T(512)S(1)}, f32[512]{0:T(512)S(1)}, u32[]{:S(2)}, u32[]{:S(2)}) %collective-permute-start) | collective-permute-done | bytes 2080 | tf_op jit(solution)/shard_map/ppermute | solution.py:212
  59.9 1.5 copy.27
  61.5 1.7 %collective-permute-start.2 = (f32[512]{0:T(512)S(1)}, f32[512]{0:T(512)S(1)}, u32[]{:S(2)}, u32[]{:S(2)}) collective-permute-start(f32[512]{0:T(512)S(1)} %add.90), channel_id=1, source_target_pairs={{0,64},{1,65},{32,96},{33,97},{64,0},{65,1},{96,32},{97,33},{128,1... | collective-permute-start | bytes 6152 | tf_op jit(solution)/shard_map/ppermute | solution.py:212
  63.1 2.0 %fusion.38 = f32[66,128,128]{2,0,1:T(8,128)S(1)} fusion(bf16[32,128,128]{2,0,1:T(8,128)(2,1)S(1)} %copy.27, f32[66,32]{0,1:T(8,128)S(1)} %pad_maximum_fusion.4), kind=kOutput, calls=%fused_computation.75 | convolution fusion | flops 415236096 | bytes 5382400 | tf_op jit(solution)/shard_map/kn,nml->kml/dot_general | solution.py:152
  65.2 2.9 %copy.28.sig_re_ref.sig_im_ref = f32[66,128,128]{2,1,0:T(8,128)} copy(f32[66,128,128]{2,0,1:T(8,128)S(1)} %fusion.38) | data formatting | bytes 8650752 | tf_op jit(solution)/shard_map/kn,nml->kml/dot_general | solution.py:152
  68.1 2.7 %copy.30.taps_re_ref.taps_im_ref = f32[66,128,128]{2,1,0:T(8,128)} copy(f32[66,128,128]{2,0,1:T(8,128)S(1)} %bitcast.122) | data formatting | bytes 8650752 | tf_op jit(solution)/shard_map/optimization_barrier | solution.py:205
  70.8 3.3 %collective-permute-start.3 = (f32[512]{0:T(512)S(1)}, f32[512]{0:T(512)S(1)}, u32[]{:S(2)}, u32[]{:S(2)}) collective-permute-start(f32[512]{0:T(512)S(1)} %add.91), channel_id=1, source_target_pairs={{0,128},{1,129},{32,160},{33,161},{64,192},{65,193},{96,224},{97,2... | collective-permute-start | bytes 6152 | tf_op jit(solution)/shard_map/ppermute | solution.py:212
  74.1 16.2 %shard_map.109 = (f32[33,128,128]{2,1,0:T(8,128)}, f32[33,128,128]{2,1,0:T(8,128)}, f32[33,128,128]{2,1,0:T(8,128)}, f32[33,128,128]{2,1,0:T(8,128)}) custom-call(f32[66,128,128]{2,1,0:T(8,128)} %copy.28.sig_re_ref.sig_im_ref, f32[66,128,128]{2,1,0:T(8,128)} %copy.28.sig_re_ref.sig_im_ref, f32[66,128,128]{2,1,0:T(8,128)} %copy.30.taps_re_ref.taps_im_ref, ...), custom_call_target="tpu_custom_call" | custom-call | flops 2214592512 | bytes 21626880 | tf_op jit(solution)/shard_map/pallas_call | solution.py:123
  91.0 2.8 %pad_maximum_fusion = f32[66,128,128]{2,1,0:T(8,128)S(1)} fusion(f32[33,128,128]{2,1,0:T(8,128)} %get-tuple-element.40, f32[33,128,128]{2,1,0:T(8,128)} %get-tuple-element.39), kind=kLoop, calls=%fused_computation.2 | loop fusion | flops 1081344 | bytes 8650752 | tf_op jit(solution)/shard_map/concatenate | solution.py:166
  93.7 5.0 %fusion.2 = bf16[32,128,128]{2,0,1:T(8,128)(2,1)S(1)} fusion(f32[66,128,128]{2,1,0:T(8,128)S(1)} %pad_maximum_fusion, f32[32,66]{1,0:T(8,128)S(1)} %pad_maximum_fusion.5), kind=kOutput, calls=%fused_computation.10 | convolution fusion | flops 415760384 | bytes 5382400 | tf_op jit(solution)/shard_map/nk,kml->nml/dot_general | solution.py:167
  98.7 1.5 copy.33
  102.2 4.7 %all-to-all-start.2 = ((bf16[16,64,512]{2,1,0:T(8,128)(2,1)}), bf16[16,64,512]{2,1,0:T(8,128)(2,1)}, u32[]{:S(2)}, u32[]{:S(2)}) async-start(bf16[16,64,512]{2,1,0:T(8,128)(2,1)} %bitcast.19), calls=%async_computation.2 | async-start | bytes 2097152 | tf_op jit(solution)/shard_map/all_to_all | solution.py:231
  106.9 4.9 %pad_maximum_fusion.1 = f32[66,128,128]{2,1,0:T(8,128)} fusion(f32[33,128,128]{2,1,0:T(8,128)} %get-tuple-element.42, f32[33,128,128]{2,1,0:T(8,128)} %get-tuple-element.41), kind=kLoop, calls=%fused_computation.3 | loop fusion | flops 1081344 | bytes 8650752 | tf_op jit(solution)/shard_map/concatenate | solution.py:166
  111.8 5.8 %copy.43 = f32[66,128,128]{1,0,2:T(8,128)} copy(f32[66,128,128]{2,1,0:T(8,128)} %pad_maximum_fusion.1) | data formatting | bytes 8650752 | tf_op jit(solution)/shard_map/concatenate | solution.py:166
  117.6 4.2 %fusion.40 = f32[32,128,128]{1,0,2:T(8,128)S(1)} fusion(f32[66,128,128]{1,0,2:T(8,128)} %copy.43, f32[32,66]{1,0:T(8,128)S(1)} %pad_maximum_fusion.5), kind=kOutput, calls=%fused_computation.77 | convolution fusion | flops 415236096 | bytes 6430976 | tf_op jit(solution)/shard_map/nk,kml->nml/dot_general | solution.py:167
  121.8 1.5 reshape.172
  124.9 9.1 %all-to-all-done.2 = bf16[16,64,512]{2,1,0:T(8,128)(2,1)} async-done(((bf16[16,64,512]{2,1,0:T(8,128)(2,1)}), bf16[16,64,512]{2,1,0:T(8,128)(2,1)}, u32[]{:S(2)}, u32[]{:S(2)}) %all-to-all-start.2) | async-done | bytes 1048608 | tf_op jit(solution)/shard_map/all_to_all | solution.py:231
  134.9 4.5 %all-to-all-start.3 = ((bf16[16,32,512]{2,1,0:T(8,128)(2,1)}), bf16[16,32,512]{2,1,0:T(8,128)(2,1)}, u32[]{:S(2)}, u32[]{:S(2)}) async-start(bf16[16,32,512]{2,1,0:T(8,128)(2,1)} %bitcast.132), calls=%async_computation.3 | async-start | bytes 1048576 | tf_op jit(solution)/shard_map/all_to_all | solution.py:241
  140.7 2.0 %fusion.14 = (bf16[1,512,512]{1,2,0:T(8,128)(2,1)}, bf16[1,512,512]{1,2,0:T(8,128)(2,1)}, bf16[1,512,512]{1,2,0:T(8,128)(2,1)}, bf16[1,512,512]{1,2,0:T(8,128)(2,1)}) fusion(bf16[512,512]{0,1:T(8,128)(2,1)S(1)} %copy-done.5, bf16[1,16,32,512]{3,2,0,1:T(8,128)(2,1)S(1)} %get-tuple-element.59, bf16[1,512,512]{1,2,0:T(8,128)(2,1)S(1)} %copy.20, ...), kind=kLoop, calls=%fused_computation.35 | loop fusion | flops 5242880 | bytes 6293504 | tf_op jit(solution)/shard_map/broadcast_in_dim | solution.py:259
  142.7 2.1 %copy.41 = bf16[1,512,512]{2,1,0:T(8,128)(2,1)} copy(bf16[1,512,512]{1,2,0:T(8,128)(2,1)} %get-tuple-element.55) | data formatting | bytes 1048576
  144.8 2.0 %copy.40 = bf16[1,512,512]{2,1,0:T(8,128)(2,1)} copy(bf16[1,512,512]{1,2,0:T(8,128)(2,1)} %get-tuple-element.56) | data formatting | bytes 1048576
  148.9 6.2 %all-to-all-done.3 = bf16[16,32,512]{2,1,0:T(8,128)(2,1)} async-done(((bf16[16,32,512]{2,1,0:T(8,128)(2,1)}), bf16[16,32,512]{2,1,0:T(8,128)(2,1)}, u32[]{:S(2)}, u32[]{:S(2)}) %all-to-all-start.3) | async-done | bytes 524320 | tf_op jit(solution)/shard_map/all_to_all | solution.py:241
  (78 shorter events, 18.9 us)
Async XLA Ops:
  0.6 14.0 %copy-start.10 = (bf16[1,512,512]{2,1,0:T(8,128)(2,1)S(1)}, bf16[1,512,512]{2,1,0:T(8,128)(2,1)}, u32[]{:S(2)}) copy-start(bf16[1,512,512]{2,1,0:T(8,128)(2,1)} %param.6) | copy-start | bytes 1572868
  2.1 12.7 %copy-start.11 = (bf16[1,512,512]{2,1,0:T(8,128)(2,1)S(1)}, bf16[1,512,512]{2,1,0:T(8,128)(2,1)}, u32[]{:S(2)}) copy-start(bf16[1,512,512]{2,1,0:T(8,128)(2,1)} %param.7) | copy-start | bytes 1572868
  2.3 12.8 %copy-start.12 = (bf16[1,512,512]{2,1,0:T(8,128)(2,1)S(1)}, bf16[1,512,512]{2,1,0:T(8,128)(2,1)}, u32[]{:S(2)}) copy-start(bf16[1,512,512]{2,1,0:T(8,128)(2,1)} %param.8) | copy-start | bytes 1572868
  4.6 20.1 %all-to-all-start = ((bf16[16,16,512]{2,1,0:T(8,128)(2,1)}), bf16[16,16,512]{2,1,0:T(8,128)(2,1)S(1)}, u32[]{:S(2)}, u32[]{:S(2)}) async-start(bf16[16,16,512]{2,1,0:T(8,128)(2,1)} %convert_element_type.154), calls=%async_computation | async-start | bytes 524288 | tf_op jit(solution)/shard_map/all_to_all | solution.py:196
  15.3 2.0 %copy-start = (bf16[1,512,512]{1,2,0:T(8,128)(2,1)}, bf16[1,512,512]{1,2,0:T(8,128)(2,1)S(1)}, u32[]{:S(2)}) copy-start(bf16[1,512,512]{1,2,0:T(8,128)(2,1)S(1)} %copy.21) | copy-start | bytes 1572868
  16.7 0.8 copy-start.2
  17.1 7.6 %copy-start.4 = (bf16[512,512]{0,1:T(8,128)(2,1)}, bf16[512,512]{0,1:T(8,128)(2,1)S(1)}, u32[]{:S(2)}) copy-start(bf16[512,512]{0,1:T(8,128)(2,1)S(1)} %get-tuple-element.53) | copy-start | bytes 1572868
  17.1 7.6 %copy-start.6 = (bf16[512,512]{0,1:T(8,128)(2,1)}, bf16[512,512]{0,1:T(8,128)(2,1)S(1)}, u32[]{:S(2)}) copy-start(bf16[512,512]{0,1:T(8,128)(2,1)S(1)} %get-tuple-element.54) | copy-start | bytes 1572868
  24.7 31.5 %all-to-all-start.1 = ((bf16[16,64,512]{2,1,0:T(8,128)(2,1)}), bf16[16,64,512]{2,1,0:T(8,128)(2,1)S(1)}, u32[]{:S(2)}, u32[]{:S(2)}) async-start(bf16[16,64,512]{2,1,0:T(8,128)(2,1)} %bitcast.127), calls=%async_computation.1 | async-start | bytes 2097152 | tf_op jit(solution)/shard_map/all_to_all | solution.py:198
  56.2 2.4 %collective-permute-start = (f32[512]{0:T(512)S(1)}, f32[512]{0:T(512)S(1)}, u32[]{:S(2)}, u32[]{:S(2)}) collective-permute-start(f32[512]{0:T(512)S(1)} %get-tuple-element.29), channel_id=1, source_target_pairs={{0,1},{1,0},{32,33},{33,32},{64,65},{65,64},{96,97},{97,96},{128,1... | collective-permute-start | bytes 6152 | tf_op jit(solution)/shard_map/ppermute | solution.py:212
  58.6 2.8 %collective-permute-start.1 = (f32[512]{0:T(512)S(1)}, f32[512]{0:T(512)S(1)}, u32[]{:S(2)}, u32[]{:S(2)}) collective-permute-start(f32[512]{0:T(512)S(1)} %add.89), channel_id=1, source_target_pairs={{0,32},{1,33},{32,0},{33,1},{64,96},{65,97},{96,64},{97,65},{128,1... | collective-permute-start | bytes 6152 | tf_op jit(solution)/shard_map/ppermute | solution.py:212
  61.5 9.3 %collective-permute-start.2 = (f32[512]{0:T(512)S(1)}, f32[512]{0:T(512)S(1)}, u32[]{:S(2)}, u32[]{:S(2)}) collective-permute-start(f32[512]{0:T(512)S(1)} %add.90), channel_id=1, source_target_pairs={{0,64},{1,65},{32,96},{33,97},{64,0},{65,1},{96,32},{97,33},{128,1... | collective-permute-start | bytes 6152 | tf_op jit(solution)/shard_map/ppermute | solution.py:212
  63.1 4.9 %slice-start = ((s8[4718592]{0:T(1024)(128)(4,1)}), s8[4194304]{0:T(1024)(128)(4,1)S(1)}, s32[]{:S(2)}) async-start(s8[4718592]{0:T(1024)(128)(4,1)} %bitcast.121), calls=%async_computation.4 | async-start | bytes 8388608
  65.2 2.9 %slice-start.1 = ((s8[4718592]{0:T(1024)(128)(4,1)}), s8[524288]{0:T(1024)(128)(4,1)S(1)}, s32[]{:S(2)}) async-start(s8[4718592]{0:T(1024)(128)(4,1)} %bitcast.121), calls=%async_computation.5 | async-start | bytes 1048576
  70.8 19.6 %collective-permute-start.3 = (f32[512]{0:T(512)S(1)}, f32[512]{0:T(512)S(1)}, u32[]{:S(2)}, u32[]{:S(2)}) collective-permute-start(f32[512]{0:T(512)S(1)} %add.91), channel_id=1, source_target_pairs={{0,128},{1,129},{32,160},{33,161},{64,192},{65,193},{96,224},{97,2... | collective-permute-start | bytes 6152 | tf_op jit(solution)/shard_map/ppermute | solution.py:212
  102.2 31.8 %all-to-all-start.2 = ((bf16[16,64,512]{2,1,0:T(8,128)(2,1)}), bf16[16,64,512]{2,1,0:T(8,128)(2,1)}, u32[]{:S(2)}, u32[]{:S(2)}) async-start(bf16[16,64,512]{2,1,0:T(8,128)(2,1)} %bitcast.19), calls=%async_computation.2 | async-start | bytes 2097152 | tf_op jit(solution)/shard_map/all_to_all | solution.py:231
  124.7 15.9 %copy-start.1 = (bf16[1,512,512]{1,2,0:T(8,128)(2,1)S(1)}, bf16[1,512,512]{1,2,0:T(8,128)(2,1)}, u32[]{:S(2)}) copy-start(bf16[1,512,512]{1,2,0:T(8,128)(2,1)} %copy-done) | copy-start | bytes 1572868
  124.8 15.9 %copy-start.3 = (bf16[1,512,512]{1,2,0:T(8,128)(2,1)S(1)}, bf16[1,512,512]{1,2,0:T(8,128)(2,1)}, u32[]{:S(2)}) copy-start(bf16[1,512,512]{1,2,0:T(8,128)(2,1)} %copy-done.2) | copy-start | bytes 1572868
  124.8 15.9 %copy-start.5 = (bf16[512,512]{0,1:T(8,128)(2,1)S(1)}, bf16[512,512]{0,1:T(8,128)(2,1)}, u32[]{:S(2)}) copy-start(bf16[512,512]{0,1:T(8,128)(2,1)} %copy-done.4) | copy-start | bytes 1572868
  124.8 15.9 %copy-start.7 = (bf16[512,512]{0,1:T(8,128)(2,1)S(1)}, bf16[512,512]{0,1:T(8,128)(2,1)}, u32[]{:S(2)}) copy-start(bf16[512,512]{0,1:T(8,128)(2,1)} %copy-done.6) | copy-start | bytes 1572868
  124.8 15.9 %copy-start.13 = (f32[512]{0:T(512)S(1)}, f32[512]{0:T(512)}, u32[]{:S(2)}) copy-start(f32[512]{0:T(512)} %param.11) | copy-start | bytes 6148
  134.9 20.2 %all-to-all-start.3 = ((bf16[16,32,512]{2,1,0:T(8,128)(2,1)}), bf16[16,32,512]{2,1,0:T(8,128)(2,1)}, u32[]{:S(2)}, u32[]{:S(2)}) async-start(bf16[16,32,512]{2,1,0:T(8,128)(2,1)} %bitcast.132), calls=%async_computation.3 | async-start | bytes 1048576 | tf_op jit(solution)/shard_map/all_to_all | solution.py:241
  142.7 4.2 %copy-start.9 = (bf16[1,512,512]{1,2,0:T(8,128)(2,1)S(1)}, bf16[1,512,512]{1,2,0:T(8,128)(2,1)}, u32[]{:S(2)}) copy-start(bf16[1,512,512]{1,2,0:T(8,128)(2,1)} %get-tuple-element.65) | copy-start | bytes 1572868
  142.7 5.2 %copy-start.8 = (bf16[1,512,512]{1,2,0:T(8,128)(2,1)S(1)}, bf16[1,512,512]{1,2,0:T(8,128)(2,1)}, u32[]{:S(2)}) copy-start(bf16[1,512,512]{1,2,0:T(8,128)(2,1)} %get-tuple-element.66) | copy-start | bytes 1572868

commit v4 on v3

--- a/solution.py
+++ b/solution.py
@@ -78,7 +78,7 @@
 
 def middle_kernel(
     sig_re_ref, sig_im_ref, taps_re_ref, taps_im_ref, fwd_ref, inv_ref,
-    pair_re_ref, pair_im_ref, cross_re_ref, cross_im_ref,
+    pair_ref, cross_ref,
 ):
     steps, inner, lanes = sig_re_ref.shape
     half_lanes = lanes // 2
@@ -103,10 +103,10 @@
             jnp.bfloat16
         )
         back = jnp.dot(inv_ref[step], second, preferred_element_type=jnp.float32)
-        pair_re_ref[step] = back[:inner, 0:lanes] - back[inner:, lanes : 2 * lanes]
-        pair_im_ref[step] = back[:inner, lanes : 2 * lanes] + back[inner:, 0:lanes]
-        cross_re_ref[step] = back[:inner, 2 * lanes : 3 * lanes] - back[inner:, 3 * lanes :]
-        cross_im_ref[step] = back[:inner, 3 * lanes :] + back[inner:, 2 * lanes : 3 * lanes]
+        pair_ref[0, step] = back[:inner, 0:lanes] - back[inner:, lanes : 2 * lanes]
+        pair_ref[1, step] = back[:inner, lanes : 2 * lanes] + back[inner:, 0:lanes]
+        cross_ref[0, step] = back[:inner, 2 * lanes : 3 * lanes] - back[inner:, 3 * lanes :]
+        cross_ref[1, step] = back[:inner, 3 * lanes :] + back[inner:, 2 * lanes : 3 * lanes]
 
 
 def spectral_middle(sig_first, taps_first, fwd_table, inv_table):
@@ -117,15 +117,16 @@
     block = pl.BlockSpec((steps, inner, lanes), lambda k: (k, 0, 0))
     block_im = pl.BlockSpec((steps, inner, lanes), lambda k: (k + count, 0, 0))
     table_block = pl.BlockSpec((steps, rows2, inner), lambda k: (k, 0, 0))
-    out_shape = jax.ShapeDtypeStruct((half, inner, lanes), jnp.float32)
+    out_block = pl.BlockSpec((2, steps, inner, lanes), lambda k: (0, k, 0, 0))
+    out_shape = jax.ShapeDtypeStruct((2, half, inner, lanes), jnp.float32)
     flops = half * 2 * 2 * rows2 * inner * 4 * lanes
-    bytes_accessed = half * (8 * inner * lanes * 4 + 2 * rows2 * inner * 2)
+    bytes_accessed = half * (4 * inner * lanes * 2 + 4 * inner * lanes * 4 + 2 * rows2 * inner * 2)
     return pl.pallas_call(
         middle_kernel,
         grid=(count,),
         in_specs=[block, block_im, block, block_im, table_block, table_block],
-        out_specs=[block] * 4,
-        out_shape=[out_shape] * 4,
+        out_specs=[out_block] * 2,
+        out_shape=[out_shape] * 2,
         cost_estimate=pl.CostEstimate(
             flops=flops, transcendentals=0, bytes_accessed=bytes_accessed
         ),
@@ -141,7 +142,7 @@
     taps_first = jnp.einsum(
         "kn,nml->kml", stage_a, taps.reshape(rows, inner, lanes), precision=full_precision
     )
-    return tables, taps_first
+    return tables, taps_first.astype(jnp.bfloat16)
 
 
 def spectral_products(signals, taps_first, tables, carry):
@@ -152,18 +153,16 @@
     sig_first = jnp.einsum(
         "kn,nml->kml", stage_a, signals.reshape(rows, inner, lanes), precision=full_precision
     )
-    pair_re, pair_im, cross_re, cross_im = spectral_middle(
-        sig_first, taps_first, fwd_table, inv_table
-    )
-    carry, pair_re, pair_im, cross_re, cross_im = lax.optimization_barrier(
-        (carry, pair_re, pair_im, cross_re, cross_im)
-    )
-    return tables, (pair_re, pair_im), (cross_re, cross_im), carry
-
-
-def spectral_inverse(back_re, back_im, tables):
+    pair_spec, cross_spec = spectral_middle(
+        sig_first.astype(jnp.bfloat16), taps_first, fwd_table, inv_table
+    )
+    carry, pair_spec, cross_spec = lax.optimization_barrier((carry, pair_spec, cross_spec))
+    return tables, pair_spec, cross_spec, carry
+
+
+def spectral_inverse(back, tables):
     inv_a = tables[1]
-    both = jnp.concatenate([back_re, back_im], axis=0)
+    both = back.reshape((back.shape[0] * back.shape[1],) + back.shape[2:])
     return jnp.einsum("nk,kml->nml", inv_a, both, precision=full_precision)
 
 
@@ -219,7 +218,7 @@
     tables, pair_spec, cross_spec, grad_skip = spectral_products(
         signals.astype(jnp.float32), taps_first, tables, grad_skip
     )
-    pair_vals = spectral_inverse(pair_spec[0], pair_spec[1], tables)
+    pair_vals = spectral_inverse(pair_spec, tables)
     pair_vals = pair_vals.reshape(seq_length, 2, batch_count, share)
 
     pair_back = pair_vals.astype(jnp.bfloat16).reshape(
@@ -230,7 +229,7 @@
     )
     pair_home = lax.all_to_all(pair_back, ("seq", "dp"), 0, 0, tiled=True)
 
-    cross = spectral_inverse(cross_spec[0], cross_spec[1], tables)
+    cross = spectral_inverse(cross_spec, tables)
     cross = cross.reshape(seq_length, 2, batch_count, share)
     slope = jnp.sum(cross[:, 0], axis=1)
     slope_blocks = jnp.swapaxes(slope.astype(jnp.bfloat16).reshape(seq_count, local_length, share), 1, 2)

time: 159 us -> 156 us (0.981)
  other arithmetic: 18.7 us -> 11.1 us
  waiting for transfers between devices: 36.6 us -> 42.8 us
    concatenate x2 -> x0, other arithmetic: 7.63 us -> none  [spectral_inverse(): both = jnp.concatenate([back_re, back_im], axis=0)]
    concatenate x1 -> x0, local copies, waits for them, and re-layouts: 5.78 us -> none  [spectral_inverse(): both = jnp.concatenate([back_re, back_im], axis=0)]
    reshape x0 -> x1, local copies, waits for them, and re-layouts: none -> 5.77 us  [spectral_inverse(): both = back.reshape((back.shape[0] * back.shape[1],) + back.shape[2:])]
    all_to_all x1, waiting for transfers between devices: 9.12 us -> 14 us  [on_device(): pair_home = lax.all_to_all(pair_back, ('seq', 'dp'), 0, 0, tiled=True)]
    optimization_barrier x1 -> x0, local copies, waits for them, and re-layouts: 2.75 us -> none  [on_device(): lax.optimization_barrier((gain_part, got, tables, taps_first))]
    dot_general x2, matrix products: 9.21 us -> 11.3 us  [spectral_inverse(): return jnp.einsum('nk,kml->nml', inv_a, both, precision=full_precision)]
    dot_general x1, matrix products: 5.36 us -> 3.27 us  [taps_spectrum_first(): jnp.einsum('kn,nml->kml', stage_a, taps.reshape(rows, inner, lanes), prec...]
    dot_general x0 -> x1, local copies, waits for them, and re-layouts: none -> 1.86 us  [taps_spectrum_first(): jnp.einsum('kn,nml->kml', stage_a, taps.reshape(rows, inner, lanes), prec...]
  transfers between devices with their start and end apart: 8 -> 8, of which waited for: 5 -> 5; matrix products, arithmetic and copies ran while one was open for 35% -> 30% of each run, Pallas kernels for 10% -> 10%
where the time goes in v4:
time: 156 us; the launch traced here: 155 us
  waiting for transfers between devices  42.8 us (27%)
  local copies, waits for them, and re-layouts  38.2 us (24%)
  starting transfers between devices  28.8 us (18%)
  matrix products  16.6 us (11%)
  Pallas kernels  16.1 us (10%)
  other arithmetic  11.1 us (7%)
    pallas_call x1, Pallas kernels, spectral_middle(): pl.pallas_call(middle_kernel, grid=(count,), in_specs=[block, block_im, b...  16.1 us
    all_to_all x1, waiting for transfers between devices, on_device(): pair_home = lax.all_to_all(pair_back, ('seq', 'dp'), 0, 0, tiled=True)  14 us
    all_to_all x1, waiting for transfers between devices, on_device(): got = lax.all_to_all(pair, ('seq', 'dp'), 0, 0, tiled=True)  13 us
    dot_general x2, matrix products, spectral_inverse(): return jnp.einsum('nk,kml->nml', inv_a, both, precision=full_precision)  11.3 us
    all_to_all x1, starting transfers between devices, on_device(): taps_got = lax.all_to_all(taps_mine, ('seq', 'dp'), 0, 0, tiled=True)  9.98 us
    unnamed x41, local copies, waits for them, and re-layouts  9.03 us
    all_to_all x1, waiting for transfers between devices, on_device(): taps_got = lax.all_to_all(taps_mine, ('seq', 'dp'), 0, 0, tiled=True)  7.38 us
    all_to_all x1, waiting for transfers between devices, on_device(): slope_home = lax.all_to_all(slope_send, ('seq', 'dp'), 0, 0, tiled=True)  6.17 us
  transfers between devices with their start and end apart: 8, of which 5 were waited for; matrix products, arithmetic and copies ran while one was open for 30% of the time, Pallas kernels for 10%

profile of v4, /device:TPU:1, one launch (start us, length us, event | category | flops | bytes accessed | tf_op | source)
XLA Modules:
  0.0 154.7 jit_solution(17181620659759670591)
XLA Ops:
  0.6 1.5 copy.20
  2.3 1.5 convert_reduce_fusion
  4.6 10.0 %all-to-all-start = ((bf16[16,16,512]{2,1,0:T(8,128)(2,1)}), bf16[16,16,512]{2,1,0:T(8,128)(2,1)S(1)}, u32[]{:S(2)}, u32[]{:S(2)}) async-start(bf16[16,16,512]{2,1,0:T(8,128)(2,1)} %convert_element_type.160), calls=%async_computation | async-start | bytes 524288 | tf_op jit(solution)/shard_map/all_to_all | solution.py:195
  17.4 7.4 %all-to-all-done = bf16[16,16,512]{2,1,0:T(8,128)(2,1)S(1)} async-done(((bf16[16,16,512]{2,1,0:T(8,128)(2,1)}), bf16[16,16,512]{2,1,0:T(8,128)(2,1)S(1)}, u32[]{:S(2)}, u32[]{:S(2)}) %all-to-all-start) | async-done | bytes 262176 | tf_op jit(solution)/shard_map/all_to_all | solution.py:195
  24.8 4.5 %all-to-all-start.1 = ((bf16[16,64,512]{2,1,0:T(8,128)(2,1)}), bf16[16,64,512]{2,1,0:T(8,128)(2,1)S(1)}, u32[]{:S(2)}, u32[]{:S(2)}) async-start(bf16[16,64,512]{2,1,0:T(8,128)(2,1)} %bitcast.129), calls=%async_computation.1 | async-start | bytes 2097152 | tf_op jit(solution)/shard_map/all_to_all | solution.py:197
  30.3 1.9 %subtract_convert_fusion = (bf16[33,128,128]{2,1,0:T(8,128)(2,1)S(1)}, bf16[33,128,128]{2,1,0:T(8,128)(2,1)S(1)}, bf16[33,128,128]{2,1,0:T(8,128)(2,1)S(1)}, bf16[33,128,128]{2,1,0:T(8,128)(2,1)S(1)}) fusion(f32[33,128]{1,0:T(8,128)S(1)} %fusion.51, f32[33,128]{1,0:T(8,128)S(1)} %fusion.52, f32[128,128]{1,0:T(8,128)S(1)} %fusion.24, f32[128,128]{1,0:T(8,128)S(1)} %fusion.25), kind=kLoop, calls=%fused_computation.7 | loop fusion | flops 9191424 | bytes 4490240 | tf_op jit(solution)/shard_map/convert.8
  32.3 2.6 %pad_maximum_fusion = (bf16[33,256,128]{2,1,0:T(8,128)(2,1)}, bf16[33,256,128]{2,1,0:T(8,128)(2,1)}) fusion(bf16[33,128,128]{2,1,0:T(8,128)(2,1)S(1)} %get-tuple-element.54, bf16[33,128,128]{2,1,0:T(8,128)(2,1)S(1)} %get-tuple-element.56, bf16[33,128,128]{2,1,0:T(8,128)(2,1)S(1)} %get-tuple-element.55, bf16[33,128,128]{2,1,0:T(8,128)(2,1)S(1)} %get-tuple-element.53), kind=kLoop, calls=%fused_computation.4 | loop fusion | flops 8650752 | bytes 8650752 | tf_op jit(solution)/shard_map/concatenate | solution.py:43
  35.8 2.3 %copy.23 = bf16[32,128,128]{2,0,1:T(8,128)(2,1)} copy(bf16[32,128,128]{1,0,2:T(8,128)(2,1)S(1)} %bitcast.130) | data formatting | bytes 2097152 | tf_op jit(solution)/shard_map/reshape | solution.py:143
  38.0 3.3 %fusion.43 = bf16[66,128,128]{2,0,1:T(8,128)(2,1)S(1)} fusion(bf16[32,128,128]{2,0,1:T(8,128)(2,1)} %copy.23, f32[66,32]{0,1:T(8,128)S(1)} %pad_maximum_fusion.2), kind=kOutput, calls=%fused_computation.80 | convolution fusion | flops 415236096 | bytes 3219712 | tf_op jit(solution)/shard_map/kn,nml->kml/dot_general | solution.py:142
  41.3 1.9 %copy.53.taps_re_ref.taps_im_ref = bf16[66,128,128]{2,1,0:T(8,128)(2,1)} copy(bf16[66,128,128]{2,0,1:T(8,128)(2,1)S(1)} %fusion.43) | data formatting | bytes 4325376 | tf_op jit(solution)/shard_map/kn,nml->kml/dot_general | solution.py:142
  43.2 13.0 %all-to-all-done.1 = bf16[16,64,512]{2,1,0:T(8,128)(2,1)S(1)} async-done(((bf16[16,64,512]{2,1,0:T(8,128)(2,1)}), bf16[16,64,512]{2,1,0:T(8,128)(2,1)S(1)}, u32[]{:S(2)}, u32[]{:S(2)}) %all-to-all-start.1) | async-done | bytes 1048608 | tf_op jit(solution)/shard_map/all_to_all | solution.py:197
  56.4 2.3 %collective-permute-done = f32[512]{0:T(512)S(1)} collective-permute-done((f32[512]{0:T(512)S(1)}, f32[512]{0:T(512)S(1)}, u32[]{:S(2)}, u32[]{:S(2)}) %collective-permute-start) | collective-permute-done | bytes 2080 | tf_op jit(solution)/shard_map/ppermute | solution.py:211
  59.2 1.4 reshape.176
  60.7 2.5 %copy.26 = bf16[32,128,128]{2,0,1:T(8,128)(2,1)S(1)} copy(bf16[32,128,128]{1,0,2:T(8,128)(2,1)} %reshape.176) | data formatting | bytes 2097152 | tf_op jit(solution)/shard_map/reshape | solution.py:154
  63.2 1.7 %collective-permute-start.2 = (f32[512]{0:T(512)S(1)}, f32[512]{0:T(512)S(1)}, u32[]{:S(2)}, u32[]{:S(2)}) collective-permute-start(f32[512]{0:T(512)S(1)} %add.90), channel_id=1, source_target_pairs={{0,64},{1,65},{32,96},{33,97},{64,0},{65,1},{96,32},{97,33},{128,1... | collective-permute-start | bytes 6152 | tf_op jit(solution)/shard_map/ppermute | solution.py:211
  64.8 2.0 %fusion.38 = bf16[66,128,128]{2,0,1:T(8,128)(2,1)S(1)} fusion(bf16[32,128,128]{2,0,1:T(8,128)(2,1)S(1)} %copy.26, f32[66,32]{0,1:T(8,128)S(1)} %pad_maximum_fusion.2), kind=kOutput, calls=%fused_computation.75 | convolution fusion | flops 415236096 | bytes 3219712 | tf_op jit(solution)/shard_map/kn,nml->kml/dot_general | solution.py:153
  66.9 1.9 %copy.52.sig_re_ref.sig_im_ref = bf16[66,128,128]{2,1,0:T(8,128)(2,1)} copy(bf16[66,128,128]{2,0,1:T(8,128)(2,1)S(1)} %fusion.38) | data formatting | bytes 4325376 | tf_op jit(solution)/shard_map/kn,nml->kml/dot_general | solution.py:153
  68.8 3.3 %collective-permute-start.3 = (f32[512]{0:T(512)S(1)}, f32[512]{0:T(512)S(1)}, u32[]{:S(2)}, u32[]{:S(2)}) collective-permute-start(f32[512]{0:T(512)S(1)} %add.91), channel_id=1, source_target_pairs={{0,128},{1,129},{32,160},{33,161},{64,192},{65,193},{96,224},{97,2... | collective-permute-start | bytes 6152 | tf_op jit(solution)/shard_map/ppermute | solution.py:211
  72.1 16.1 %shard_map.109 = (f32[2,33,128,128]{3,2,1,0:T(8,128)}, f32[2,33,128,128]{3,2,1,0:T(8,128)}) custom-call(bf16[66,128,128]{2,1,0:T(8,128)(2,1)} %copy.52.sig_re_ref.sig_im_ref, bf16[66,128,128]{2,1,0:T(8,128)(2,1)} %copy.52.sig_re_ref.sig_im_ref, bf16[66,128,128]{2,1,0:T(8,128)(2,1)} %copy.53.taps_re_ref.taps_im_ref, ...), custom_call_target="tpu_custom_call" | custom-call | flops 2214592512 | bytes 17301504 | tf_op jit(solution)/shard_map/pallas_call | solution.py:124
  88.8 7.1 %fusion.2 = bf16[32,128,128]{2,0,1:T(8,128)(2,1)S(1)} fusion(f32[66,128,128]{2,1,0:T(8,128)} %bitcast.123, f32[32,66]{1,0:T(8,128)S(1)} %pad_maximum_fusion.3), kind=kOutput, calls=%fused_computation.10 | convolution fusion | flops 415760384 | bytes 5382400 | tf_op jit(solution)/shard_map/nk,kml->nml/dot_general | solution.py:166
  95.9 1.5 copy.29
  99.4 4.7 %all-to-all-start.2 = ((bf16[16,64,512]{2,1,0:T(8,128)(2,1)}), bf16[16,64,512]{2,1,0:T(8,128)(2,1)}, u32[]{:S(2)}, u32[]{:S(2)}) async-start(bf16[16,64,512]{2,1,0:T(8,128)(2,1)} %bitcast.20), calls=%async_computation.2 | async-start | bytes 2097152 | tf_op jit(solution)/shard_map/all_to_all | solution.py:230
  104.1 5.8 %copy.39 = f32[66,128,128]{1,0,2:T(8,128)} copy(f32[66,128,128]{2,1,0:T(8,128)} %bitcast.126) | data formatting | bytes 8650752 | tf_op jit(solution)/shard_map/reshape | solution.py:165
  109.8 4.2 %fusion.40 = f32[32,128,128]{1,0,2:T(8,128)S(1)} fusion(f32[66,128,128]{1,0,2:T(8,128)} %copy.39, f32[32,66]{1,0:T(8,128)S(1)} %pad_maximum_fusion.3), kind=kOutput, calls=%fused_computation.77 | convolution fusion | flops 415236096 | bytes 6430976 | tf_op jit(solution)/shard_map/nk,kml->nml/dot_general | solution.py:166
  114.1 1.5 reshape.180
  115.6 1.3 slice_reduce_fusion
  117.2 14.0 %all-to-all-done.2 = bf16[16,64,512]{2,1,0:T(8,128)(2,1)} async-done(((bf16[16,64,512]{2,1,0:T(8,128)(2,1)}), bf16[16,64,512]{2,1,0:T(8,128)(2,1)}, u32[]{:S(2)}, u32[]{:S(2)}) %all-to-all-start.2) | async-done | bytes 1048608 | tf_op jit(solution)/shard_map/all_to_all | solution.py:230
  132.0 4.5 %all-to-all-start.3 = ((bf16[16,32,512]{2,1,0:T(8,128)(2,1)}), bf16[16,32,512]{2,1,0:T(8,128)(2,1)}, u32[]{:S(2)}, u32[]{:S(2)}) async-start(bf16[16,32,512]{2,1,0:T(8,128)(2,1)} %bitcast.134), calls=%async_computation.3 | async-start | bytes 1048576 | tf_op jit(solution)/shard_map/all_to_all | solution.py:240
  137.8 2.0 %fusion.14 = (bf16[1,512,512]{1,2,0:T(8,128)(2,1)}, bf16[1,512,512]{1,2,0:T(8,128)(2,1)}, bf16[1,512,512]{1,2,0:T(8,128)(2,1)}, bf16[1,512,512]{1,2,0:T(8,128)(2,1)}) fusion(bf16[512,512]{0,1:T(8,128)(2,1)S(1)} %copy-done.5, bf16[1,16,32,512]{3,2,0,1:T(8,128)(2,1)S(1)} %get-tuple-element.51, bf16[1,512,512]{1,2,0:T(8,128)(2,1)S(1)} %copy.18, ...), kind=kLoop, calls=%fused_computation.35 | loop fusion | flops 5242880 | bytes 6293504 | tf_op jit(solution)/shard_map/broadcast_in_dim | solution.py:258
  139.8 2.1 %copy.37 = bf16[1,512,512]{2,1,0:T(8,128)(2,1)} copy(bf16[1,512,512]{1,2,0:T(8,128)(2,1)} %get-tuple-element.47) | data formatting | bytes 1048576
  142.0 2.0 %copy.36 = bf16[1,512,512]{2,1,0:T(8,128)(2,1)} copy(bf16[1,512,512]{1,2,0:T(8,128)(2,1)} %get-tuple-element.48) | data formatting | bytes 1048576
  146.0 6.2 %all-to-all-done.3 = bf16[16,32,512]{2,1,0:T(8,128)(2,1)} async-done(((bf16[16,32,512]{2,1,0:T(8,128)(2,1)}), bf16[16,32,512]{2,1,0:T(8,128)(2,1)}, u32[]{:S(2)}, u32[]{:S(2)}) %all-to-all-start.3) | async-done | bytes 524320 | tf_op jit(solution)/shard_map/all_to_all | solution.py:240
  (73 shorter events, 15.7 us)
Async XLA Ops:
  0.6 14.0 %copy-start.10 = (bf16[1,512,512]{2,1,0:T(8,128)(2,1)S(1)}, bf16[1,512,512]{2,1,0:T(8,128)(2,1)}, u32[]{:S(2)}) copy-start(bf16[1,512,512]{2,1,0:T(8,128)(2,1)} %param.6) | copy-start | bytes 1572868
  2.1 12.7 %copy-start.11 = (bf16[1,512,512]{2,1,0:T(8,128)(2,1)S(1)}, bf16[1,512,512]{2,1,0:T(8,128)(2,1)}, u32[]{:S(2)}) copy-start(bf16[1,512,512]{2,1,0:T(8,128)(2,1)} %param.7) | copy-start | bytes 1572868
  2.3 12.8 %copy-start.12 = (bf16[1,512,512]{2,1,0:T(8,128)(2,1)S(1)}, bf16[1,512,512]{2,1,0:T(8,128)(2,1)}, u32[]{:S(2)}) copy-start(bf16[1,512,512]{2,1,0:T(8,128)(2,1)} %param.8) | copy-start | bytes 1572868
  3.8 11.5 %copy-start.13 = (bf16[1,512,512]{2,1,0:T(8,128)(2,1)S(1)}, bf16[1,512,512]{2,1,0:T(8,128)(2,1)}, u32[]{:S(2)}) copy-start(bf16[1,512,512]{2,1,0:T(8,128)(2,1)} %param.9) | copy-start | bytes 1572868
  4.6 20.1 %all-to-all-start = ((bf16[16,16,512]{2,1,0:T(8,128)(2,1)}), bf16[16,16,512]{2,1,0:T(8,128)(2,1)S(1)}, u32[]{:S(2)}, u32[]{:S(2)}) async-start(bf16[16,16,512]{2,1,0:T(8,128)(2,1)} %convert_element_type.160), calls=%async_computation | async-start | bytes 524288 | tf_op jit(solution)/shard_map/all_to_all | solution.py:195
  15.3 0.8 copy-start
  15.5 0.8 copy-start.2
  15.9 8.8 %copy-start.4 = (bf16[512,512]{0,1:T(8,128)(2,1)}, bf16[512,512]{0,1:T(8,128)(2,1)S(1)}, u32[]{:S(2)}) copy-start(bf16[512,512]{0,1:T(8,128)(2,1)S(1)} %get-tuple-element.45) | copy-start | bytes 1572868
  15.9 8.8 %copy-start.6 = (bf16[512,512]{0,1:T(8,128)(2,1)}, bf16[512,512]{0,1:T(8,128)(2,1)S(1)}, u32[]{:S(2)}) copy-start(bf16[512,512]{0,1:T(8,128)(2,1)S(1)} %get-tuple-element.46) | copy-start | bytes 1572868
  24.8 31.5 %all-to-all-start.1 = ((bf16[16,64,512]{2,1,0:T(8,128)(2,1)}), bf16[16,64,512]{2,1,0:T(8,128)(2,1)S(1)}, u32[]{:S(2)}, u32[]{:S(2)}) async-start(bf16[16,64,512]{2,1,0:T(8,128)(2,1)} %bitcast.129), calls=%async_computation.1 | async-start | bytes 2097152 | tf_op jit(solution)/shard_map/all_to_all | solution.py:197
  56.2 2.4 %collective-permute-start = (f32[512]{0:T(512)S(1)}, f32[512]{0:T(512)S(1)}, u32[]{:S(2)}, u32[]{:S(2)}) collective-permute-start(f32[512]{0:T(512)S(1)} %get-tuple-element.25), channel_id=1, source_target_pairs={{0,1},{1,0},{32,33},{33,32},{64,65},{65,64},{96,97},{97,96},{128,1... | collective-permute-start | bytes 6152 | tf_op jit(solution)/shard_map/ppermute | solution.py:211
  58.7 4.5 %collective-permute-start.1 = (f32[512]{0:T(512)S(1)}, f32[512]{0:T(512)S(1)}, u32[]{:S(2)}, u32[]{:S(2)}) collective-permute-start(f32[512]{0:T(512)S(1)} %add.89), channel_id=1, source_target_pairs={{0,32},{1,33},{32,0},{33,1},{64,96},{65,97},{96,64},{97,65},{128,1... | collective-permute-start | bytes 6152 | tf_op jit(solution)/shard_map/ppermute | solution.py:211
  63.2 5.6 %collective-permute-start.2 = (f32[512]{0:T(512)S(1)}, f32[512]{0:T(512)S(1)}, u32[]{:S(2)}, u32[]{:S(2)}) collective-permute-start(f32[512]{0:T(512)S(1)} %add.90), channel_id=1, source_target_pairs={{0,64},{1,65},{32,96},{33,97},{64,0},{65,1},{96,32},{97,33},{128,1... | collective-permute-start | bytes 6152 | tf_op jit(solution)/shard_map/ppermute | solution.py:211
  68.8 19.4 %collective-permute-start.3 = (f32[512]{0:T(512)S(1)}, f32[512]{0:T(512)S(1)}, u32[]{:S(2)}, u32[]{:S(2)}) collective-permute-start(f32[512]{0:T(512)S(1)} %add.91), channel_id=1, source_target_pairs={{0,128},{1,129},{32,160},{33,161},{64,192},{65,193},{96,224},{97,2... | collective-permute-start | bytes 6152 | tf_op jit(solution)/shard_map/ppermute | solution.py:211
  99.4 31.8 %all-to-all-start.2 = ((bf16[16,64,512]{2,1,0:T(8,128)(2,1)}), bf16[16,64,512]{2,1,0:T(8,128)(2,1)}, u32[]{:S(2)}, u32[]{:S(2)}) async-start(bf16[16,64,512]{2,1,0:T(8,128)(2,1)} %bitcast.20), calls=%async_computation.2 | async-start | bytes 2097152 | tf_op jit(solution)/shard_map/all_to_all | solution.py:230
  117.0 20.7 %copy-start.1 = (bf16[1,512,512]{1,2,0:T(8,128)(2,1)S(1)}, bf16[1,512,512]{1,2,0:T(8,128)(2,1)}, u32[]{:S(2)}) copy-start(bf16[1,512,512]{1,2,0:T(8,128)(2,1)} %copy-done) | copy-start | bytes 1572868
  117.0 20.7 %copy-start.3 = (bf16[1,512,512]{1,2,0:T(8,128)(2,1)S(1)}, bf16[1,512,512]{1,2,0:T(8,128)(2,1)}, u32[]{:S(2)}) copy-start(bf16[1,512,512]{1,2,0:T(8,128)(2,1)} %copy-done.2) | copy-start | bytes 1572868
  117.1 20.7 %copy-start.5 = (bf16[512,512]{0,1:T(8,128)(2,1)S(1)}, bf16[512,512]{0,1:T(8,128)(2,1)}, u32[]{:S(2)}) copy-start(bf16[512,512]{0,1:T(8,128)(2,1)} %copy-done.4) | copy-start | bytes 1572868
  117.1 20.7 %copy-start.7 = (bf16[512,512]{0,1:T(8,128)(2,1)S(1)}, bf16[512,512]{0,1:T(8,128)(2,1)}, u32[]{:S(2)}) copy-start(bf16[512,512]{0,1:T(8,128)(2,1)} %copy-done.6) | copy-start | bytes 1572868
  117.1 20.7 %copy-start.14 = (f32[512]{0:T(512)S(1)}, f32[512]{0:T(512)}, u32[]{:S(2)}) copy-start(f32[512]{0:T(512)} %param.11) | copy-start | bytes 6148
  132.0 20.2 %all-to-all-start.3 = ((bf16[16,32,512]{2,1,0:T(8,128)(2,1)}), bf16[16,32,512]{2,1,0:T(8,128)(2,1)}, u32[]{:S(2)}, u32[]{:S(2)}) async-start(bf16[16,32,512]{2,1,0:T(8,128)(2,1)} %bitcast.134), calls=%async_computation.3 | async-start | bytes 1048576 | tf_op jit(solution)/shard_map/all_to_all | solution.py:240
  139.8 4.2 %copy-start.9 = (bf16[1,512,512]{1,2,0:T(8,128)(2,1)S(1)}, bf16[1,512,512]{1,2,0:T(8,128)(2,1)}, u32[]{:S(2)}) copy-start(bf16[1,512,512]{1,2,0:T(8,128)(2,1)} %get-tuple-element.57) | copy-start | bytes 1572868
  139.8 5.2 %copy-start.8 = (bf16[1,512,512]{1,2,0:T(8,128)(2,1)S(1)}, bf16[1,512,512]{1,2,0:T(8,128)(2,1)}, u32[]{:S(2)}) copy-start(bf16[1,512,512]{1,2,0:T(8,128)(2,1)} %get-tuple-element.58) | copy-start | bytes 1572868

commit v5 on v4

--- a/solution.py
+++ b/solution.py
@@ -7,7 +7,7 @@
 from jax.experimental.pallas import tpu as pltpu
 from jax.sharding import PartitionSpec as P
 
-full_precision = lax.Precision.HIGHEST
+full_precision = lax.Precision.HIGH
 
 
 def spectral_tables(seq_length):

time: 156 us -> 154 us (0.987)
  matrix products: 16.6 us -> 13.6 us
    dot_general x2, matrix products: 11.3 us -> 9.53 us  [spectral_inverse(): return jnp.einsum('nk,kml->nml', inv_a, both, precision=full_precision)]
  transfers between devices with their start and end apart: 8 -> 8, of which waited for: 5 -> 5; matrix products, arithmetic and copies ran while one was open for 30% -> 30% of each run, Pallas kernels for 10% -> 11%
where the time goes in v5:
time: 154 us; the launch traced here: 153 us
  waiting for transfers between devices  44.1 us (29%)
  local copies, waits for them, and re-layouts  38.2 us (25%)
  starting transfers between devices  29 us (19%)
  Pallas kernels  16.1 us (10%)
  matrix products  13.6 us (9%)
  other arithmetic  11.1 us (7%)
    pallas_call x1, Pallas kernels, spectral_middle(): pl.pallas_call(middle_kernel, grid=(count,), in_specs=[block, block_im, b...  16.1 us
    all_to_all x1, waiting for transfers between devices, on_device(): pair_home = lax.all_to_all(pair_back, ('seq', 'dp'), 0, 0, tiled=True)  14.6 us
    all_to_all x1, waiting for transfers between devices, on_device(): got = lax.all_to_all(pair, ('seq', 'dp'), 0, 0, tiled=True)  13.6 us
    all_to_all x1, starting transfers between devices, on_device(): taps_got = lax.all_to_all(taps_mine, ('seq', 'dp'), 0, 0, tiled=True)  9.98 us
    dot_general x2, matrix products, spectral_inverse(): return jnp.einsum('nk,kml->nml', inv_a, both, precision=full_precision)  9.53 us
    unnamed x41, local copies, waits for them, and re-layouts  9.03 us
    all_to_all x1, waiting for transfers between devices, on_device(): taps_got = lax.all_to_all(taps_mine, ('seq', 'dp'), 0, 0, tiled=True)  7.38 us
    all_to_all x1, waiting for transfers between devices, on_device(): slope_home = lax.all_to_all(slope_send, ('seq', 'dp'), 0, 0, tiled=True)  6.17 us
  transfers between devices with their start and end apart: 8, of which 5 were waited for; matrix products, arithmetic and copies ran while one was open for 30% of the time, Pallas kernels for 11%

profile of v5, /device:TPU:1, one launch (start us, length us, event | category | flops | bytes accessed | tf_op | source)
XLA Modules:
  0.0 153.1 jit_solution(1825188824624194727)
XLA Ops:
  0.6 1.5 copy.20
  2.3 1.5 convert_reduce_fusion
  4.6 10.0 %all-to-all-start = ((bf16[16,16,512]{2,1,0:T(8,128)(2,1)}), bf16[16,16,512]{2,1,0:T(8,128)(2,1)S(1)}, u32[]{:S(2)}, u32[]{:S(2)}) async-start(bf16[16,16,512]{2,1,0:T(8,128)(2,1)} %convert_element_type.160), calls=%async_computation | async-start | bytes 524288 | tf_op jit(solution)/shard_map/all_to_all | solution.py:195
  17.4 7.4 %all-to-all-done = bf16[16,16,512]{2,1,0:T(8,128)(2,1)S(1)} async-done(((bf16[16,16,512]{2,1,0:T(8,128)(2,1)}), bf16[16,16,512]{2,1,0:T(8,128)(2,1)S(1)}, u32[]{:S(2)}, u32[]{:S(2)}) %all-to-all-start) | async-done | bytes 262176 | tf_op jit(solution)/shard_map/all_to_all | solution.py:195
  24.8 4.5 %all-to-all-start.1 = ((bf16[16,64,512]{2,1,0:T(8,128)(2,1)}), bf16[16,64,512]{2,1,0:T(8,128)(2,1)S(1)}, u32[]{:S(2)}, u32[]{:S(2)}) async-start(bf16[16,64,512]{2,1,0:T(8,128)(2,1)} %bitcast.129), calls=%async_computation.1 | async-start | bytes 2097152 | tf_op jit(solution)/shard_map/all_to_all | solution.py:197
  30.3 1.9 %subtract_convert_fusion = (bf16[33,128,128]{2,1,0:T(8,128)(2,1)S(1)}, bf16[33,128,128]{2,1,0:T(8,128)(2,1)S(1)}, bf16[33,128,128]{2,1,0:T(8,128)(2,1)S(1)}, bf16[33,128,128]{2,1,0:T(8,128)(2,1)S(1)}) fusion(f32[33,128]{1,0:T(8,128)S(1)} %fusion.51, f32[33,128]{1,0:T(8,128)S(1)} %fusion.52, f32[128,128]{1,0:T(8,128)S(1)} %fusion.24, f32[128,128]{1,0:T(8,128)S(1)} %fusion.25), kind=kLoop, calls=%fused_computation.7 | loop fusion | flops 9191424 | bytes 4490240 | tf_op jit(solution)/shard_map/convert.8
  32.3 2.6 %pad_maximum_fusion = (bf16[33,256,128]{2,1,0:T(8,128)(2,1)}, bf16[33,256,128]{2,1,0:T(8,128)(2,1)}) fusion(bf16[33,128,128]{2,1,0:T(8,128)(2,1)S(1)} %get-tuple-element.54, bf16[33,128,128]{2,1,0:T(8,128)(2,1)S(1)} %get-tuple-element.56, bf16[33,128,128]{2,1,0:T(8,128)(2,1)S(1)} %get-tuple-element.55, bf16[33,128,128]{2,1,0:T(8,128)(2,1)S(1)} %get-tuple-element.53), kind=kLoop, calls=%fused_computation.4 | loop fusion | flops 8650752 | bytes 8650752 | tf_op jit(solution)/shard_map/concatenate | solution.py:43
  35.8 2.3 %copy.23 = bf16[32,128,128]{2,0,1:T(8,128)(2,1)} copy(bf16[32,128,128]{1,0,2:T(8,128)(2,1)S(1)} %bitcast.130) | data formatting | bytes 2097152 | tf_op jit(solution)/shard_map/reshape | solution.py:143
  38.0 2.7 %fusion.43 = bf16[66,128,128]{2,0,1:T(8,128)(2,1)S(1)} fusion(bf16[32,128,128]{2,0,1:T(8,128)(2,1)} %copy.23, f32[66,32]{0,1:T(8,128)S(1)} %pad_maximum_fusion.2), kind=kOutput, calls=%fused_computation.80 | convolution fusion | flops 207618048 | bytes 3219712 | tf_op jit(solution)/shard_map/kn,nml->kml/dot_general | solution.py:142
  40.7 1.9 %copy.53.taps_re_ref.taps_im_ref = bf16[66,128,128]{2,1,0:T(8,128)(2,1)} copy(bf16[66,128,128]{2,0,1:T(8,128)(2,1)S(1)} %fusion.43) | data formatting | bytes 4325376 | tf_op jit(solution)/shard_map/kn,nml->kml/dot_general | solution.py:142
  42.6 13.6 %all-to-all-done.1 = bf16[16,64,512]{2,1,0:T(8,128)(2,1)S(1)} async-done(((bf16[16,64,512]{2,1,0:T(8,128)(2,1)}), bf16[16,64,512]{2,1,0:T(8,128)(2,1)S(1)}, u32[]{:S(2)}, u32[]{:S(2)}) %all-to-all-start.1) | async-done | bytes 1048608 | tf_op jit(solution)/shard_map/all_to_all | solution.py:197
  56.4 2.3 %collective-permute-done = f32[512]{0:T(512)S(1)} collective-permute-done((f32[512]{0:T(512)S(1)}, f32[512]{0:T(512)S(1)}, u32[]{:S(2)}, u32[]{:S(2)}) %collective-permute-start) | collective-permute-done | bytes 2080 | tf_op jit(solution)/shard_map/ppermute | solution.py:211
  59.2 1.4 reshape.176
  60.7 2.5 %copy.26 = bf16[32,128,128]{2,0,1:T(8,128)(2,1)S(1)} copy(bf16[32,128,128]{1,0,2:T(8,128)(2,1)} %reshape.176) | data formatting | bytes 2097152 | tf_op jit(solution)/shard_map/reshape | solution.py:154
  63.2 1.8 %collective-permute-start.2 = (f32[512]{0:T(512)S(1)}, f32[512]{0:T(512)S(1)}, u32[]{:S(2)}, u32[]{:S(2)}) collective-permute-start(f32[512]{0:T(512)S(1)} %add.90), channel_id=1, source_target_pairs={{0,64},{1,65},{32,96},{33,97},{64,0},{65,1},{96,32},{97,33},{128,1... | collective-permute-start | bytes 6152 | tf_op jit(solution)/shard_map/ppermute | solution.py:211
  65.0 1.4 fusion.38
  66.5 1.9 %copy.52.sig_re_ref.sig_im_ref = bf16[66,128,128]{2,1,0:T(8,128)(2,1)} copy(bf16[66,128,128]{2,0,1:T(8,128)(2,1)S(1)} %fusion.38) | data formatting | bytes 4325376 | tf_op jit(solution)/shard_map/kn,nml->kml/dot_general | solution.py:153
  68.3 3.3 %collective-permute-start.3 = (f32[512]{0:T(512)S(1)}, f32[512]{0:T(512)S(1)}, u32[]{:S(2)}, u32[]{:S(2)}) collective-permute-start(f32[512]{0:T(512)S(1)} %add.91), channel_id=1, source_target_pairs={{0,128},{1,129},{32,160},{33,161},{64,192},{65,193},{96,224},{97,2... | collective-permute-start | bytes 6152 | tf_op jit(solution)/shard_map/ppermute | solution.py:211
  71.7 16.1 %shard_map.109 = (f32[2,33,128,128]{3,2,1,0:T(8,128)}, f32[2,33,128,128]{3,2,1,0:T(8,128)}) custom-call(bf16[66,128,128]{2,1,0:T(8,128)(2,1)} %copy.52.sig_re_ref.sig_im_ref, bf16[66,128,128]{2,1,0:T(8,128)(2,1)} %copy.52.sig_re_ref.sig_im_ref, bf16[66,128,128]{2,1,0:T(8,128)(2,1)} %copy.53.taps_re_ref.taps_im_ref, ...), custom_call_target="tpu_custom_call" | custom-call | flops 2214592512 | bytes 17301504 | tf_op jit(solution)/shard_map/pallas_call | solution.py:124
  88.3 5.9 %fusion.2 = bf16[32,128,128]{2,0,1:T(8,128)(2,1)S(1)} fusion(f32[66,128,128]{2,1,0:T(8,128)} %bitcast.123, f32[32,66]{1,0:T(8,128)S(1)} %pad_maximum_fusion.3), kind=kOutput, calls=%fused_computation.10 | convolution fusion | flops 208142336 | bytes 5382400 | tf_op jit(solution)/shard_map/nk,kml->nml/dot_general | solution.py:166
  94.2 1.5 %copy.29 = bf16[32,128,128]{1,0,2:T(8,128)(2,1)S(1)} copy(bf16[32,128,128]{2,0,1:T(8,128)(2,1)S(1)} %fusion.2) | data formatting | bytes 2097152 | tf_op jit(solution)/shard_map/convert_element_type | solution.py:224
  97.7 4.7 %all-to-all-start.2 = ((bf16[16,64,512]{2,1,0:T(8,128)(2,1)}), bf16[16,64,512]{2,1,0:T(8,128)(2,1)}, u32[]{:S(2)}, u32[]{:S(2)}) async-start(bf16[16,64,512]{2,1,0:T(8,128)(2,1)} %bitcast.20), calls=%async_computation.2 | async-start | bytes 2097152 | tf_op jit(solution)/shard_map/all_to_all | solution.py:230
  102.4 5.8 %copy.39 = f32[66,128,128]{1,0,2:T(8,128)} copy(f32[66,128,128]{2,1,0:T(8,128)} %bitcast.126) | data formatting | bytes 8650752 | tf_op jit(solution)/shard_map/reshape | solution.py:165
  108.2 3.6 %fusion.40 = f32[32,128,128]{1,0,2:T(8,128)S(1)} fusion(f32[66,128,128]{1,0,2:T(8,128)} %copy.39, f32[32,66]{1,0:T(8,128)S(1)} %pad_maximum_fusion.3), kind=kOutput, calls=%fused_computation.77 | convolution fusion | flops 207618048 | bytes 6430976 | tf_op jit(solution)/shard_map/nk,kml->nml/dot_general | solution.py:166
  111.9 1.5 %reshape.180 = f32[4096,2,2,32]{0,3,2,1:T(8,128)} reshape(f32[32,128,128]{1,0,2:T(8,128)S(1)} %fusion.40) | data formatting | bytes 4194304 | tf_op jit(solution)/shard_map/reshape | solution.py:233
  113.4 1.3 slice_reduce_fusion
  114.9 14.6 %all-to-all-done.2 = bf16[16,64,512]{2,1,0:T(8,128)(2,1)} async-done(((bf16[16,64,512]{2,1,0:T(8,128)(2,1)}), bf16[16,64,512]{2,1,0:T(8,128)(2,1)}, u32[]{:S(2)}, u32[]{:S(2)}) %all-to-all-start.2) | async-done | bytes 1048608 | tf_op jit(solution)/shard_map/all_to_all | solution.py:230
  130.4 4.5 %all-to-all-start.3 = ((bf16[16,32,512]{2,1,0:T(8,128)(2,1)}), bf16[16,32,512]{2,1,0:T(8,128)(2,1)}, u32[]{:S(2)}, u32[]{:S(2)}) async-start(bf16[16,32,512]{2,1,0:T(8,128)(2,1)} %bitcast.134), calls=%async_computation.3 | async-start | bytes 1048576 | tf_op jit(solution)/shard_map/all_to_all | solution.py:240
  136.2 2.0 %fusion.14 = (bf16[1,512,512]{1,2,0:T(8,128)(2,1)}, bf16[1,512,512]{1,2,0:T(8,128)(2,1)}, bf16[1,512,512]{1,2,0:T(8,128)(2,1)}, bf16[1,512,512]{1,2,0:T(8,128)(2,1)}) fusion(bf16[512,512]{0,1:T(8,128)(2,1)S(1)} %copy-done.5, bf16[1,16,32,512]{3,2,0,1:T(8,128)(2,1)S(1)} %get-tuple-element.51, bf16[1,512,512]{1,2,0:T(8,128)(2,1)S(1)} %copy.18, ...), kind=kLoop, calls=%fused_computation.35 | loop fusion | flops 5242880 | bytes 6293504 | tf_op jit(solution)/shard_map/broadcast_in_dim | solution.py:258
  138.2 2.1 %copy.37 = bf16[1,512,512]{2,1,0:T(8,128)(2,1)} copy(bf16[1,512,512]{1,2,0:T(8,128)(2,1)} %get-tuple-element.47) | data formatting | bytes 1048576
  140.4 2.0 %copy.36 = bf16[1,512,512]{2,1,0:T(8,128)(2,1)} copy(bf16[1,512,512]{1,2,0:T(8,128)(2,1)} %get-tuple-element.48) | data formatting | bytes 1048576
  144.4 6.2 %all-to-all-done.3 = bf16[16,32,512]{2,1,0:T(8,128)(2,1)} async-done(((bf16[16,32,512]{2,1,0:T(8,128)(2,1)}), bf16[16,32,512]{2,1,0:T(8,128)(2,1)}, u32[]{:S(2)}, u32[]{:S(2)}) %all-to-all-start.3) | async-done | bytes 524320 | tf_op jit(solution)/shard_map/all_to_all | solution.py:240
  (73 shorter events, 15.7 us)
Async XLA Ops:
  0.6 14.0 %copy-start.10 = (bf16[1,512,512]{2,1,0:T(8,128)(2,1)S(1)}, bf16[1,512,512]{2,1,0:T(8,128)(2,1)}, u32[]{:S(2)}) copy-start(bf16[1,512,512]{2,1,0:T(8,128)(2,1)} %param.6) | copy-start | bytes 1572868
  2.1 12.7 %copy-start.11 = (bf16[1,512,512]{2,1,0:T(8,128)(2,1)S(1)}, bf16[1,512,512]{2,1,0:T(8,128)(2,1)}, u32[]{:S(2)}) copy-start(bf16[1,512,512]{2,1,0:T(8,128)(2,1)} %param.7) | copy-start | bytes 1572868
  2.3 12.8 %copy-start.12 = (bf16[1,512,512]{2,1,0:T(8,128)(2,1)S(1)}, bf16[1,512,512]{2,1,0:T(8,128)(2,1)}, u32[]{:S(2)}) copy-start(bf16[1,512,512]{2,1,0:T(8,128)(2,1)} %param.8) | copy-start | bytes 1572868
  3.8 11.5 %copy-start.13 = (bf16[1,512,512]{2,1,0:T(8,128)(2,1)S(1)}, bf16[1,512,512]{2,1,0:T(8,128)(2,1)}, u32[]{:S(2)}) copy-start(bf16[1,512,512]{2,1,0:T(8,128)(2,1)} %param.9) | copy-start | bytes 1572868
  4.6 20.1 %all-to-all-start = ((bf16[16,16,512]{2,1,0:T(8,128)(2,1)}), bf16[16,16,512]{2,1,0:T(8,128)(2,1)S(1)}, u32[]{:S(2)}, u32[]{:S(2)}) async-start(bf16[16,16,512]{2,1,0:T(8,128)(2,1)} %convert_element_type.160), calls=%async_computation | async-start | bytes 524288 | tf_op jit(solution)/shard_map/all_to_all | solution.py:195
  15.3 0.8 copy-start
  15.5 0.8 copy-start.2
  15.9 8.8 %copy-start.4 = (bf16[512,512]{0,1:T(8,128)(2,1)}, bf16[512,512]{0,1:T(8,128)(2,1)S(1)}, u32[]{:S(2)}) copy-start(bf16[512,512]{0,1:T(8,128)(2,1)S(1)} %get-tuple-element.45) | copy-start | bytes 1572868
  15.9 8.8 %copy-start.6 = (bf16[512,512]{0,1:T(8,128)(2,1)}, bf16[512,512]{0,1:T(8,128)(2,1)S(1)}, u32[]{:S(2)}) copy-start(bf16[512,512]{0,1:T(8,128)(2,1)S(1)} %get-tuple-element.46) | copy-start | bytes 1572868
  24.8 31.5 %all-to-all-start.1 = ((bf16[16,64,512]{2,1,0:T(8,128)(2,1)}), bf16[16,64,512]{2,1,0:T(8,128)(2,1)S(1)}, u32[]{:S(2)}, u32[]{:S(2)}) async-start(bf16[16,64,512]{2,1,0:T(8,128)(2,1)} %bitcast.129), calls=%async_computation.1 | async-start | bytes 2097152 | tf_op jit(solution)/shard_map/all_to_all | solution.py:197
  56.2 2.4 %collective-permute-start = (f32[512]{0:T(512)S(1)}, f32[512]{0:T(512)S(1)}, u32[]{:S(2)}, u32[]{:S(2)}) collective-permute-start(f32[512]{0:T(512)S(1)} %get-tuple-element.25), channel_id=1, source_target_pairs={{0,1},{1,0},{32,33},{33,32},{64,65},{65,64},{96,97},{97,96},{128,1... | collective-permute-start | bytes 6152 | tf_op jit(solution)/shard_map/ppermute | solution.py:211
  58.7 4.5 %collective-permute-start.1 = (f32[512]{0:T(512)S(1)}, f32[512]{0:T(512)S(1)}, u32[]{:S(2)}, u32[]{:S(2)}) collective-permute-start(f32[512]{0:T(512)S(1)} %add.89), channel_id=1, source_target_pairs={{0,32},{1,33},{32,0},{33,1},{64,96},{65,97},{96,64},{97,65},{128,1... | collective-permute-start | bytes 6152 | tf_op jit(solution)/shard_map/ppermute | solution.py:211
  63.2 5.1 %collective-permute-start.2 = (f32[512]{0:T(512)S(1)}, f32[512]{0:T(512)S(1)}, u32[]{:S(2)}, u32[]{:S(2)}) collective-permute-start(f32[512]{0:T(512)S(1)} %add.90), channel_id=1, source_target_pairs={{0,64},{1,65},{32,96},{33,97},{64,0},{65,1},{96,32},{97,33},{128,1... | collective-permute-start | bytes 6152 | tf_op jit(solution)/shard_map/ppermute | solution.py:211
  68.3 19.4 %collective-permute-start.3 = (f32[512]{0:T(512)S(1)}, f32[512]{0:T(512)S(1)}, u32[]{:S(2)}, u32[]{:S(2)}) collective-permute-start(f32[512]{0:T(512)S(1)} %add.91), channel_id=1, source_target_pairs={{0,128},{1,129},{32,160},{33,161},{64,192},{65,193},{96,224},{97,2... | collective-permute-start | bytes 6152 | tf_op jit(solution)/shard_map/ppermute | solution.py:211
  97.7 31.8 %all-to-all-start.2 = ((bf16[16,64,512]{2,1,0:T(8,128)(2,1)}), bf16[16,64,512]{2,1,0:T(8,128)(2,1)}, u32[]{:S(2)}, u32[]{:S(2)}) async-start(bf16[16,64,512]{2,1,0:T(8,128)(2,1)} %bitcast.20), calls=%async_computation.2 | async-start | bytes 2097152 | tf_op jit(solution)/shard_map/all_to_all | solution.py:230
  114.8 21.4 %copy-start.1 = (bf16[1,512,512]{1,2,0:T(8,128)(2,1)S(1)}, bf16[1,512,512]{1,2,0:T(8,128)(2,1)}, u32[]{:S(2)}) copy-start(bf16[1,512,512]{1,2,0:T(8,128)(2,1)} %copy-done) | copy-start | bytes 1572868
  114.8 21.4 %copy-start.3 = (bf16[1,512,512]{1,2,0:T(8,128)(2,1)S(1)}, bf16[1,512,512]{1,2,0:T(8,128)(2,1)}, u32[]{:S(2)}) copy-start(bf16[1,512,512]{1,2,0:T(8,128)(2,1)} %copy-done.2) | copy-start | bytes 1572868
  114.8 21.4 %copy-start.5 = (bf16[512,512]{0,1:T(8,128)(2,1)S(1)}, bf16[512,512]{0,1:T(8,128)(2,1)}, u32[]{:S(2)}) copy-start(bf16[512,512]{0,1:T(8,128)(2,1)} %copy-done.4) | copy-start | bytes 1572868
  114.8 21.4 %copy-start.7 = (bf16[512,512]{0,1:T(8,128)(2,1)S(1)}, bf16[512,512]{0,1:T(8,128)(2,1)}, u32[]{:S(2)}) copy-start(bf16[512,512]{0,1:T(8,128)(2,1)} %copy-done.6) | copy-start | bytes 1572868
  114.8 21.4 %copy-start.14 = (f32[512]{0:T(512)S(1)}, f32[512]{0:T(512)}, u32[]{:S(2)}) copy-start(f32[512]{0:T(512)} %param.11) | copy-start | bytes 6148
  130.4 20.2 %all-to-all-start.3 = ((bf16[16,32,512]{2,1,0:T(8,128)(2,1)}), bf16[16,32,512]{2,1,0:T(8,128)(2,1)}, u32[]{:S(2)}, u32[]{:S(2)}) async-start(bf16[16,32,512]{2,1,0:T(8,128)(2,1)} %bitcast.134), calls=%async_computation.3 | async-start | bytes 1048576 | tf_op jit(solution)/shard_map/all_to_all | solution.py:240
  138.2 4.2 %copy-start.9 = (bf16[1,512,512]{1,2,0:T(8,128)(2,1)S(1)}, bf16[1,512,512]{1,2,0:T(8,128)(2,1)}, u32[]{:S(2)}) copy-start(bf16[1,512,512]{1,2,0:T(8,128)(2,1)} %get-tuple-element.57) | copy-start | bytes 1572868
  138.2 5.2 %copy-start.8 = (bf16[1,512,512]{1,2,0:T(8,128)(2,1)S(1)}, bf16[1,512,512]{1,2,0:T(8,128)(2,1)}, u32[]{:S(2)}) copy-start(bf16[1,512,512]{1,2,0:T(8,128)(2,1)} %get-tuple-element.58) | copy-start | bytes 1572868

commit v6 on v5

--- a/solution.py
+++ b/solution.py
@@ -7,7 +7,7 @@
 from jax.experimental.pallas import tpu as pltpu
 from jax.sharding import PartitionSpec as P
 
-full_precision = lax.Precision.HIGH
+full_precision = lax.Precision.DEFAULT
 
 
 def spectral_tables(seq_length):

time: 154 us -> 153 us (level)
  waiting for transfers between devices: 44.1 us -> 49.4 us
  matrix products: 13.6 us -> 9.77 us
  local copies, waits for them, and re-layouts: 38.2 us -> 36.5 us
    all_to_all x1, waiting for transfers between devices: 14.6 us -> 19.3 us  [on_device(): pair_home = lax.all_to_all(pair_back, ('seq', 'dp'), 0, 0, tiled=True)]
    dot_general x2, matrix products: 9.53 us -> 6.96 us  [spectral_inverse(): return jnp.einsum('nk,kml->nml', inv_a, both, precision=full_precision)]
    reshape x1, local copies, waits for them, and re-layouts: 5.77 us -> 3.88 us  [spectral_inverse(): both = back.reshape((back.shape[0] * back.shape[1],) + back.shape[2:])]
  transfers between devices with their start and end apart: 8 -> 8, of which waited for: 5 -> 5; matrix products, arithmetic and copies ran while one was open for 30% -> 26% of each run, Pallas kernels for 11% -> 11%
where the time goes in v6:
time: 153 us; the launch traced here: 152 us
  waiting for transfers between devices  49.4 us (32%)
  local copies, waits for them, and re-layouts  36.5 us (24%)
  starting transfers between devices  29.6 us (19%)
  Pallas kernels  16.1 us (11%)
  other arithmetic  9.92 us (6%)
  matrix products  9.77 us (6%)
    all_to_all x1, waiting for transfers between devices, on_device(): pair_home = lax.all_to_all(pair_back, ('seq', 'dp'), 0, 0, tiled=True)  19.3 us
    pallas_call x1, Pallas kernels, spectral_middle(): pl.pallas_call(middle_kernel, grid=(count,), in_specs=[block, block_im, b...  16.1 us
    all_to_all x1, waiting for transfers between devices, on_device(): got = lax.all_to_all(pair, ('seq', 'dp'), 0, 0, tiled=True)  14.3 us
    all_to_all x1, starting transfers between devices, on_device(): taps_got = lax.all_to_all(taps_mine, ('seq', 'dp'), 0, 0, tiled=True)  9.98 us
    unnamed x41, local copies, waits for them, and re-layouts  9.03 us
    all_to_all x1, waiting for transfers between devices, on_device(): taps_got = lax.all_to_all(taps_mine, ('seq', 'dp'), 0, 0, tiled=True)  7.38 us
    dot_general x2, matrix products, spectral_inverse(): return jnp.einsum('nk,kml->nml', inv_a, both, precision=full_precision)  6.96 us
    all_to_all x1, waiting for transfers between devices, on_device(): slope_home = lax.all_to_all(slope_send, ('seq', 'dp'), 0, 0, tiled=True)  6.17 us
  transfers between devices with their start and end apart: 8, of which 5 were waited for; matrix products, arithmetic and copies ran while one was open for 26% of the time, Pallas kernels for 11%

profile of v6, /device:TPU:1, one launch (start us, length us, event | category | flops | bytes accessed | tf_op | source)
XLA Modules:
  0.0 152.3 jit_solution(3555799528772699959)
XLA Ops:
  0.6 1.5 copy.20
  2.3 1.5 %convert_reduce_fusion = bf16[16,32,256]{2,1,0:T(8,128)(2,1)S(1)} fusion(bf16[16,32,2,256]{3,2,1,0:T(2,128)(2,1)S(1)} %reshape.171, s32[]{:T(128)S(6)} %select_n.69), kind=kLoop, calls=%fused_computation.39 | loop fusion | bytes 524292 | tf_op jit(solution)/shard_map/convert_element_type | solution.py:194
  4.6 10.0 %all-to-all-start = ((bf16[16,16,512]{2,1,0:T(8,128)(2,1)}), bf16[16,16,512]{2,1,0:T(8,128)(2,1)S(1)}, u32[]{:S(2)}, u32[]{:S(2)}) async-start(bf16[16,16,512]{2,1,0:T(8,128)(2,1)} %convert_element_type.160), calls=%async_computation | async-start | bytes 524288 | tf_op jit(solution)/shard_map/all_to_all | solution.py:195
  17.4 7.4 %all-to-all-done = bf16[16,16,512]{2,1,0:T(8,128)(2,1)S(1)} async-done(((bf16[16,16,512]{2,1,0:T(8,128)(2,1)}), bf16[16,16,512]{2,1,0:T(8,128)(2,1)S(1)}, u32[]{:S(2)}, u32[]{:S(2)}) %all-to-all-start) | async-done | bytes 262176 | tf_op jit(solution)/shard_map/all_to_all | solution.py:195
  24.8 4.5 %all-to-all-start.1 = ((bf16[16,64,512]{2,1,0:T(8,128)(2,1)}), bf16[16,64,512]{2,1,0:T(8,128)(2,1)S(1)}, u32[]{:S(2)}, u32[]{:S(2)}) async-start(bf16[16,64,512]{2,1,0:T(8,128)(2,1)} %bitcast.128), calls=%async_computation.1 | async-start | bytes 2097152 | tf_op jit(solution)/shard_map/all_to_all | solution.py:197
  30.3 1.9 %subtract_convert_fusion = (bf16[33,128,128]{2,1,0:T(8,128)(2,1)S(1)}, bf16[33,128,128]{2,1,0:T(8,128)(2,1)S(1)}, bf16[33,128,128]{2,1,0:T(8,128)(2,1)S(1)}, bf16[33,128,128]{2,1,0:T(8,128)(2,1)S(1)}) fusion(f32[33,128]{1,0:T(8,128)S(1)} %fusion.51, f32[33,128]{1,0:T(8,128)S(1)} %fusion.52, f32[128,128]{1,0:T(8,128)S(1)} %fusion.24, f32[128,128]{1,0:T(8,128)S(1)} %fusion.25), kind=kLoop, calls=%fused_computation.7 | loop fusion | flops 9191424 | bytes 4490240 | tf_op jit(solution)/shard_map/convert.8
  32.3 2.6 %pad_maximum_fusion = (bf16[33,256,128]{2,1,0:T(8,128)(2,1)}, bf16[33,256,128]{2,1,0:T(8,128)(2,1)}) fusion(bf16[33,128,128]{2,1,0:T(8,128)(2,1)S(1)} %get-tuple-element.54, bf16[33,128,128]{2,1,0:T(8,128)(2,1)S(1)} %get-tuple-element.56, bf16[33,128,128]{2,1,0:T(8,128)(2,1)S(1)} %get-tuple-element.55, bf16[33,128,128]{2,1,0:T(8,128)(2,1)S(1)} %get-tuple-element.53), kind=kLoop, calls=%fused_computation.4 | loop fusion | flops 8650752 | bytes 8650752 | tf_op jit(solution)/shard_map/concatenate | solution.py:43
  35.8 2.3 %copy.23 = bf16[32,128,128]{2,0,1:T(8,128)(2,1)} copy(bf16[32,128,128]{1,0,2:T(8,128)(2,1)S(1)} %bitcast.129) | data formatting | bytes 2097152 | tf_op jit(solution)/shard_map/reshape | solution.py:143
  38.1 2.0 %fusion.43 = bf16[66,128,128]{2,0,1:T(8,128)(2,1)S(1)} fusion(bf16[32,128,128]{2,0,1:T(8,128)(2,1)} %copy.23, bf16[66,32]{0,1:T(8,128)(2,1)S(1)} %pad_maximum_fusion.2), kind=kOutput, calls=%fused_computation.80 | convolution fusion | flops 69206016 | bytes 3215488 | tf_op jit(solution)/shard_map/kn,nml->kml/dot_general | solution.py:142
  40.1 1.9 %copy.53.taps_re_ref.taps_im_ref = bf16[66,128,128]{2,1,0:T(8,128)(2,1)} copy(bf16[66,128,128]{2,0,1:T(8,128)(2,1)S(1)} %fusion.43) | data formatting | bytes 4325376 | tf_op jit(solution)/shard_map/kn,nml->kml/dot_general | solution.py:142
  42.0 14.3 %all-to-all-done.1 = bf16[16,64,512]{2,1,0:T(8,128)(2,1)S(1)} async-done(((bf16[16,64,512]{2,1,0:T(8,128)(2,1)}), bf16[16,64,512]{2,1,0:T(8,128)(2,1)S(1)}, u32[]{:S(2)}, u32[]{:S(2)}) %all-to-all-start.1) | async-done | bytes 1048608 | tf_op jit(solution)/shard_map/all_to_all | solution.py:197
  56.4 2.3 %collective-permute-done = f32[512]{0:T(512)S(1)} collective-permute-done((f32[512]{0:T(512)S(1)}, f32[512]{0:T(512)S(1)}, u32[]{:S(2)}, u32[]{:S(2)}) %collective-permute-start) | collective-permute-done | bytes 2080 | tf_op jit(solution)/shard_map/ppermute | solution.py:211
  59.2 1.4 reshape.176
  60.7 2.5 %copy.26 = bf16[32,128,128]{2,0,1:T(8,128)(2,1)S(1)} copy(bf16[32,128,128]{1,0,2:T(8,128)(2,1)} %reshape.176) | data formatting | bytes 2097152 | tf_op jit(solution)/shard_map/reshape | solution.py:154
  63.2 1.8 %collective-permute-start.2 = (f32[512]{0:T(512)S(1)}, f32[512]{0:T(512)S(1)}, u32[]{:S(2)}, u32[]{:S(2)}) collective-permute-start(f32[512]{0:T(512)S(1)} %add.90), channel_id=1, source_target_pairs={{0,64},{1,65},{32,96},{33,97},{64,0},{65,1},{96,32},{97,33},{128,1... | collective-permute-start | bytes 6152 | tf_op jit(solution)/shard_map/ppermute | solution.py:211
  65.8 1.9 %copy.52.sig_re_ref.sig_im_ref = bf16[66,128,128]{2,1,0:T(8,128)(2,1)} copy(bf16[66,128,128]{2,0,1:T(8,128)(2,1)S(1)} %fusion.38) | data formatting | bytes 4325376 | tf_op jit(solution)/shard_map/kn,nml->kml/dot_general | solution.py:153
  67.7 3.3 %collective-permute-start.3 = (f32[512]{0:T(512)S(1)}, f32[512]{0:T(512)S(1)}, u32[]{:S(2)}, u32[]{:S(2)}) collective-permute-start(f32[512]{0:T(512)S(1)} %add.91), channel_id=1, source_target_pairs={{0,128},{1,129},{32,160},{33,161},{64,192},{65,193},{96,224},{97,2... | collective-permute-start | bytes 6152 | tf_op jit(solution)/shard_map/ppermute | solution.py:211
  71.0 16.1 %shard_map.109 = (f32[2,33,128,128]{3,2,1,0:T(8,128)}, f32[2,33,128,128]{3,2,1,0:T(8,128)}) custom-call(bf16[66,128,128]{2,1,0:T(8,128)(2,1)} %copy.52.sig_re_ref.sig_im_ref, bf16[66,128,128]{2,1,0:T(8,128)(2,1)} %copy.52.sig_re_ref.sig_im_ref, bf16[66,128,128]{2,1,0:T(8,128)(2,1)} %copy.53.taps_re_ref.taps_im_ref, ...), custom_call_target="tpu_custom_call" | custom-call | flops 2214592512 | bytes 17301504 | tf_op jit(solution)/shard_map/pallas_call | solution.py:124
  87.7 5.1 %fusion.2 = bf16[32,128,128]{2,0,1:T(8,128)(2,1)S(1)} fusion(f32[66,128,128]{2,1,0:T(8,128)} %bitcast.134, bf16[32,66]{1,0:T(8,128)(2,1)S(1)} %pad_maximum_fusion.3), kind=kOutput, calls=%fused_computation.10 | convolution fusion | flops 69206016 | bytes 5378176 | tf_op jit(solution)/shard_map/nk,kml->nml/dot_general | solution.py:166
  92.8 1.5 %copy.29 = bf16[32,128,128]{1,0,2:T(8,128)(2,1)S(1)} copy(bf16[32,128,128]{2,0,1:T(8,128)(2,1)S(1)} %fusion.2) | data formatting | bytes 2097152 | tf_op jit(solution)/shard_map/convert_element_type | solution.py:224
  95.0 1.3 copy.30
  96.3 5.3 %all-to-all-start.2 = ((bf16[16,64,512]{2,1,0:T(8,128)(2,1)}), bf16[16,64,512]{2,1,0:T(8,128)(2,1)}, u32[]{:S(2)}, u32[]{:S(2)}) async-start(bf16[16,64,512]{2,1,0:T(8,128)(2,1)} %bitcast.20), calls=%async_computation.2 | async-start | bytes 2097152 | tf_op jit(solution)/shard_map/all_to_all | solution.py:230
  101.7 3.9 %copy.39 = bf16[66,128,128]{1,0,2:T(8,128)(2,1)S(1)} copy(f32[66,128,128]{2,1,0:T(8,128)} %bitcast.125) | data formatting | bytes 6488064 | tf_op jit(solution)/shard_map/reshape | solution.py:165
  105.5 1.9 %fusion.40 = f32[32,128,128]{1,0,2:T(8,128)} fusion(bf16[66,128,128]{1,0,2:T(8,128)(2,1)S(1)} %copy.39, bf16[32,66]{1,0:T(8,128)(2,1)S(1)} %pad_maximum_fusion.3), kind=kOutput, calls=%fused_computation.77 | convolution fusion | flops 69206016 | bytes 4264064 | tf_op jit(solution)/shard_map/nk,kml->nml/dot_general | solution.py:166
  107.4 1.7 %reshape.180 = f32[4096,2,2,32]{0,3,2,1:T(8,128)S(1)} reshape(f32[32,128,128]{1,0,2:T(8,128)} %fusion.40) | data formatting | bytes 4194304 | tf_op jit(solution)/shard_map/reshape | solution.py:233
  109.5 19.3 %all-to-all-done.2 = bf16[16,64,512]{2,1,0:T(8,128)(2,1)} async-done(((bf16[16,64,512]{2,1,0:T(8,128)(2,1)}), bf16[16,64,512]{2,1,0:T(8,128)(2,1)}, u32[]{:S(2)}, u32[]{:S(2)}) %all-to-all-start.2) | async-done | bytes 1048608 | tf_op jit(solution)/shard_map/all_to_all | solution.py:230
  129.6 4.5 %all-to-all-start.3 = ((bf16[16,32,512]{2,1,0:T(8,128)(2,1)}), bf16[16,32,512]{2,1,0:T(8,128)(2,1)}, u32[]{:S(2)}, u32[]{:S(2)}) async-start(bf16[16,32,512]{2,1,0:T(8,128)(2,1)} %bitcast.133), calls=%async_computation.3 | async-start | bytes 1048576 | tf_op jit(solution)/shard_map/all_to_all | solution.py:240
  135.4 2.0 %fusion.14 = (bf16[1,512,512]{1,2,0:T(8,128)(2,1)}, bf16[1,512,512]{1,2,0:T(8,128)(2,1)}, bf16[1,512,512]{1,2,0:T(8,128)(2,1)}, bf16[1,512,512]{1,2,0:T(8,128)(2,1)}) fusion(bf16[512,512]{0,1:T(8,128)(2,1)S(1)} %copy-done.5, bf16[1,16,32,512]{3,2,0,1:T(8,128)(2,1)S(1)} %get-tuple-element.51, bf16[1,512,512]{1,2,0:T(8,128)(2,1)S(1)} %copy.18, ...), kind=kLoop, calls=%fused_computation.35 | loop fusion | flops 5242880 | bytes 6293504 | tf_op jit(solution)/shard_map/broadcast_in_dim | solution.py:258
  137.5 2.1 %copy.37 = bf16[1,512,512]{2,1,0:T(8,128)(2,1)} copy(bf16[1,512,512]{1,2,0:T(8,128)(2,1)} %get-tuple-element.47) | data formatting | bytes 1048576
  139.6 2.0 %copy.36 = bf16[1,512,512]{2,1,0:T(8,128)(2,1)} copy(bf16[1,512,512]{1,2,0:T(8,128)(2,1)} %get-tuple-element.48) | data formatting | bytes 1048576
  143.7 6.2 %all-to-all-done.3 = bf16[16,32,512]{2,1,0:T(8,128)(2,1)} async-done(((bf16[16,32,512]{2,1,0:T(8,128)(2,1)}), bf16[16,32,512]{2,1,0:T(8,128)(2,1)}, u32[]{:S(2)}, u32[]{:S(2)}) %all-to-all-start.3) | async-done | bytes 524320 | tf_op jit(solution)/shard_map/all_to_all | solution.py:240
  151.0 1.3 copy.38
  (73 shorter events, 13.9 us)
Async XLA Ops:
  0.6 14.0 %copy-start.10 = (bf16[1,512,512]{2,1,0:T(8,128)(2,1)S(1)}, bf16[1,512,512]{2,1,0:T(8,128)(2,1)}, u32[]{:S(2)}) copy-start(bf16[1,512,512]{2,1,0:T(8,128)(2,1)} %param.6) | copy-start | bytes 1572868
  2.1 12.7 %copy-start.11 = (bf16[1,512,512]{2,1,0:T(8,128)(2,1)S(1)}, bf16[1,512,512]{2,1,0:T(8,128)(2,1)}, u32[]{:S(2)}) copy-start(bf16[1,512,512]{2,1,0:T(8,128)(2,1)} %param.7) | copy-start | bytes 1572868
  2.3 12.8 %copy-start.12 = (bf16[1,512,512]{2,1,0:T(8,128)(2,1)S(1)}, bf16[1,512,512]{2,1,0:T(8,128)(2,1)}, u32[]{:S(2)}) copy-start(bf16[1,512,512]{2,1,0:T(8,128)(2,1)} %param.8) | copy-start | bytes 1572868
  3.8 11.5 %copy-start.13 = (bf16[1,512,512]{2,1,0:T(8,128)(2,1)S(1)}, bf16[1,512,512]{2,1,0:T(8,128)(2,1)}, u32[]{:S(2)}) copy-start(bf16[1,512,512]{2,1,0:T(8,128)(2,1)} %param.9) | copy-start | bytes 1572868
  4.6 20.1 %all-to-all-start = ((bf16[16,16,512]{2,1,0:T(8,128)(2,1)}), bf16[16,16,512]{2,1,0:T(8,128)(2,1)S(1)}, u32[]{:S(2)}, u32[]{:S(2)}) async-start(bf16[16,16,512]{2,1,0:T(8,128)(2,1)} %convert_element_type.160), calls=%async_computation | async-start | bytes 524288 | tf_op jit(solution)/shard_map/all_to_all | solution.py:195
  15.3 0.8 copy-start
  15.5 0.8 copy-start.2
  15.9 8.8 %copy-start.4 = (bf16[512,512]{0,1:T(8,128)(2,1)}, bf16[512,512]{0,1:T(8,128)(2,1)S(1)}, u32[]{:S(2)}) copy-start(bf16[512,512]{0,1:T(8,128)(2,1)S(1)} %get-tuple-element.45) | copy-start | bytes 1572868
  15.9 8.8 %copy-start.6 = (bf16[512,512]{0,1:T(8,128)(2,1)}, bf16[512,512]{0,1:T(8,128)(2,1)S(1)}, u32[]{:S(2)}) copy-start(bf16[512,512]{0,1:T(8,128)(2,1)S(1)} %get-tuple-element.46) | copy-start | bytes 1572868
  24.8 31.5 %all-to-all-start.1 = ((bf16[16,64,512]{2,1,0:T(8,128)(2,1)}), bf16[16,64,512]{2,1,0:T(8,128)(2,1)S(1)}, u32[]{:S(2)}, u32[]{:S(2)}) async-start(bf16[16,64,512]{2,1,0:T(8,128)(2,1)} %bitcast.128), calls=%async_computation.1 | async-start | bytes 2097152 | tf_op jit(solution)/shard_map/all_to_all | solution.py:197
  56.2 2.4 %collective-permute-start = (f32[512]{0:T(512)S(1)}, f32[512]{0:T(512)S(1)}, u32[]{:S(2)}, u32[]{:S(2)}) collective-permute-start(f32[512]{0:T(512)S(1)} %get-tuple-element.25), channel_id=1, source_target_pairs={{0,1},{1,0},{32,33},{33,32},{64,65},{65,64},{96,97},{97,96},{128,1... | collective-permute-start | bytes 6152 | tf_op jit(solution)/shard_map/ppermute | solution.py:211
  58.7 4.5 %collective-permute-start.1 = (f32[512]{0:T(512)S(1)}, f32[512]{0:T(512)S(1)}, u32[]{:S(2)}, u32[]{:S(2)}) collective-permute-start(f32[512]{0:T(512)S(1)} %add.89), channel_id=1, source_target_pairs={{0,32},{1,33},{32,0},{33,1},{64,96},{65,97},{96,64},{97,65},{128,1... | collective-permute-start | bytes 6152 | tf_op jit(solution)/shard_map/ppermute | solution.py:211
  63.2 4.5 %collective-permute-start.2 = (f32[512]{0:T(512)S(1)}, f32[512]{0:T(512)S(1)}, u32[]{:S(2)}, u32[]{:S(2)}) collective-permute-start(f32[512]{0:T(512)S(1)} %add.90), channel_id=1, source_target_pairs={{0,64},{1,65},{32,96},{33,97},{64,0},{65,1},{96,32},{97,33},{128,1... | collective-permute-start | bytes 6152 | tf_op jit(solution)/shard_map/ppermute | solution.py:211
  67.7 19.4 %collective-permute-start.3 = (f32[512]{0:T(512)S(1)}, f32[512]{0:T(512)S(1)}, u32[]{:S(2)}, u32[]{:S(2)}) collective-permute-start(f32[512]{0:T(512)S(1)} %add.91), channel_id=1, source_target_pairs={{0,128},{1,129},{32,160},{33,161},{64,192},{65,193},{96,224},{97,2... | collective-permute-start | bytes 6152 | tf_op jit(solution)/shard_map/ppermute | solution.py:211
  96.3 32.5 %all-to-all-start.2 = ((bf16[16,64,512]{2,1,0:T(8,128)(2,1)}), bf16[16,64,512]{2,1,0:T(8,128)(2,1)}, u32[]{:S(2)}, u32[]{:S(2)}) async-start(bf16[16,64,512]{2,1,0:T(8,128)(2,1)} %bitcast.20), calls=%async_computation.2 | async-start | bytes 2097152 | tf_op jit(solution)/shard_map/all_to_all | solution.py:230
  109.3 26.1 %copy-start.1 = (bf16[1,512,512]{1,2,0:T(8,128)(2,1)S(1)}, bf16[1,512,512]{1,2,0:T(8,128)(2,1)}, u32[]{:S(2)}) copy-start(bf16[1,512,512]{1,2,0:T(8,128)(2,1)} %copy-done) | copy-start | bytes 1572868
  109.3 26.1 %copy-start.3 = (bf16[1,512,512]{1,2,0:T(8,128)(2,1)S(1)}, bf16[1,512,512]{1,2,0:T(8,128)(2,1)}, u32[]{:S(2)}) copy-start(bf16[1,512,512]{1,2,0:T(8,128)(2,1)} %copy-done.2) | copy-start | bytes 1572868
  109.3 26.1 %copy-start.5 = (bf16[512,512]{0,1:T(8,128)(2,1)S(1)}, bf16[512,512]{0,1:T(8,128)(2,1)}, u32[]{:S(2)}) copy-start(bf16[512,512]{0,1:T(8,128)(2,1)} %copy-done.4) | copy-start | bytes 1572868
  109.3 26.1 %copy-start.7 = (bf16[512,512]{0,1:T(8,128)(2,1)S(1)}, bf16[512,512]{0,1:T(8,128)(2,1)}, u32[]{:S(2)}) copy-start(bf16[512,512]{0,1:T(8,128)(2,1)} %copy-done.6) | copy-start | bytes 1572868
  109.4 26.1 %copy-start.14 = (f32[512]{0:T(512)S(1)}, f32[512]{0:T(512)}, u32[]{:S(2)}) copy-start(f32[512]{0:T(512)} %param.11) | copy-start | bytes 6148
  129.6 20.2 %all-to-all-start.3 = ((bf16[16,32,512]{2,1,0:T(8,128)(2,1)}), bf16[16,32,512]{2,1,0:T(8,128)(2,1)}, u32[]{:S(2)}, u32[]{:S(2)}) async-start(bf16[16,32,512]{2,1,0:T(8,128)(2,1)} %bitcast.133), calls=%async_computation.3 | async-start | bytes 1048576 | tf_op jit(solution)/shard_map/all_to_all | solution.py:240
  137.5 4.2 %copy-start.9 = (bf16[1,512,512]{1,2,0:T(8,128)(2,1)S(1)}, bf16[1,512,512]{1,2,0:T(8,128)(2,1)}, u32[]{:S(2)}) copy-start(bf16[1,512,512]{1,2,0:T(8,128)(2,1)} %get-tuple-element.57) | copy-start | bytes 1572868
  137.5 5.2 %copy-start.8 = (bf16[1,512,512]{1,2,0:T(8,128)(2,1)S(1)}, bf16[1,512,512]{1,2,0:T(8,128)(2,1)}, u32[]{:S(2)}) copy-start(bf16[1,512,512]{1,2,0:T(8,128)(2,1)} %get-tuple-element.58) | copy-start | bytes 1572868

commit v7 on v6

--- a/solution.py
+++ b/solution.py
@@ -112,7 +112,7 @@
 def spectral_middle(sig_first, taps_first, fwd_table, inv_table):
     half, rows2, inner = fwd_table.shape
     lanes = sig_first.shape[2]
-    steps = 3 if half % 3 == 0 else 1
+    steps = 11 if half % 11 == 0 else 1
     count = half // steps
     block = pl.BlockSpec((steps, inner, lanes), lambda k: (k, 0, 0))
     block_im = pl.BlockSpec((steps, inner, lanes), lambda k: (k + count, 0, 0))

time: 153 us -> 151 us (0.987)
  Pallas kernels: 16.1 us -> 14 us
    pallas_call x1, Pallas kernels: 16.1 us -> 14 us  [spectral_middle(): pl.pallas_call(middle_kernel, grid=(count,), in_specs=[block, block_im, b...]
  transfers between devices with their start and end apart: 8 -> 8, of which waited for: 5 -> 5; matrix products, arithmetic and copies ran while one was open for 26% -> 26% of each run, Pallas kernels for 11% -> 9%
where the time goes in v7:
time: 151 us; the launch traced here: 150 us
  waiting for transfers between devices  49.4 us (33%)
  local copies, waits for them, and re-layouts  36.5 us (24%)
  starting transfers between devices  29.6 us (20%)
  Pallas kernels  14 us (9%)
  other arithmetic  9.92 us (7%)
  matrix products  9.77 us (6%)
    all_to_all x1, waiting for transfers between devices, on_device(): pair_home = lax.all_to_all(pair_back, ('seq', 'dp'), 0, 0, tiled=True)  19.3 us
    all_to_all x1, waiting for transfers between devices, on_device(): got = lax.all_to_all(pair, ('seq', 'dp'), 0, 0, tiled=True)  14.3 us
    pallas_call x1, Pallas kernels, spectral_middle(): pl.pallas_call(middle_kernel, grid=(count,), in_specs=[block, block_im, b...  14 us
    all_to_all x1, starting transfers between devices, on_device(): taps_got = lax.all_to_all(taps_mine, ('seq', 'dp'), 0, 0, tiled=True)  9.98 us
    unnamed x41, local copies, waits for them, and re-layouts  9.03 us
    all_to_all x1, waiting for transfers between devices, on_device(): taps_got = lax.all_to_all(taps_mine, ('seq', 'dp'), 0, 0, tiled=True)  7.38 us
    dot_general x2, matrix products, spectral_inverse(): return jnp.einsum('nk,kml->nml', inv_a, both, precision=full_precision)  6.96 us
    all_to_all x1, waiting for transfers between devices, on_device(): slope_home = lax.all_to_all(slope_send, ('seq', 'dp'), 0, 0, tiled=True)  6.17 us
  transfers between devices with their start and end apart: 8, of which 5 were waited for; matrix products, arithmetic and copies ran while one was open for 26% of the time, Pallas kernels for 9%

profile of v7, /device:TPU:1, one launch (start us, length us, event | category | flops | bytes accessed | tf_op | source)
XLA Modules:
  0.0 150.2 jit_solution(8149984032964727015)
XLA Ops:
  0.6 1.5 copy.20
  2.3 1.5 %convert_reduce_fusion = bf16[16,32,256]{2,1,0:T(8,128)(2,1)S(1)} fusion(bf16[16,32,2,256]{3,2,1,0:T(2,128)(2,1)S(1)} %reshape.171, s32[]{:T(128)S(6)} %select_n.69), kind=kLoop, calls=%fused_computation.39 | loop fusion | bytes 524292 | tf_op jit(solution)/shard_map/convert_element_type | solution.py:194
  4.6 10.0 %all-to-all-start = ((bf16[16,16,512]{2,1,0:T(8,128)(2,1)}), bf16[16,16,512]{2,1,0:T(8,128)(2,1)S(1)}, u32[]{:S(2)}, u32[]{:S(2)}) async-start(bf16[16,16,512]{2,1,0:T(8,128)(2,1)} %convert_element_type.160), calls=%async_computation | async-start | bytes 524288 | tf_op jit(solution)/shard_map/all_to_all | solution.py:195
  17.4 7.4 %all-to-all-done = bf16[16,16,512]{2,1,0:T(8,128)(2,1)S(1)} async-done(((bf16[16,16,512]{2,1,0:T(8,128)(2,1)}), bf16[16,16,512]{2,1,0:T(8,128)(2,1)S(1)}, u32[]{:S(2)}, u32[]{:S(2)}) %all-to-all-start) | async-done | bytes 262176 | tf_op jit(solution)/shard_map/all_to_all | solution.py:195
  24.8 4.5 %all-to-all-start.1 = ((bf16[16,64,512]{2,1,0:T(8,128)(2,1)}), bf16[16,64,512]{2,1,0:T(8,128)(2,1)S(1)}, u32[]{:S(2)}, u32[]{:S(2)}) async-start(bf16[16,64,512]{2,1,0:T(8,128)(2,1)} %bitcast.128), calls=%async_computation.1 | async-start | bytes 2097152 | tf_op jit(solution)/shard_map/all_to_all | solution.py:197
  30.3 1.9 %subtract_convert_fusion = (bf16[33,128,128]{2,1,0:T(8,128)(2,1)S(1)}, bf16[33,128,128]{2,1,0:T(8,128)(2,1)S(1)}, bf16[33,128,128]{2,1,0:T(8,128)(2,1)S(1)}, bf16[33,128,128]{2,1,0:T(8,128)(2,1)S(1)}) fusion(f32[33,128]{1,0:T(8,128)S(1)} %fusion.51, f32[33,128]{1,0:T(8,128)S(1)} %fusion.52, f32[128,128]{1,0:T(8,128)S(1)} %fusion.24, f32[128,128]{1,0:T(8,128)S(1)} %fusion.25), kind=kLoop, calls=%fused_computation.7 | loop fusion | flops 9191424 | bytes 4490240 | tf_op jit(solution)/shard_map/convert.8
  32.3 2.6 %pad_maximum_fusion = (bf16[33,256,128]{2,1,0:T(8,128)(2,1)}, bf16[33,256,128]{2,1,0:T(8,128)(2,1)}) fusion(bf16[33,128,128]{2,1,0:T(8,128)(2,1)S(1)} %get-tuple-element.54, bf16[33,128,128]{2,1,0:T(8,128)(2,1)S(1)} %get-tuple-element.56, bf16[33,128,128]{2,1,0:T(8,128)(2,1)S(1)} %get-tuple-element.55, bf16[33,128,128]{2,1,0:T(8,128)(2,1)S(1)} %get-tuple-element.53), kind=kLoop, calls=%fused_computation.4 | loop fusion | flops 8650752 | bytes 8650752 | tf_op jit(solution)/shard_map/concatenate | solution.py:43
  35.8 2.3 %copy.23 = bf16[32,128,128]{2,0,1:T(8,128)(2,1)} copy(bf16[32,128,128]{1,0,2:T(8,128)(2,1)S(1)} %bitcast.129) | data formatting | bytes 2097152 | tf_op jit(solution)/shard_map/reshape | solution.py:143
  38.1 2.0 %fusion.43 = bf16[66,128,128]{2,0,1:T(8,128)(2,1)S(1)} fusion(bf16[32,128,128]{2,0,1:T(8,128)(2,1)} %copy.23, bf16[66,32]{0,1:T(8,128)(2,1)S(1)} %pad_maximum_fusion.2), kind=kOutput, calls=%fused_computation.80 | convolution fusion | flops 69206016 | bytes 3215488 | tf_op jit(solution)/shard_map/kn,nml->kml/dot_general | solution.py:142
  40.1 1.9 %copy.53.taps_re_ref.taps_im_ref = bf16[66,128,128]{2,1,0:T(8,128)(2,1)} copy(bf16[66,128,128]{2,0,1:T(8,128)(2,1)S(1)} %fusion.43) | data formatting | bytes 4325376 | tf_op jit(solution)/shard_map/kn,nml->kml/dot_general | solution.py:142
  42.0 14.3 %all-to-all-done.1 = bf16[16,64,512]{2,1,0:T(8,128)(2,1)S(1)} async-done(((bf16[16,64,512]{2,1,0:T(8,128)(2,1)}), bf16[16,64,512]{2,1,0:T(8,128)(2,1)S(1)}, u32[]{:S(2)}, u32[]{:S(2)}) %all-to-all-start.1) | async-done | bytes 1048608 | tf_op jit(solution)/shard_map/all_to_all | solution.py:197
  56.4 2.3 %collective-permute-done = f32[512]{0:T(512)S(1)} collective-permute-done((f32[512]{0:T(512)S(1)}, f32[512]{0:T(512)S(1)}, u32[]{:S(2)}, u32[]{:S(2)}) %collective-permute-start) | collective-permute-done | bytes 2080 | tf_op jit(solution)/shard_map/ppermute | solution.py:211
  59.2 1.4 reshape.176
  60.7 2.5 %copy.26 = bf16[32,128,128]{2,0,1:T(8,128)(2,1)S(1)} copy(bf16[32,128,128]{1,0,2:T(8,128)(2,1)} %reshape.176) | data formatting | bytes 2097152 | tf_op jit(solution)/shard_map/reshape | solution.py:154
  63.2 1.8 %collective-permute-start.2 = (f32[512]{0:T(512)S(1)}, f32[512]{0:T(512)S(1)}, u32[]{:S(2)}, u32[]{:S(2)}) collective-permute-start(f32[512]{0:T(512)S(1)} %add.90), channel_id=1, source_target_pairs={{0,64},{1,65},{32,96},{33,97},{64,0},{65,1},{96,32},{97,33},{128,1... | collective-permute-start | bytes 6152 | tf_op jit(solution)/shard_map/ppermute | solution.py:211
  65.8 1.9 %copy.52.sig_re_ref.sig_im_ref = bf16[66,128,128]{2,1,0:T(8,128)(2,1)} copy(bf16[66,128,128]{2,0,1:T(8,128)(2,1)S(1)} %fusion.38) | data formatting | bytes 4325376 | tf_op jit(solution)/shard_map/kn,nml->kml/dot_general | solution.py:153
  67.7 3.3 %collective-permute-start.3 = (f32[512]{0:T(512)S(1)}, f32[512]{0:T(512)S(1)}, u32[]{:S(2)}, u32[]{:S(2)}) collective-permute-start(f32[512]{0:T(512)S(1)} %add.91), channel_id=1, source_target_pairs={{0,128},{1,129},{32,160},{33,161},{64,192},{65,193},{96,224},{97,2... | collective-permute-start | bytes 6152 | tf_op jit(solution)/shard_map/ppermute | solution.py:211
  71.0 14.0 %shard_map.109 = (f32[2,33,128,128]{3,2,1,0:T(8,128)}, f32[2,33,128,128]{3,2,1,0:T(8,128)}) custom-call(bf16[66,128,128]{2,1,0:T(8,128)(2,1)} %copy.52.sig_re_ref.sig_im_ref, bf16[66,128,128]{2,1,0:T(8,128)(2,1)} %copy.52.sig_re_ref.sig_im_ref, bf16[66,128,128]{2,1,0:T(8,128)(2,1)} %copy.53.taps_re_ref.taps_im_ref, ...), custom_call_target="tpu_custom_call" | custom-call | flops 2214592512 | bytes 17301504 | tf_op jit(solution)/shard_map/pallas_call | solution.py:124
  85.6 5.1 %fusion.2 = bf16[32,128,128]{2,0,1:T(8,128)(2,1)S(1)} fusion(f32[66,128,128]{2,1,0:T(8,128)} %bitcast.134, bf16[32,66]{1,0:T(8,128)(2,1)S(1)} %pad_maximum_fusion.3), kind=kOutput, calls=%fused_computation.10 | convolution fusion | flops 69206016 | bytes 5378176 | tf_op jit(solution)/shard_map/nk,kml->nml/dot_general | solution.py:166
  90.7 1.5 %copy.29 = bf16[32,128,128]{1,0,2:T(8,128)(2,1)S(1)} copy(bf16[32,128,128]{2,0,1:T(8,128)(2,1)S(1)} %fusion.2) | data formatting | bytes 2097152 | tf_op jit(solution)/shard_map/convert_element_type | solution.py:224
  92.9 1.3 copy.30
  94.2 5.3 %all-to-all-start.2 = ((bf16[16,64,512]{2,1,0:T(8,128)(2,1)}), bf16[16,64,512]{2,1,0:T(8,128)(2,1)}, u32[]{:S(2)}, u32[]{:S(2)}) async-start(bf16[16,64,512]{2,1,0:T(8,128)(2,1)} %bitcast.20), calls=%async_computation.2 | async-start | bytes 2097152 | tf_op jit(solution)/shard_map/all_to_all | solution.py:230
  99.5 3.9 %copy.39 = bf16[66,128,128]{1,0,2:T(8,128)(2,1)S(1)} copy(f32[66,128,128]{2,1,0:T(8,128)} %bitcast.125) | data formatting | bytes 6488064 | tf_op jit(solution)/shard_map/reshape | solution.py:165
  103.4 1.9 %fusion.40 = f32[32,128,128]{1,0,2:T(8,128)} fusion(bf16[66,128,128]{1,0,2:T(8,128)(2,1)S(1)} %copy.39, bf16[32,66]{1,0:T(8,128)(2,1)S(1)} %pad_maximum_fusion.3), kind=kOutput, calls=%fused_computation.77 | convolution fusion | flops 69206016 | bytes 4264064 | tf_op jit(solution)/shard_map/nk,kml->nml/dot_general | solution.py:166
  105.3 1.7 %reshape.180 = f32[4096,2,2,32]{0,3,2,1:T(8,128)S(1)} reshape(f32[32,128,128]{1,0,2:T(8,128)} %fusion.40) | data formatting | bytes 4194304 | tf_op jit(solution)/shard_map/reshape | solution.py:233
  107.3 19.3 %all-to-all-done.2 = bf16[16,64,512]{2,1,0:T(8,128)(2,1)} async-done(((bf16[16,64,512]{2,1,0:T(8,128)(2,1)}), bf16[16,64,512]{2,1,0:T(8,128)(2,1)}, u32[]{:S(2)}, u32[]{:S(2)}) %all-to-all-start.2) | async-done | bytes 1048608 | tf_op jit(solution)/shard_map/all_to_all | solution.py:230
  127.5 4.5 %all-to-all-start.3 = ((bf16[16,32,512]{2,1,0:T(8,128)(2,1)}), bf16[16,32,512]{2,1,0:T(8,128)(2,1)}, u32[]{:S(2)}, u32[]{:S(2)}) async-start(bf16[16,32,512]{2,1,0:T(8,128)(2,1)} %bitcast.133), calls=%async_computation.3 | async-start | bytes 1048576 | tf_op jit(solution)/shard_map/all_to_all | solution.py:240
  133.3 2.0 %fusion.14 = (bf16[1,512,512]{1,2,0:T(8,128)(2,1)}, bf16[1,512,512]{1,2,0:T(8,128)(2,1)}, bf16[1,512,512]{1,2,0:T(8,128)(2,1)}, bf16[1,512,512]{1,2,0:T(8,128)(2,1)}) fusion(bf16[512,512]{0,1:T(8,128)(2,1)S(1)} %copy-done.5, bf16[1,16,32,512]{3,2,0,1:T(8,128)(2,1)S(1)} %get-tuple-element.51, bf16[1,512,512]{1,2,0:T(8,128)(2,1)S(1)} %copy.18, ...), kind=kLoop, calls=%fused_computation.35 | loop fusion | flops 5242880 | bytes 6293504 | tf_op jit(solution)/shard_map/broadcast_in_dim | solution.py:258
  135.3 2.1 %copy.37 = bf16[1,512,512]{2,1,0:T(8,128)(2,1)} copy(bf16[1,512,512]{1,2,0:T(8,128)(2,1)} %get-tuple-element.47) | data formatting | bytes 1048576
  137.5 2.0 %copy.36 = bf16[1,512,512]{2,1,0:T(8,128)(2,1)} copy(bf16[1,512,512]{1,2,0:T(8,128)(2,1)} %get-tuple-element.48) | data formatting | bytes 1048576
  141.5 6.2 %all-to-all-done.3 = bf16[16,32,512]{2,1,0:T(8,128)(2,1)} async-done(((bf16[16,32,512]{2,1,0:T(8,128)(2,1)}), bf16[16,32,512]{2,1,0:T(8,128)(2,1)}, u32[]{:S(2)}, u32[]{:S(2)}) %all-to-all-start.3) | async-done | bytes 524320 | tf_op jit(solution)/shard_map/all_to_all | solution.py:240
  148.9 1.3 copy.38
  (73 shorter events, 13.9 us)
Async XLA Ops:
  0.6 14.0 %copy-start.10 = (bf16[1,512,512]{2,1,0:T(8,128)(2,1)S(1)}, bf16[1,512,512]{2,1,0:T(8,128)(2,1)}, u32[]{:S(2)}) copy-start(bf16[1,512,512]{2,1,0:T(8,128)(2,1)} %param.6) | copy-start | bytes 1572868
  2.1 12.7 %copy-start.11 = (bf16[1,512,512]{2,1,0:T(8,128)(2,1)S(1)}, bf16[1,512,512]{2,1,0:T(8,128)(2,1)}, u32[]{:S(2)}) copy-start(bf16[1,512,512]{2,1,0:T(8,128)(2,1)} %param.7) | copy-start | bytes 1572868
  2.3 12.8 %copy-start.12 = (bf16[1,512,512]{2,1,0:T(8,128)(2,1)S(1)}, bf16[1,512,512]{2,1,0:T(8,128)(2,1)}, u32[]{:S(2)}) copy-start(bf16[1,512,512]{2,1,0:T(8,128)(2,1)} %param.8) | copy-start | bytes 1572868
  3.8 11.5 %copy-start.13 = (bf16[1,512,512]{2,1,0:T(8,128)(2,1)S(1)}, bf16[1,512,512]{2,1,0:T(8,128)(2,1)}, u32[]{:S(2)}) copy-start(bf16[1,512,512]{2,1,0:T(8,128)(2,1)} %param.9) | copy-start | bytes 1572868
  4.6 20.1 %all-to-all-start = ((bf16[16,16,512]{2,1,0:T(8,128)(2,1)}), bf16[16,16,512]{2,1,0:T(8,128)(2,1)S(1)}, u32[]{:S(2)}, u32[]{:S(2)}) async-start(bf16[16,16,512]{2,1,0:T(8,128)(2,1)} %convert_element_type.160), calls=%async_computation | async-start | bytes 524288 | tf_op jit(solution)/shard_map/all_to_all | solution.py:195
  15.3 0.8 copy-start
  15.5 0.8 copy-start.2
  15.9 8.8 %copy-start.4 = (bf16[512,512]{0,1:T(8,128)(2,1)}, bf16[512,512]{0,1:T(8,128)(2,1)S(1)}, u32[]{:S(2)}) copy-start(bf16[512,512]{0,1:T(8,128)(2,1)S(1)} %get-tuple-element.45) | copy-start | bytes 1572868
  15.9 8.8 %copy-start.6 = (bf16[512,512]{0,1:T(8,128)(2,1)}, bf16[512,512]{0,1:T(8,128)(2,1)S(1)}, u32[]{:S(2)}) copy-start(bf16[512,512]{0,1:T(8,128)(2,1)S(1)} %get-tuple-element.46) | copy-start | bytes 1572868
  24.8 31.5 %all-to-all-start.1 = ((bf16[16,64,512]{2,1,0:T(8,128)(2,1)}), bf16[16,64,512]{2,1,0:T(8,128)(2,1)S(1)}, u32[]{:S(2)}, u32[]{:S(2)}) async-start(bf16[16,64,512]{2,1,0:T(8,128)(2,1)} %bitcast.128), calls=%async_computation.1 | async-start | bytes 2097152 | tf_op jit(solution)/shard_map/all_to_all | solution.py:197
  56.2 2.4 %collective-permute-start = (f32[512]{0:T(512)S(1)}, f32[512]{0:T(512)S(1)}, u32[]{:S(2)}, u32[]{:S(2)}) collective-permute-start(f32[512]{0:T(512)S(1)} %get-tuple-element.25), channel_id=1, source_target_pairs={{0,1},{1,0},{32,33},{33,32},{64,65},{65,64},{96,97},{97,96},{128,1... | collective-permute-start | bytes 6152 | tf_op jit(solution)/shard_map/ppermute | solution.py:211
  58.7 4.5 %collective-permute-start.1 = (f32[512]{0:T(512)S(1)}, f32[512]{0:T(512)S(1)}, u32[]{:S(2)}, u32[]{:S(2)}) collective-permute-start(f32[512]{0:T(512)S(1)} %add.89), channel_id=1, source_target_pairs={{0,32},{1,33},{32,0},{33,1},{64,96},{65,97},{96,64},{97,65},{128,1... | collective-permute-start | bytes 6152 | tf_op jit(solution)/shard_map/ppermute | solution.py:211
  63.2 4.5 %collective-permute-start.2 = (f32[512]{0:T(512)S(1)}, f32[512]{0:T(512)S(1)}, u32[]{:S(2)}, u32[]{:S(2)}) collective-permute-start(f32[512]{0:T(512)S(1)} %add.90), channel_id=1, source_target_pairs={{0,64},{1,65},{32,96},{33,97},{64,0},{65,1},{96,32},{97,33},{128,1... | collective-permute-start | bytes 6152 | tf_op jit(solution)/shard_map/ppermute | solution.py:211
  67.7 17.3 %collective-permute-start.3 = (f32[512]{0:T(512)S(1)}, f32[512]{0:T(512)S(1)}, u32[]{:S(2)}, u32[]{:S(2)}) collective-permute-start(f32[512]{0:T(512)S(1)} %add.91), channel_id=1, source_target_pairs={{0,128},{1,129},{32,160},{33,161},{64,192},{65,193},{96,224},{97,2... | collective-permute-start | bytes 6152 | tf_op jit(solution)/shard_map/ppermute | solution.py:211
  94.2 32.5 %all-to-all-start.2 = ((bf16[16,64,512]{2,1,0:T(8,128)(2,1)}), bf16[16,64,512]{2,1,0:T(8,128)(2,1)}, u32[]{:S(2)}, u32[]{:S(2)}) async-start(bf16[16,64,512]{2,1,0:T(8,128)(2,1)} %bitcast.20), calls=%async_computation.2 | async-start | bytes 2097152 | tf_op jit(solution)/shard_map/all_to_all | solution.py:230
  107.2 26.1 %copy-start.1 = (bf16[1,512,512]{1,2,0:T(8,128)(2,1)S(1)}, bf16[1,512,512]{1,2,0:T(8,128)(2,1)}, u32[]{:S(2)}) copy-start(bf16[1,512,512]{1,2,0:T(8,128)(2,1)} %copy-done) | copy-start | bytes 1572868
  107.2 26.1 %copy-start.3 = (bf16[1,512,512]{1,2,0:T(8,128)(2,1)S(1)}, bf16[1,512,512]{1,2,0:T(8,128)(2,1)}, u32[]{:S(2)}) copy-start(bf16[1,512,512]{1,2,0:T(8,128)(2,1)} %copy-done.2) | copy-start | bytes 1572868
  107.2 26.1 %copy-start.5 = (bf16[512,512]{0,1:T(8,128)(2,1)S(1)}, bf16[512,512]{0,1:T(8,128)(2,1)}, u32[]{:S(2)}) copy-start(bf16[512,512]{0,1:T(8,128)(2,1)} %copy-done.4) | copy-start | bytes 1572868
  107.2 26.1 %copy-start.7 = (bf16[512,512]{0,1:T(8,128)(2,1)S(1)}, bf16[512,512]{0,1:T(8,128)(2,1)}, u32[]{:S(2)}) copy-start(bf16[512,512]{0,1:T(8,128)(2,1)} %copy-done.6) | copy-start | bytes 1572868
  107.2 26.1 %copy-start.14 = (f32[512]{0:T(512)S(1)}, f32[512]{0:T(512)}, u32[]{:S(2)}) copy-start(f32[512]{0:T(512)} %param.11) | copy-start | bytes 6148
  127.5 20.2 %all-to-all-start.3 = ((bf16[16,32,512]{2,1,0:T(8,128)(2,1)}), bf16[16,32,512]{2,1,0:T(8,128)(2,1)}, u32[]{:S(2)}, u32[]{:S(2)}) async-start(bf16[16,32,512]{2,1,0:T(8,128)(2,1)} %bitcast.133), calls=%async_computation.3 | async-start | bytes 1048576 | tf_op jit(solution)/shard_map/all_to_all | solution.py:240
  135.3 4.2 %copy-start.9 = (bf16[1,512,512]{1,2,0:T(8,128)(2,1)S(1)}, bf16[1,512,512]{1,2,0:T(8,128)(2,1)}, u32[]{:S(2)}) copy-start(bf16[1,512,512]{1,2,0:T(8,128)(2,1)} %get-tuple-element.57) | copy-start | bytes 1572868
  135.3 5.2 %copy-start.8 = (bf16[1,512,512]{1,2,0:T(8,128)(2,1)S(1)}, bf16[1,512,512]{1,2,0:T(8,128)(2,1)}, u32[]{:S(2)}) copy-start(bf16[1,512,512]{1,2,0:T(8,128)(2,1)} %get-tuple-element.58) | copy-start | bytes 1572868

commit v8 on v7

--- a/solution.py
+++ b/solution.py
@@ -103,10 +103,10 @@
             jnp.bfloat16
         )
         back = jnp.dot(inv_ref[step], second, preferred_element_type=jnp.float32)
-        pair_ref[0, step] = back[:inner, 0:lanes] - back[inner:, lanes : 2 * lanes]
-        pair_ref[1, step] = back[:inner, lanes : 2 * lanes] + back[inner:, 0:lanes]
-        cross_ref[0, step] = back[:inner, 2 * lanes : 3 * lanes] - back[inner:, 3 * lanes :]
-        cross_ref[1, step] = back[:inner, 3 * lanes :] + back[inner:, 2 * lanes : 3 * lanes]
+        pair_ref[0, step] = (back[:inner, 0:lanes] - back[inner:, lanes : 2 * lanes]).astype(pair_ref.dtype)
+        pair_ref[1, step] = (back[:inner, lanes : 2 * lanes] + back[inner:, 0:lanes]).astype(pair_ref.dtype)
+        cross_ref[0, step] = (back[:inner, 2 * lanes : 3 * lanes] - back[inner:, 3 * lanes :]).astype(cross_ref.dtype)
+        cross_ref[1, step] = (back[:inner, 3 * lanes :] + back[inner:, 2 * lanes : 3 * lanes]).astype(cross_ref.dtype)
 
 
 def spectral_middle(sig_first, taps_first, fwd_table, inv_table):
@@ -118,7 +118,7 @@
     block_im = pl.BlockSpec((steps, inner, lanes), lambda k: (k + count, 0, 0))
     table_block = pl.BlockSpec((steps, rows2, inner), lambda k: (k, 0, 0))
     out_block = pl.BlockSpec((2, steps, inner, lanes), lambda k: (0, k, 0, 0))
-    out_shape = jax.ShapeDtypeStruct((2, half, inner, lanes), jnp.float32)
+    out_shape = jax.ShapeDtypeStruct((2, half, inner, lanes), jnp.bfloat16)
     flops = half * 2 * 2 * rows2 * inner * 4 * lanes
     bytes_accessed = half * (4 * inner * lanes * 2 + 4 * inner * lanes * 4 + 2 * rows2 * inner * 2)
     return pl.pallas_call(

time: 151 us -> 149 us (0.987)
  matrix products: 9.77 us -> 8.03 us
    dot_general x2, matrix products: 6.96 us -> 5.23 us  [spectral_inverse(): return jnp.einsum('nk,kml->nml', inv_a, both, precision=full_precision)]
where the time goes in v8:
time: 149 us; the launch traced here: 148 us
  waiting for transfers between devices  50.3 us (34%)
  local copies, waits for them, and re-layouts  35.8 us (24%)
  starting transfers between devices  29.5 us (20%)
  Pallas kernels  13.5 us (9%)
  other arithmetic  9.82 us (7%)
  matrix products  8.03 us (5%)
    all_to_all x1, waiting for transfers between devices, on_device(): pair_home = lax.all_to_all(pair_back, ('seq', 'dp'), 0, 0, tiled=True)  20.1 us
    all_to_all x1, waiting for transfers between devices, on_device(): got = lax.all_to_all(pair, ('seq', 'dp'), 0, 0, tiled=True)  14.3 us
    pallas_call x1, Pallas kernels, spectral_middle(): pl.pallas_call(middle_kernel, grid=(count,), in_specs=[block, block_im, b...  13.5 us
    all_to_all x1, starting transfers between devices, on_device(): taps_got = lax.all_to_all(taps_mine, ('seq', 'dp'), 0, 0, tiled=True)  9.98 us
    unnamed x41, local copies, waits for them, and re-layouts  9.03 us
    all_to_all x1, waiting for transfers between devices, on_device(): taps_got = lax.all_to_all(taps_mine, ('seq', 'dp'), 0, 0, tiled=True)  7.38 us
    all_to_all x1, waiting for transfers between devices, on_device(): slope_home = lax.all_to_all(slope_send, ('seq', 'dp'), 0, 0, tiled=True)  6.17 us
    ppermute x4, starting transfers between devices, on_device(): total = total + lax.ppermute(total, ('seq', 'dp'), partners)  5.34 us
  transfers between devices with their start and end apart: 8, of which 5 were waited for; matrix products, arithmetic and copies ran while one was open for 26% of the time, Pallas kernels for 9%

profile of v8, /device:TPU:1, one launch (start us, length us, event | category | flops | bytes accessed | tf_op | source)
XLA Modules:
  0.0 148.0 jit_solution(5647821321840369529)
XLA Ops:
  0.6 1.5 %copy.20 = bf16[512,512]{1,0:T(8,128)(2,1)S(1)} copy(f32[512,512]{0,1:T(8,128)} %bitcast.136) | data formatting | bytes 1572864 | tf_op jit(solution)/shard_map/transpose | solution.py:191
  2.3 1.5 %convert_reduce_fusion = bf16[16,32,256]{2,1,0:T(8,128)(2,1)S(1)} fusion(bf16[16,32,2,256]{3,2,1,0:T(2,128)(2,1)S(1)} %reshape.171, s32[]{:T(128)S(6)} %select_n.69), kind=kLoop, calls=%fused_computation.39 | loop fusion | bytes 524292 | tf_op jit(solution)/shard_map/convert_element_type | solution.py:194
  4.6 10.0 %all-to-all-start = ((bf16[16,16,512]{2,1,0:T(8,128)(2,1)}), bf16[16,16,512]{2,1,0:T(8,128)(2,1)S(1)}, u32[]{:S(2)}, u32[]{:S(2)}) async-start(bf16[16,16,512]{2,1,0:T(8,128)(2,1)} %convert_element_type.160), calls=%async_computation | async-start | bytes 524288 | tf_op jit(solution)/shard_map/all_to_all | solution.py:195
  17.4 7.4 %all-to-all-done = bf16[16,16,512]{2,1,0:T(8,128)(2,1)S(1)} async-done(((bf16[16,16,512]{2,1,0:T(8,128)(2,1)}), bf16[16,16,512]{2,1,0:T(8,128)(2,1)S(1)}, u32[]{:S(2)}, u32[]{:S(2)}) %all-to-all-start) | async-done | bytes 262176 | tf_op jit(solution)/shard_map/all_to_all | solution.py:195
  24.8 4.5 %all-to-all-start.1 = ((bf16[16,64,512]{2,1,0:T(8,128)(2,1)}), bf16[16,64,512]{2,1,0:T(8,128)(2,1)S(1)}, u32[]{:S(2)}, u32[]{:S(2)}) async-start(bf16[16,64,512]{2,1,0:T(8,128)(2,1)} %bitcast.127), calls=%async_computation.1 | async-start | bytes 2097152 | tf_op jit(solution)/shard_map/all_to_all | solution.py:197
  30.3 1.9 %subtract_convert_fusion = (bf16[33,128,128]{2,1,0:T(8,128)(2,1)S(1)}, bf16[33,128,128]{2,1,0:T(8,128)(2,1)S(1)}, bf16[33,128,128]{2,1,0:T(8,128)(2,1)S(1)}, bf16[33,128,128]{2,1,0:T(8,128)(2,1)S(1)}) fusion(f32[33,128]{1,0:T(8,128)S(1)} %fusion.51, f32[33,128]{1,0:T(8,128)S(1)} %fusion.52, f32[128,128]{1,0:T(8,128)S(1)} %fusion.24, f32[128,128]{1,0:T(8,128)S(1)} %fusion.25), kind=kLoop, calls=%fused_computation.7 | loop fusion | flops 9191424 | bytes 4490240 | tf_op jit(solution)/shard_map/convert.8
  32.3 2.5 %pad_maximum_fusion = (bf16[33,256,128]{2,1,0:T(8,128)(2,1)}, bf16[33,256,128]{2,1,0:T(8,128)(2,1)}) fusion(bf16[33,128,128]{2,1,0:T(8,128)(2,1)S(1)} %get-tuple-element.54, bf16[33,128,128]{2,1,0:T(8,128)(2,1)S(1)} %get-tuple-element.56, bf16[33,128,128]{2,1,0:T(8,128)(2,1)S(1)} %get-tuple-element.55, bf16[33,128,128]{2,1,0:T(8,128)(2,1)S(1)} %get-tuple-element.53), kind=kLoop, calls=%fused_computation.4 | loop fusion | flops 8650752 | bytes 8650752 | tf_op jit(solution)/shard_map/concatenate | solution.py:43
  35.7 2.3 %copy.23 = bf16[32,128,128]{2,0,1:T(8,128)(2,1)} copy(bf16[32,128,128]{1,0,2:T(8,128)(2,1)S(1)} %bitcast.128) | data formatting | bytes 2097152 | tf_op jit(solution)/shard_map/reshape | solution.py:143
  38.0 2.0 %fusion.43 = bf16[66,128,128]{2,0,1:T(8,128)(2,1)S(1)} fusion(bf16[32,128,128]{2,0,1:T(8,128)(2,1)} %copy.23, bf16[66,32]{0,1:T(8,128)(2,1)S(1)} %pad_maximum_fusion.2), kind=kOutput, calls=%fused_computation.80 | convolution fusion | flops 69206016 | bytes 3215488 | tf_op jit(solution)/shard_map/kn,nml->kml/dot_general | solution.py:142
  40.0 1.9 %copy.53.taps_re_ref.taps_im_ref = bf16[66,128,128]{2,1,0:T(8,128)(2,1)} copy(bf16[66,128,128]{2,0,1:T(8,128)(2,1)S(1)} %fusion.43) | data formatting | bytes 4325376 | tf_op jit(solution)/shard_map/kn,nml->kml/dot_general | solution.py:142
  41.9 14.3 %all-to-all-done.1 = bf16[16,64,512]{2,1,0:T(8,128)(2,1)S(1)} async-done(((bf16[16,64,512]{2,1,0:T(8,128)(2,1)}), bf16[16,64,512]{2,1,0:T(8,128)(2,1)S(1)}, u32[]{:S(2)}, u32[]{:S(2)}) %all-to-all-start.1) | async-done | bytes 1048608 | tf_op jit(solution)/shard_map/all_to_all | solution.py:197
  56.4 2.3 %collective-permute-done = f32[512]{0:T(512)S(1)} collective-permute-done((f32[512]{0:T(512)S(1)}, f32[512]{0:T(512)S(1)}, u32[]{:S(2)}, u32[]{:S(2)}) %collective-permute-start) | collective-permute-done | bytes 2080 | tf_op jit(solution)/shard_map/ppermute | solution.py:211
  59.2 1.4 reshape.176
  60.7 2.5 %copy.26 = bf16[32,128,128]{2,0,1:T(8,128)(2,1)S(1)} copy(bf16[32,128,128]{1,0,2:T(8,128)(2,1)} %reshape.176) | data formatting | bytes 2097152 | tf_op jit(solution)/shard_map/reshape | solution.py:154
  63.2 1.8 %collective-permute-start.2 = (f32[512]{0:T(512)S(1)}, f32[512]{0:T(512)S(1)}, u32[]{:S(2)}, u32[]{:S(2)}) collective-permute-start(f32[512]{0:T(512)S(1)} %add.90), channel_id=1, source_target_pairs={{0,64},{1,65},{32,96},{33,97},{64,0},{65,1},{96,32},{97,33},{128,1... | collective-permute-start | bytes 6152 | tf_op jit(solution)/shard_map/ppermute | solution.py:211
  65.8 2.0 %copy.52.sig_re_ref.sig_im_ref = bf16[66,128,128]{2,1,0:T(8,128)(2,1)} copy(bf16[66,128,128]{2,0,1:T(8,128)(2,1)S(1)} %fusion.38) | data formatting | bytes 4325376 | tf_op jit(solution)/shard_map/kn,nml->kml/dot_general | solution.py:153
  67.8 3.3 %collective-permute-start.3 = (f32[512]{0:T(512)S(1)}, f32[512]{0:T(512)S(1)}, u32[]{:S(2)}, u32[]{:S(2)}) collective-permute-start(f32[512]{0:T(512)S(1)} %add.91), channel_id=1, source_target_pairs={{0,128},{1,129},{32,160},{33,161},{64,192},{65,193},{96,224},{97,2... | collective-permute-start | bytes 6152 | tf_op jit(solution)/shard_map/ppermute | solution.py:211
  71.1 13.5 %shard_map.109 = (bf16[2,33,128,128]{3,2,1,0:T(8,128)(2,1)}, bf16[2,33,128,128]{3,2,1,0:T(8,128)(2,1)}) custom-call(bf16[66,128,128]{2,1,0:T(8,128)(2,1)} %copy.52.sig_re_ref.sig_im_ref, bf16[66,128,128]{2,1,0:T(8,128)(2,1)} %copy.52.sig_re_ref.sig_im_ref, bf16[66,128,128]{2,1,0:T(8,128)(2,1)} %copy.53.taps_re_ref.taps_im_ref, ...), custom_call_target="tpu_custom_call" | custom-call | flops 2214592512 | bytes 17301504 | tf_op jit(solution)/shard_map/pallas_call | solution.py:124
  85.2 3.4 %fusion.2 = bf16[32,128,128]{2,0,1:T(8,128)(2,1)S(1)} fusion(bf16[66,128,128]{2,1,0:T(8,128)(2,1)} %bitcast.132, bf16[32,66]{1,0:T(8,128)(2,1)S(1)} %pad_maximum_fusion.3), kind=kOutput, calls=%fused_computation.10 | convolution fusion | flops 69206016 | bytes 3215488 | tf_op jit(solution)/shard_map/nk,kml->nml/dot_general | solution.py:166
  88.6 1.5 %copy.29 = bf16[32,128,128]{1,0,2:T(8,128)(2,1)S(1)} copy(bf16[32,128,128]{2,0,1:T(8,128)(2,1)S(1)} %fusion.2) | data formatting | bytes 2097152 | tf_op jit(solution)/shard_map/convert_element_type | solution.py:224
  90.8 1.3 copy.30
  92.1 5.2 %all-to-all-start.2 = ((bf16[16,64,512]{2,1,0:T(8,128)(2,1)}), bf16[16,64,512]{2,1,0:T(8,128)(2,1)}, u32[]{:S(2)}, u32[]{:S(2)}) async-start(bf16[16,64,512]{2,1,0:T(8,128)(2,1)} %bitcast.20), calls=%async_computation.2 | async-start | bytes 2097152 | tf_op jit(solution)/shard_map/all_to_all | solution.py:230
  97.3 3.1 %copy.39 = bf16[66,128,128]{1,0,2:T(8,128)(2,1)S(1)} copy(bf16[66,128,128]{2,1,0:T(8,128)(2,1)} %bitcast.133) | data formatting | bytes 4325376 | tf_op jit(solution)/shard_map/reshape | solution.py:165
  100.4 1.9 %fusion.40 = f32[32,128,128]{1,0,2:T(8,128)} fusion(bf16[66,128,128]{1,0,2:T(8,128)(2,1)S(1)} %copy.39, bf16[32,66]{1,0:T(8,128)(2,1)S(1)} %pad_maximum_fusion.3), kind=kOutput, calls=%fused_computation.77 | convolution fusion | flops 69206016 | bytes 4264064 | tf_op jit(solution)/shard_map/nk,kml->nml/dot_general | solution.py:166
  102.3 1.7 %reshape.180 = f32[4096,2,2,32]{0,3,2,1:T(8,128)S(1)} reshape(f32[32,128,128]{1,0,2:T(8,128)} %fusion.40) | data formatting | bytes 4194304 | tf_op jit(solution)/shard_map/reshape | solution.py:233
  104.3 20.1 %all-to-all-done.2 = bf16[16,64,512]{2,1,0:T(8,128)(2,1)} async-done(((bf16[16,64,512]{2,1,0:T(8,128)(2,1)}), bf16[16,64,512]{2,1,0:T(8,128)(2,1)}, u32[]{:S(2)}, u32[]{:S(2)}) %all-to-all-start.2) | async-done | bytes 1048608 | tf_op jit(solution)/shard_map/all_to_all | solution.py:230
  125.3 4.5 %all-to-all-start.3 = ((bf16[16,32,512]{2,1,0:T(8,128)(2,1)}), bf16[16,32,512]{2,1,0:T(8,128)(2,1)}, u32[]{:S(2)}, u32[]{:S(2)}) async-start(bf16[16,32,512]{2,1,0:T(8,128)(2,1)} %bitcast.134), calls=%async_computation.3 | async-start | bytes 1048576 | tf_op jit(solution)/shard_map/all_to_all | solution.py:240
  131.1 2.0 %fusion.14 = (bf16[1,512,512]{1,2,0:T(8,128)(2,1)}, bf16[1,512,512]{1,2,0:T(8,128)(2,1)}, bf16[1,512,512]{1,2,0:T(8,128)(2,1)}, bf16[1,512,512]{1,2,0:T(8,128)(2,1)}) fusion(bf16[512,512]{0,1:T(8,128)(2,1)S(1)} %copy-done.5, bf16[1,16,32,512]{3,2,0,1:T(8,128)(2,1)S(1)} %get-tuple-element.51, bf16[1,512,512]{1,2,0:T(8,128)(2,1)S(1)} %copy.18, ...), kind=kLoop, calls=%fused_computation.35 | loop fusion | flops 5242880 | bytes 6293504 | tf_op jit(solution)/shard_map/broadcast_in_dim | solution.py:258
  133.1 2.1 %copy.37 = bf16[1,512,512]{2,1,0:T(8,128)(2,1)} copy(bf16[1,512,512]{1,2,0:T(8,128)(2,1)} %get-tuple-element.47) | data formatting | bytes 1048576
  135.3 2.0 %copy.36 = bf16[1,512,512]{2,1,0:T(8,128)(2,1)} copy(bf16[1,512,512]{1,2,0:T(8,128)(2,1)} %get-tuple-element.48) | data formatting | bytes 1048576
  139.3 6.2 %all-to-all-done.3 = bf16[16,32,512]{2,1,0:T(8,128)(2,1)} async-done(((bf16[16,32,512]{2,1,0:T(8,128)(2,1)}), bf16[16,32,512]{2,1,0:T(8,128)(2,1)}, u32[]{:S(2)}, u32[]{:S(2)}) %all-to-all-start.3) | async-done | bytes 524320 | tf_op jit(solution)/shard_map/all_to_all | solution.py:240
  146.7 1.3 copy.38
  (73 shorter events, 13.9 us)
Async XLA Ops:
  0.6 14.0 %copy-start.10 = (bf16[1,512,512]{2,1,0:T(8,128)(2,1)S(1)}, bf16[1,512,512]{2,1,0:T(8,128)(2,1)}, u32[]{:S(2)}) copy-start(bf16[1,512,512]{2,1,0:T(8,128)(2,1)} %param.6) | copy-start | bytes 1572868
  2.1 12.7 %copy-start.11 = (bf16[1,512,512]{2,1,0:T(8,128)(2,1)S(1)}, bf16[1,512,512]{2,1,0:T(8,128)(2,1)}, u32[]{:S(2)}) copy-start(bf16[1,512,512]{2,1,0:T(8,128)(2,1)} %param.7) | copy-start | bytes 1572868
  2.3 12.8 %copy-start.12 = (bf16[1,512,512]{2,1,0:T(8,128)(2,1)S(1)}, bf16[1,512,512]{2,1,0:T(8,128)(2,1)}, u32[]{:S(2)}) copy-start(bf16[1,512,512]{2,1,0:T(8,128)(2,1)} %param.8) | copy-start | bytes 1572868
  3.8 11.5 %copy-start.13 = (bf16[1,512,512]{2,1,0:T(8,128)(2,1)S(1)}, bf16[1,512,512]{2,1,0:T(8,128)(2,1)}, u32[]{:S(2)}) copy-start(bf16[1,512,512]{2,1,0:T(8,128)(2,1)} %param.9) | copy-start | bytes 1572868
  4.6 20.1 %all-to-all-start = ((bf16[16,16,512]{2,1,0:T(8,128)(2,1)}), bf16[16,16,512]{2,1,0:T(8,128)(2,1)S(1)}, u32[]{:S(2)}, u32[]{:S(2)}) async-start(bf16[16,16,512]{2,1,0:T(8,128)(2,1)} %convert_element_type.160), calls=%async_computation | async-start | bytes 524288 | tf_op jit(solution)/shard_map/all_to_all | solution.py:195
  15.3 0.8 copy-start
  15.5 0.8 copy-start.2
  15.9 8.8 %copy-start.4 = (bf16[512,512]{0,1:T(8,128)(2,1)}, bf16[512,512]{0,1:T(8,128)(2,1)S(1)}, u32[]{:S(2)}) copy-start(bf16[512,512]{0,1:T(8,128)(2,1)S(1)} %get-tuple-element.45) | copy-start | bytes 1572868
  15.9 8.8 %copy-start.6 = (bf16[512,512]{0,1:T(8,128)(2,1)}, bf16[512,512]{0,1:T(8,128)(2,1)S(1)}, u32[]{:S(2)}) copy-start(bf16[512,512]{0,1:T(8,128)(2,1)S(1)} %get-tuple-element.46) | copy-start | bytes 1572868
  24.8 31.5 %all-to-all-start.1 = ((bf16[16,64,512]{2,1,0:T(8,128)(2,1)}), bf16[16,64,512]{2,1,0:T(8,128)(2,1)S(1)}, u32[]{:S(2)}, u32[]{:S(2)}) async-start(bf16[16,64,512]{2,1,0:T(8,128)(2,1)} %bitcast.127), calls=%async_computation.1 | async-start | bytes 2097152 | tf_op jit(solution)/shard_map/all_to_all | solution.py:197
  56.2 2.4 %collective-permute-start = (f32[512]{0:T(512)S(1)}, f32[512]{0:T(512)S(1)}, u32[]{:S(2)}, u32[]{:S(2)}) collective-permute-start(f32[512]{0:T(512)S(1)} %get-tuple-element.25), channel_id=1, source_target_pairs={{0,1},{1,0},{32,33},{33,32},{64,65},{65,64},{96,97},{97,96},{128,1... | collective-permute-start | bytes 6152 | tf_op jit(solution)/shard_map/ppermute | solution.py:211
  58.7 4.5 %collective-permute-start.1 = (f32[512]{0:T(512)S(1)}, f32[512]{0:T(512)S(1)}, u32[]{:S(2)}, u32[]{:S(2)}) collective-permute-start(f32[512]{0:T(512)S(1)} %add.89), channel_id=1, source_target_pairs={{0,32},{1,33},{32,0},{33,1},{64,96},{65,97},{96,64},{97,65},{128,1... | collective-permute-start | bytes 6152 | tf_op jit(solution)/shard_map/ppermute | solution.py:211
  63.2 4.6 %collective-permute-start.2 = (f32[512]{0:T(512)S(1)}, f32[512]{0:T(512)S(1)}, u32[]{:S(2)}, u32[]{:S(2)}) collective-permute-start(f32[512]{0:T(512)S(1)} %add.90), channel_id=1, source_target_pairs={{0,64},{1,65},{32,96},{33,97},{64,0},{65,1},{96,32},{97,33},{128,1... | collective-permute-start | bytes 6152 | tf_op jit(solution)/shard_map/ppermute | solution.py:211
  67.8 16.8 %collective-permute-start.3 = (f32[512]{0:T(512)S(1)}, f32[512]{0:T(512)S(1)}, u32[]{:S(2)}, u32[]{:S(2)}) collective-permute-start(f32[512]{0:T(512)S(1)} %add.91), channel_id=1, source_target_pairs={{0,128},{1,129},{32,160},{33,161},{64,192},{65,193},{96,224},{97,2... | collective-permute-start | bytes 6152 | tf_op jit(solution)/shard_map/ppermute | solution.py:211
  92.1 32.4 %all-to-all-start.2 = ((bf16[16,64,512]{2,1,0:T(8,128)(2,1)}), bf16[16,64,512]{2,1,0:T(8,128)(2,1)}, u32[]{:S(2)}, u32[]{:S(2)}) async-start(bf16[16,64,512]{2,1,0:T(8,128)(2,1)} %bitcast.20), calls=%async_computation.2 | async-start | bytes 2097152 | tf_op jit(solution)/shard_map/all_to_all | solution.py:230
  104.2 26.9 %copy-start.1 = (bf16[1,512,512]{1,2,0:T(8,128)(2,1)S(1)}, bf16[1,512,512]{1,2,0:T(8,128)(2,1)}, u32[]{:S(2)}) copy-start(bf16[1,512,512]{1,2,0:T(8,128)(2,1)} %copy-done) | copy-start | bytes 1572868
  104.2 26.9 %copy-start.3 = (bf16[1,512,512]{1,2,0:T(8,128)(2,1)S(1)}, bf16[1,512,512]{1,2,0:T(8,128)(2,1)}, u32[]{:S(2)}) copy-start(bf16[1,512,512]{1,2,0:T(8,128)(2,1)} %copy-done.2) | copy-start | bytes 1572868
  104.2 26.9 %copy-start.5 = (bf16[512,512]{0,1:T(8,128)(2,1)S(1)}, bf16[512,512]{0,1:T(8,128)(2,1)}, u32[]{:S(2)}) copy-start(bf16[512,512]{0,1:T(8,128)(2,1)} %copy-done.4) | copy-start | bytes 1572868
  104.2 26.9 %copy-start.7 = (bf16[512,512]{0,1:T(8,128)(2,1)S(1)}, bf16[512,512]{0,1:T(8,128)(2,1)}, u32[]{:S(2)}) copy-start(bf16[512,512]{0,1:T(8,128)(2,1)} %copy-done.6) | copy-start | bytes 1572868
  104.2 26.9 %copy-start.14 = (f32[512]{0:T(512)S(1)}, f32[512]{0:T(512)}, u32[]{:S(2)}) copy-start(f32[512]{0:T(512)} %param.11) | copy-start | bytes 6148
  125.3 20.2 %all-to-all-start.3 = ((bf16[16,32,512]{2,1,0:T(8,128)(2,1)}), bf16[16,32,512]{2,1,0:T(8,128)(2,1)}, u32[]{:S(2)}, u32[]{:S(2)}) async-start(bf16[16,32,512]{2,1,0:T(8,128)(2,1)} %bitcast.134), calls=%async_computation.3 | async-start | bytes 1048576 | tf_op jit(solution)/shard_map/all_to_all | solution.py:240
  133.1 4.2 %copy-start.9 = (bf16[1,512,512]{1,2,0:T(8,128)(2,1)S(1)}, bf16[1,512,512]{1,2,0:T(8,128)(2,1)}, u32[]{:S(2)}) copy-start(bf16[1,512,512]{1,2,0:T(8,128)(2,1)} %get-tuple-element.57) | copy-start | bytes 1572868
  133.1 5.2 %copy-start.8 = (bf16[1,512,512]{1,2,0:T(8,128)(2,1)S(1)}, bf16[1,512,512]{1,2,0:T(8,128)(2,1)}, u32[]{:S(2)}) copy-start(bf16[1,512,512]{1,2,0:T(8,128)(2,1)} %get-tuple-element.58) | copy-start | bytes 1572868
